TPU v7x, 256 devices: a whole 4x4x8 slice. The times are simulated.
256 devices in a mesh: tm: 4 (over y), row: 4 (over x), col: 16 (over z, core).
Axes of the slice: x: 4, y: 4, z: 8, core: 2. Of those that a mesh axis runs over, the one named last changes fastest.
Arguments:
- day_block: float32 [4, 4, 16, 32, 4, 4, 128], P('tm', None, 'col', None, None, 'row'), as said below
- left_coupling: float32 [4, 4, 16, 32, 4, 4, 128], P('tm', None, 'col', None, None, 'row'), may hold values from -0.125 to 0.125
- right_coupling: float32 [4, 4, 16, 32, 4, 4, 128], P('tm', None, 'col', None, None, 'row'), may hold values from -0.125 to 0.125
- separator_block: float32 [4, 4, 16, 32, 4, 4, 128], P('tm', None, 'col', None, None, 'row')
- arrow_coupling: float32 [4, 4, 16, 32, 64], P('tm', None, 'col'), may hold values from -0.125 to 0.125
- arrow_block: float32 [64, 64], replicated
Outputs:
- day_factor: float32 [4, 4, 16, 32, 4, 4, 128], P('tm', None, 'col', None, None, 'row')
- left_factor: float32 [4, 4, 16, 32, 4, 4, 128], P('tm', None, 'col', None, None, 'row')
- right_factor: float32 [4, 4, 16, 32, 4, 4, 128], P('tm', None, 'col', None, None, 'row')
- arrow_factor: float32 [4, 4, 16, 32, 64], P('tm', None, 'col')
- separator: float32 [4, 4, 16, 32, 4, 4, 128], P('tm', None, 'col', None, None, 'row')
- arrowhead: float32 [64, 64], replicated
Inputs may be any that keep to these rules, and one draw needn't show every extreme that they name: Each group's day_block and separator_block, and arrow_block, is an exactly symmetric matrix with all eigenvalues at least 1.
All inputs are finite; a program needn't handle non-finite values.
Results may differ from a plain program's by a relative error of at most 0.0001.
Values sent between devices are 32-bit elements; how exact they have to be, the bound alone decides.
No kernel may reach another device: no remote copies, remote signals or barrier semaphores. Data moves between devices by JAX's collectives and lax.ppermute only.
A program may use at most 128 MiB of HBM per device.

v0:
```python
import jax
import jax.numpy as jnp
from jax import lax
from jax.sharding import PartitionSpec as P


def passed_along(value, axis, steps):
    count = lax.axis_size(axis)
    initial, last = (max(0, -steps), min(count, count - steps))
    return lax.ppermute(value, axis, [(source, source + steps) for source in range(initial, last)])


def product(left, right):
    return jnp.dot(left, right, precision=lax.Precision.HIGHEST, preferred_element_type=jnp.float32)


def lower_inverse(factor):
    identity = jnp.eye(factor.shape[0], dtype=jnp.float32)
    return lax.linalg.triangular_solve(factor, identity, left_side=True, lower=True)


def reorder_nodes(whole, panels, col_width):
    count = whole.shape[0]
    col_count = lax.axis_size("col")
    spread = whole.reshape(count, panels, col_count, col_width)
    return jnp.transpose(spread, (2, 1, 3, 0)).reshape(col_count * panels * col_width, count)


def separator_term(solved, panels, col_width, row_width):
    whole = lax.all_gather(
        solved.reshape(solved.shape[0], panels, 1, row_width), "row", axis=2, tiled=True
    )
    ordered = reorder_nodes(whole, panels, col_width)
    return lax.psum_scatter(product(ordered, solved), "col", scatter_dimension=0, tiled=True)


def per_device(
    day_block, left_coupling, right_coupling, separator_block, arrow_coupling, arrow_block
):
    panels = day_block.shape[1]
    col_width = day_block.shape[3]
    row_width = day_block.shape[6]
    panel_size = col_width * lax.axis_size("col")
    arrow_rows = arrow_block.shape[0]
    col_index = lax.axis_index("col")
    row_index = lax.axis_index("row")
    matrix = day_block.reshape(panels, col_width, panels, row_width)
    left_part = left_coupling.reshape(panels, col_width, panels, row_width)
    right_part = right_coupling.reshape(panels, col_width, panels, row_width)
    arrow_part = arrow_coupling.reshape(panels, col_width, arrow_rows)
    rows_at = col_index * col_width + lax.broadcasted_iota(jnp.int32, (col_width, row_width), 0)
    cols_at = row_index * row_width + lax.broadcasted_iota(jnp.int32, (col_width, row_width), 1)
    factor_blocks = []
    left_blocks = []
    right_blocks = []
    arrow_blocks = []
    for current in range(panels):
        remain = panels - current
        gathered_day, gathered_left, gathered_right, gathered_arrow = (
            lax.all_gather(matrix[current, :, current:, :], "col", axis=0, tiled=True),
            lax.all_gather(left_part[current], "col", axis=0, tiled=True),
            lax.all_gather(right_part[current], "col", axis=0, tiled=True),
            lax.all_gather(arrow_part[current], "col", axis=0, tiled=True),
        )
        diagonal_full = lax.all_gather(gathered_day[:, 0:1, :], "row", axis=1, tiled=True).reshape(
            panel_size, panel_size
        )
        factor = jnp.linalg.cholesky(diagonal_full)
        inverse = lower_inverse(factor)
        owned = product(inverse, gathered_day.reshape(panel_size, remain * row_width)).reshape(
            panel_size, remain, row_width
        )
        if remain > 1:
            later = lax.all_gather(owned[:, 1:, None, :], "row", axis=2, tiled=True).reshape(
                panel_size, remain - 1, panel_size
            )
        solved_left = product(inverse, gathered_left.reshape(panel_size, panels * row_width))
        solved_right = product(inverse, gathered_right.reshape(panel_size, panels * row_width))
        solved_arrow = product(inverse, gathered_arrow)
        mine_rows = lax.dynamic_slice_in_dim(owned, col_index * col_width, col_width, 0)
        diagonal_part = jnp.where(cols_at >= rows_at, mine_rows[:, 0, :], 0.0)
        factor_blocks.append(
            jnp.concatenate(
                [
                    jnp.zeros((col_width, current, row_width), jnp.float32),
                    diagonal_part[:, None, :],
                    mine_rows[:, 1:, :],
                ],
                axis=1,
            )
        )
        left_blocks.append(
            lax.dynamic_slice_in_dim(solved_left, col_index * col_width, col_width, 0)
        )
        right_blocks.append(
            lax.dynamic_slice_in_dim(solved_right, col_index * col_width, col_width, 0)
        )
        arrow_blocks.append(
            lax.dynamic_slice_in_dim(solved_arrow, col_index * col_width, col_width, 0)
        )
        if remain > 1:
            mine_later = lax.dynamic_slice_in_dim(later, col_index * col_width, col_width, 2)
            mine_later = mine_later.reshape(panel_size, (remain - 1) * col_width).T
            owned_later = owned[:, 1:, :].reshape(panel_size, (remain - 1) * row_width)
            matrix = matrix.at[current + 1 :, :, current + 1 :, :].add(
                -product(mine_later, owned_later).reshape(
                    remain - 1, col_width, remain - 1, row_width
                )
            )
            left_part = left_part.at[current + 1 :].add(
                -product(mine_later, solved_left).reshape(remain - 1, col_width, panels, row_width)
            )
            right_part = right_part.at[current + 1 :].add(
                -product(mine_later, solved_right).reshape(remain - 1, col_width, panels, row_width)
            )
            arrow_part = arrow_part.at[current + 1 :].add(
                -product(mine_later, solved_arrow).reshape(remain - 1, col_width, arrow_rows)
            )
    day_factor = jnp.stack(factor_blocks).reshape(day_block.shape)
    left_solved = jnp.stack(left_blocks).reshape(panels * col_width, panels * row_width)
    right_solved = jnp.stack(right_blocks).reshape(panels * col_width, panels * row_width)
    arrow_solved = jnp.stack(arrow_blocks).reshape(panels * col_width, arrow_rows)
    separator_local = separator_block.reshape(panels * col_width, panels * row_width)
    right_term = separator_term(right_solved, panels, col_width, row_width)
    left_term = separator_term(left_solved, panels, col_width, row_width)
    from_next = passed_along(left_term, "tm", -1)
    separator = separator_local - right_term - from_next
    arrow_local = product(arrow_solved.T, arrow_solved)
    arrow_total = lax.psum(arrow_local, ("tm", "col"))
    arrowhead = arrow_block - arrow_total
    return (
        day_factor,
        left_solved.reshape(left_coupling.shape),
        right_solved.reshape(right_coupling.shape),
        arrow_solved.reshape(arrow_coupling.shape),
        separator.reshape(separator_block.shape),
        arrowhead,
    )


def solution(mesh):
    return jax.shard_map(
        per_device,
        mesh=mesh,
        in_specs=(
            P("tm", None, "col", None, None, "row", None),
            P("tm", None, "col", None, None, "row", None),
            P("tm", None, "col", None, None, "row", None),
            P("tm", None, "col", None, None, "row", None),
            P("tm", None, "col", None, None),
            P(),
        ),
        out_specs=(
            P("tm", None, "col", None, None, "row", None),
            P("tm", None, "col", None, None, "row", None),
            P("tm", None, "col", None, None, "row", None),
            P("tm", None, "col", None, None),
            P("tm", None, "col", None, None, "row", None),
            P(),
        ),
        check_vma=False,
    )
```

profile of v0, /device:TPU:8, one launch (start us, length us, event | category | flops | bytes accessed | tf_op | source)
XLA Modules:
  0.0 1515.8 jit_solution(10383593552836481364)
XLA Ops:
  8.8 43.1 %all-gather.49.cloned.1.call-done = f32[1,1,1,512,4,1,128]{6,4,5,2,1,0,3:T(4,128)} async-done(((f32[1,1,1,32,4,1,128]{6,4,5,2,1,0,3:T(4,128)}), f32[1,1,1,512,4,1,128]{6,4,5,2,1,0,3:T(4,128)}) %all-gather.49.cloned.1.call-update) | async-done | bytes 1048592 | tf_op jit(solution)/shard_map/all_gather | solution.py:60
  56.7 22.7 %all-gather.39.cloned.1.call-done = f32[512,4,128]{2,0,1:T(8,128)} async-done(((f32[512,1,128]{2,0,1:T(8,128)}), f32[512,4,128]{2,0,1:T(8,128)}) %all-gather.39.cloned.1.call-update) | async-done | bytes 1048592 | tf_op jit(solution)/shard_map/all_gather | solution.py:65
  82.6 11.7 cholesky.462
  94.3 9.8 custom-call.35
  106.8 11.7 cholesky.481
  118.5 10.2 custom-call.36
  130.3 11.7 cholesky.502
  142.7 9.8 custom-call.37
  154.0 11.9 cholesky.519
  169.9 8.0 while.20
  177.9 39.3 %custom-call.38 = f32[4,128,128]{1,2,0:T(8,128)S(1)} custom-call(f32[4,128,128]{2,1,0:T(8,128)S(1)} %get-tuple-element.178), custom_call_target="InvertDiagBlocksLowerTriangular" | custom-call | tf_op jit(solution)/shard_map/triangular_solve/custom-call.3 | solution.py:19
  229.1 44.2 %all-gather.51.cloned.1.call-done = f32[512,3,512]{2,0,1:T(8,128)} async-done(((f32[512,3,128]{2,0,1:T(8,128)}), f32[512,3,512]{2,0,1:T(8,128)}) %all-gather.51.cloned.1.call-update) | async-done | bytes 3145744 | tf_op jit(solution)/shard_map/all_gather | solution.py:74
  278.4 19.6 %all-gather.2 = f32[1,512,3,128]{3,1,2,0:T(8,128)S(1)} all-gather(f32[1,32,3,128]{3,1,2,0:T(8,128)S(1)} %slice.678), channel_id=4, replica_groups=mesh['tm'=4,'row'=4,'col'=16] {'col'}, dimensions={1}, use_global_device_ids=true | all-gather | bytes 835584 | tf_op jit(solution)/shard_map/all_gather | solution.py:60
  300.2 23.7 %all-gather.41.cloned.1.call-done = f32[512,4,128]{2,0,1:T(8,128)} async-done(((f32[512,1,128]{2,0,1:T(8,128)}), f32[512,4,128]{2,0,1:T(8,128)}) %all-gather.41.cloned.1.call-update) | async-done | bytes 1048592 | tf_op jit(solution)/shard_map/all_gather | solution.py:65
  329.1 11.7 cholesky.534
  341.5 9.8 custom-call.39
  354.0 11.7 cholesky.553
  366.4 10.2 custom-call.40
  378.2 11.7 cholesky.574
  390.6 9.8 custom-call.41
  401.8 11.9 cholesky.591
  418.2 11.6 while.21
  429.8 39.3 %custom-call.42 = f32[4,128,128]{1,2,0:T(8,128)S(1)} custom-call(f32[4,128,128]{2,1,0:T(8,128)S(1)} %get-tuple-element.179), custom_call_target="InvertDiagBlocksLowerTriangular" | custom-call | tf_op jit(solution)/shard_map/triangular_solve/custom-call.3 | solution.py:19
  486.5 31.8 %all-gather.53.cloned.1.call-done = f32[512,2,512]{2,0,1:T(8,128)} async-done(((f32[512,2,128]{2,0,1:T(8,128)}), f32[512,2,512]{2,0,1:T(8,128)}) %all-gather.53.cloned.1.call-update) | async-done | bytes 2097168 | tf_op jit(solution)/shard_map/all_gather | solution.py:74
  523.3 19.0 %all-gather.4 = f32[1,512,2,128]{3,1,2,0:T(8,128)S(1)} all-gather(f32[1,32,2,128]{3,1,2,0:T(8,128)S(1)} %slice.689), channel_id=6, replica_groups=mesh['tm'=4,'row'=4,'col'=16] {'col'}, dimensions={1}, use_global_device_ids=true | all-gather | bytes 557056 | tf_op jit(solution)/shard_map/all_gather | solution.py:60
  543.9 16.2 %all-gather.59.cloned.1.call-done = f32[1,1,1,512,4,1,128]{6,4,5,2,1,0,3:T(4,128)} async-done(((f32[1,1,1,32,4,1,128]{6,4,5,2,1,0,3:T(4,128)}), f32[1,1,1,512,4,1,128]{6,4,5,2,1,0,3:T(4,128)}) %all-gather.59.cloned.1.call-update) | async-done | bytes 1048592 | tf_op jit(solution)/shard_map/all_gather | solution.py:61
  571.4 27.8 %all-gather.67.cloned.1.call-done = f32[1,1,1,512,4,1,128]{6,4,5,2,1,0,3:T(4,128)} async-done(((f32[1,1,1,32,4,1,128]{6,4,5,2,1,0,3:T(4,128)}), f32[1,1,1,512,4,1,128]{6,4,5,2,1,0,3:T(4,128)}) %all-gather.67.cloned.1.call-update) | async-done | bytes 1048592 | tf_op jit(solution)/shard_map/all_gather | solution.py:62
  610.7 16.1 %all-gather.43.cloned.1.call-done = f32[512,4,128]{2,0,1:T(8,128)} async-done(((f32[512,1,128]{2,0,1:T(8,128)}), f32[512,4,128]{2,0,1:T(8,128)}) %all-gather.43.cloned.1.call-update) | async-done | bytes 1048592 | tf_op jit(solution)/shard_map/all_gather | solution.py:65
  632.0 11.7 cholesky.606
  644.4 9.8 custom-call.43
  657.5 11.7 cholesky.625
  669.9 10.0 custom-call.44
  682.4 11.7 cholesky.646
  694.8 9.8 custom-call.45
  706.0 11.9 cholesky.663
  722.3 11.5 while.22
  733.8 39.3 %custom-call.46 = f32[4,128,128]{1,2,0:T(8,128)S(1)} custom-call(f32[4,128,128]{2,1,0:T(8,128)S(1)} %get-tuple-element.180), custom_call_target="InvertDiagBlocksLowerTriangular" | custom-call | tf_op jit(solution)/shard_map/triangular_solve/custom-call.3 | solution.py:19
  787.8 4.1 fusion.196
  801.1 4.0 fusion.195
  816.1 19.5 %all-gather.6 = f32[1,512,1,128]{3,1,2,0:T(8,128)} all-gather(f32[1,32,1,128]{3,1,2,0:T(8,128)S(1)} %fusion.15), channel_id=8, replica_groups=mesh['tm'=4,'row'=4,'col'=16] {'col'}, dimensions={1}, use_global_device_ids=true | all-gather | bytes 278528 | tf_op jit(solution)/shard_map/all_gather | solution.py:60
  835.7 17.2 %all-gather.63.cloned.1.call-done = f32[1,512,4,128]{3,1,2,0:T(8,128)} async-done(((f32[1,32,4,128]{3,1,2,0:T(8,128)}), f32[1,512,4,128]{3,1,2,0:T(8,128)}) %all-gather.63.cloned.1.call-update) | async-done | bytes 1048592 | tf_op jit(solution)/shard_map/all_gather | solution.py:61
  855.5 4.1 fusion.194
  868.1 24.0 %all-gather.71.cloned.1.call-done = f32[1,512,4,128]{3,1,2,0:T(8,128)} async-done(((f32[1,32,4,128]{3,1,2,0:T(8,128)}), f32[1,512,4,128]{3,1,2,0:T(8,128)}) %all-gather.71.cloned.1.call-update) | async-done | bytes 1048592 | tf_op jit(solution)/shard_map/all_gather | solution.py:62
  894.6 4.1 fusion.193
  904.5 14.4 all-gather.57.cloned.1.call-done
  924.2 11.7 cholesky.678
  936.6 10.4 custom-call.47
  951.8 13.2 cholesky.697
  967.1 11.5 custom-call.48
  982.4 13.2 cholesky.718
  997.7 11.3 custom-call.49
  1011.9 13.6 cholesky.735
  1030.7 11.6 while.23
  1042.3 39.3 %custom-call.50 = f32[4,128,128]{1,2,0:T(8,128)S(1)} custom-call(f32[4,128,128]{2,1,0:T(8,128)S(1)} %get-tuple-element.181), custom_call_target="InvertDiagBlocksLowerTriangular" | custom-call | tf_op jit(solution)/shard_map/triangular_solve/custom-call.3 | solution.py:19
  1106.4 16.4 %all-gather.47.cloned.1.call-done = f32[128,4,4,128]{3,0,1,2:T(8,128)} async-done(((f32[128,4,1,128]{3,0,1,2:T(8,128)}), f32[128,4,4,128]{3,0,1,2:T(8,128)}) %all-gather.47.cloned.1.call-update) | async-done | bytes 1048592 | tf_op jit(solution)/shard_map/all_gather | solution.py:30
  1124.5 5.0 fusion.202
  1129.7 21.8 %all-gather.45.cloned.1.call-done = f32[128,4,4,128]{3,0,1,2:T(8,128)} async-done(((f32[128,4,1,128]{3,0,1,2:T(8,128)}), f32[128,4,4,128]{3,0,1,2:T(8,128)}) %all-gather.45.cloned.1.call-update) | async-done | bytes 1048592 | tf_op jit(solution)/shard_map/all_gather | solution.py:30
  1153.2 5.0 fusion.201
  1158.8 18.3 %all-gather.16 = f32[1,1,1,512,64]{4,3,2,1,0:T(8,128)S(1)} all-gather(f32[1,1,1,32,64]{4,3,2,1,0:T(8,128)S(1)} %slice-done.1), channel_id=18, replica_groups=mesh['tm'=4,'row'=4,'col'=16] {'col'}, dimensions={3}, use_global_device_ids=true | all-gather | bytes 139264 | tf_op jit(solution)/shard_map/all_gather | solution.py:63
  1186.0 15.8 %all-gather.17 = f32[1,512,64]{2,1,0:T(8,128)S(1)} all-gather(f32[1,32,64]{2,1,0:T(8,128)S(1)} %slice.716), channel_id=19, replica_groups=mesh['tm'=4,'row'=4,'col'=16] {'col'}, dimensions={1}, use_global_device_ids=true | all-gather | bytes 139264 | tf_op jit(solution)/shard_map/all_gather | solution.py:63
  1207.3 16.2 %all-gather.18 = f32[1,512,64]{2,1,0:T(8,128)S(1)} all-gather(f32[1,32,64]{2,1,0:T(8,128)S(1)} %slice.718), channel_id=20, replica_groups=mesh['tm'=4,'row'=4,'col'=16] {'col'}, dimensions={1}, use_global_device_ids=true | all-gather | bytes 139264 | tf_op jit(solution)/shard_map/all_gather | solution.py:63
  1229.4 16.1 %all-gather.19 = f32[1,512,64]{2,1,0:T(8,128)S(1)} all-gather(f32[1,32,64]{2,1,0:T(8,128)S(1)} %fusion.13), channel_id=21, replica_groups=mesh['tm'=4,'row'=4,'col'=16] {'col'}, dimensions={1}, use_global_device_ids=true | all-gather | bytes 139264 | tf_op jit(solution)/shard_map/all_gather | solution.py:63
  1248.9 214.0 %psum.7 = f32[64,64]{1,0:T(8,128)S(1)} all-reduce(f32[64,64]{1,0:T(8,128)S(1)} %convolution_bitcast_fusion), channel_id=1, replica_groups=mesh['tm'=4,'row'=4,'col'=16] {'tm','col'}, use_global_device_ids=true, to_apply=%region_10.0 | all-reduce | flops 4096 | bytes 32768 | tf_op jit(solution)/shard_map/psum | solution.py:129
  1465.0 37.8 %collective-permute-start = (f32[128,512]{1,0:T(8,128)}, f32[128,512]{1,0:T(8,128)S(1)}, u32[]{:S(2)}, u32[]{:S(2)}) collective-permute-start(f32[128,512]{1,0:T(8,128)} %reduce-scatter.5.cloned.1.call-done), channel_id=1, source_target_pairs={{64,0},{128,64},{192,128},{65,1},{129,65},{193,129},{66,2},{130,66... | collective-permute-start | bytes 786440 | tf_op jit(solution)/shard_map/ppermute | solution.py:10
  (478 shorter events, 294.7 us)
Async XLA Ops:
  7.2 44.7 %all-gather.49.cloned.1.call-start = ((), (), s32[]{:S(2)}) async-start(), calls=%async_computation.9 | async-start | bytes 1114112 | tf_op jit(solution)/shard_map/all_gather | solution.py:60
  8.7 70.7 %all-gather.39.cloned.1.call-start = ((), (), s32[]{:S(2)}) async-start(), calls=%async_computation.2 | async-start | bytes 1310720 | tf_op jit(solution)/shard_map/all_gather | solution.py:65
  54.0 219.3 %all-gather.51.cloned.1.call-start = ((), (), s32[]{:S(2)}) async-start(), calls=%async_computation.10 | async-start | bytes 3932160 | tf_op jit(solution)/shard_map/all_gather | solution.py:74
  177.9 39.8 %copy-start.23 = (f32[512,512]{1,0:T(8,128)}, f32[512,512]{1,0:T(8,128)S(1)}, u32[]{:S(2)}) copy-start(f32[512,512]{1,0:T(8,128)S(1)} %get-tuple-element.505) | copy-start | bytes 3145732
  219.8 7.7 copy-start.59
  220.3 378.9 %copy-start = (f32[128,512]{1,0:T(8,128)}, f32[128,512]{1,0:T(8,128)S(1)}, u32[]{:S(2)}) copy-start(f32[128,512]{1,0:T(8,128)S(1)} %fusion.151) | copy-start | bytes 786436
  222.4 53.1 %copy-start.11 = (f32[128,512]{1,0:T(8,128)}, f32[128,512]{1,0:T(8,128)S(1)}, u32[]{:S(2)}) copy-start(f32[128,512]{1,0:T(8,128)S(1)} %fusion.150) | copy-start | bytes 786436
  227.5 96.4 %all-gather.41.cloned.1.call-start = ((), (), s32[]{:S(2)}) async-start(), calls=%async_computation.3 | async-start | bytes 1310720 | tf_op jit(solution)/shard_map/all_gather | solution.py:65
  276.9 327.9 %copy-start.9 = (f32[512,3,32]{0,2,1:T(8,128)}, f32[512,3,32]{0,2,1:T(8,128)S(1)}, u32[]{:S(2)}) copy-start(f32[512,3,32]{0,2,1:T(8,128)S(1)} %copy.124) | copy-start | bytes 589828
  298.7 219.6 %all-gather.53.cloned.1.call-start = ((), (), s32[]{:S(2)}) async-start(), calls=%async_computation.11 | async-start | bytes 2621440 | tf_op jit(solution)/shard_map/all_gather | solution.py:74
  469.1 3.4 copy-start.50
  472.9 47.4 %copy-start.2 = (f32[128,512]{1,0:T(8,128)}, f32[128,512]{1,0:T(8,128)S(1)}, u32[]{:S(2)}) copy-start(f32[128,512]{1,0:T(8,128)S(1)} %fusion.145) | copy-start | bytes 786436
  480.5 79.6 %copy-start.12 = (f32[128,512]{1,0:T(8,128)S(1)}, f32[128,512]{1,0:T(8,128)}, u32[]{:S(2)}) copy-start(f32[128,512]{1,0:T(8,128)} %copy-done.11) | copy-start | bytes 786436
  481.3 78.8 %all-gather.59.cloned.1.call-start = ((), (), s32[]{:S(2)}) async-start(), calls=%async_computation.14 | async-start | bytes 1114112 | tf_op jit(solution)/shard_map/all_gather | solution.py:61
  482.9 116.3 %all-gather.67.cloned.1.call-start = ((), (), s32[]{:S(2)}) async-start(), calls=%async_computation.18 | async-start | bytes 1114112 | tf_op jit(solution)/shard_map/all_gather | solution.py:62
  484.4 142.4 %all-gather.43.cloned.1.call-start = ((), (), s32[]{:S(2)}) async-start(), calls=%async_computation.4 | async-start | bytes 1310720 | tf_op jit(solution)/shard_map/all_gather | solution.py:65
  520.4 46.3 %slice-start = ((f32[1,4,1,32,4,1,128]{6,5,4,3,2,1,0:T(1,128)}), f32[1,3,1,32,4,1,128]{6,5,4,3,2,1,0:T(1,128)S(1)}, s32[]{:S(2)}) async-start(f32[1,4,1,32,4,1,128]{6,5,4,3,2,1,0:T(1,128)} %param.34), calls=%async_computation.22 | async-start | bytes 393216 | tf_op jit(solution)/shard_map/slice.420
  523.3 45.8 %copy-start.57 = (f32[2,32,2,128]{3,1,2,0:T(8,128)}, f32[2,32,2,128]{3,1,2,0:T(8,128)S(1)}, u32[]{:S(2)}) copy-start(f32[2,32,2,128]{3,1,2,0:T(8,128)S(1)} %fusion.9) | copy-start | bytes 196612
  543.8 241.4 %all-gather.61.cloned.1.call-start = ((), (), s32[]{:S(2)}) async-start(), calls=%async_computation.15 | async-start | bytes 1114112 | tf_op jit(solution)/shard_map/all_gather | solution.py:61
  569.1 34.2 %copy-start.39 = (f32[3,32,4,128]{3,1,2,0:T(8,128)}, f32[3,32,4,128]{3,1,2,0:T(8,128)S(1)}, u32[]{:S(2)}) copy-start(f32[3,32,4,128]{3,1,2,0:T(8,128)S(1)} %fusion) | copy-start | bytes 589828
  569.8 228.8 %all-gather.69.cloned.1.call-start = ((), (), s32[]{:S(2)}) async-start(), calls=%async_computation.19 | async-start | bytes 1114112 | tf_op jit(solution)/shard_map/all_gather | solution.py:62
  608.2 204.1 %all-gather.55.cloned.1.call-start = ((), (), s32[]{:S(2)}) async-start(), calls=%async_computation.12 | async-start | bytes 1310720 | tf_op jit(solution)/shard_map/all_gather | solution.py:74
  775.2 119.4 %copy-start.5 = (f32[128,512]{1,0:T(8,128)}, f32[128,512]{1,0:T(8,128)S(1)}, u32[]{:S(2)}) copy-start(f32[128,512]{1,0:T(8,128)S(1)} %fusion.141) | copy-start | bytes 786436
  775.2 12.6 copy-start.3
  775.2 12.6 copy-start.15
  777.9 116.7 %copy-start.17 = (f32[128,512]{1,0:T(8,128)}, f32[128,512]{1,0:T(8,128)S(1)}, u32[]{:S(2)}) copy-start(f32[128,512]{1,0:T(8,128)S(1)} %fusion.139) | copy-start | bytes 786436
  785.2 67.8 %all-gather.63.cloned.1.call-start = ((), (), s32[]{:S(2)}) async-start(), calls=%async_computation.16 | async-start | bytes 1114112 | tf_op jit(solution)/shard_map/all_gather | solution.py:61
  798.1 94.0 %all-gather.71.cloned.1.call-start = ((), (), s32[]{:S(2)}) async-start(), calls=%async_computation.20 | async-start | bytes 1114112 | tf_op jit(solution)/shard_map/all_gather | solution.py:62
  805.2 50.4 %copy-start.29 = (f32[128,512]{1,0:T(8,128)S(1)}, f32[128,512]{1,0:T(8,128)}, u32[]{:S(2)}) copy-start(f32[128,512]{1,0:T(8,128)} %copy-done.28) | copy-start | bytes 786436
  810.1 49.5 %copy-start.45 = (f32[2,32,4,128]{3,1,2,0:T(8,128)}, f32[2,32,4,128]{3,1,2,0:T(8,128)S(1)}, u32[]{:S(2)}) copy-start(f32[2,32,4,128]{3,1,2,0:T(8,128)S(1)} %fusion.3) | copy-start | bytes 393220
  810.8 108.1 %all-gather.57.cloned.1.call-start = ((), (), s32[]{:S(2)}) async-start(), calls=%async_computation.13 | async-start | bytes 1310720 | tf_op jit(solution)/shard_map/all_gather | solution.py:65
  814.9 47.2 %copy-start.47 = (f32[2,32,4,128]{3,1,2,0:T(8,128)S(1)}, f32[2,32,4,128]{3,1,2,0:T(8,128)}, u32[]{:S(2)}) copy-start(f32[2,32,4,128]{3,1,2,0:T(8,128)} %copy-done.46) | copy-start | bytes 393220
  835.7 253.7 %all-gather.65.cloned.1.call-start = ((), (), s32[]{:S(2)}) async-start(), calls=%async_computation.17 | async-start | bytes 1114112 | tf_op jit(solution)/shard_map/all_gather | solution.py:61
  865.1 235.0 %all-gather.73.cloned.1.call-start = ((), (), s32[]{:S(2)}) async-start(), calls=%async_computation.21 | async-start | bytes 1114112 | tf_op jit(solution)/shard_map/all_gather | solution.py:62
  904.3 218.5 %all-gather.47.cloned.1.call-start = ((), (), s32[]{:S(2)}) async-start(), calls=%async_computation.7 | async-start | bytes 1310720 | tf_op jit(solution)/shard_map/all_gather | solution.py:30
  1083.7 18.0 %copy-start.7 = (f32[128,512]{1,0:T(8,128)}, f32[128,512]{1,0:T(8,128)S(1)}, u32[]{:S(2)}) copy-start(f32[128,512]{1,0:T(8,128)S(1)} %fusion.135) | copy-start | bytes 786436
  1086.4 15.3 %copy-start.19 = (f32[128,512]{1,0:T(8,128)}, f32[128,512]{1,0:T(8,128)S(1)}, u32[]{:S(2)}) copy-start(f32[128,512]{1,0:T(8,128)S(1)} %fusion.133) | copy-start | bytes 786436
  1089.3 12.4 copy-start.31
  1094.8 5.3 copy-start.33
  1095.7 55.9 %all-gather.45.cloned.1.call-start = ((), (), s32[]{:S(2)}) async-start(), calls=%async_computation.5 | async-start | bytes 1310720 | tf_op jit(solution)/shard_map/all_gather | solution.py:30
  1104.6 19.9 %copy-start.34 = (f32[4,32,512]{2,1,0:T(8,128)S(1)}, f32[4,32,512]{2,1,0:T(8,128)}, u32[]{:S(2)}) copy-start(f32[4,32,512]{2,1,0:T(8,128)} %copy-done.33) | copy-start | bytes 786436
  1106.4 358.7 %reduce-scatter.5.cloned.1.call-start = ((), (), s32[]{:S(2)}) async-start(), calls=%async_computation.8 | async-start | bytes 4456448 | tf_op jit(solution)/shard_map/reduce_scatter | solution.py:34
  1129.5 376.3 %reduce-scatter.3.cloned.1.call-start = ((), (), s32[]{:S(2)}) async-start(), calls=%async_computation.6 | async-start | bytes 4456448 | tf_op jit(solution)/shard_map/reduce_scatter | solution.py:34
  1153.2 5.6 slice-start.1
  1153.2 24.9 %copy-start.1 = (f32[128,512]{1,0:T(8,128)S(1)}, f32[128,512]{1,0:T(8,128)}, u32[]{:S(2)}) copy-start(f32[128,512]{1,0:T(8,128)} %copy-done) | copy-start | bytes 786436
  1153.2 24.9 %copy-start.13 = (f32[128,512]{1,0:T(8,128)S(1)}, f32[128,512]{1,0:T(8,128)}, u32[]{:S(2)}) copy-start(f32[128,512]{1,0:T(8,128)} %copy-done.11) | copy-start | bytes 786436
  1158.2 25.9 %copy-start.10 = (f32[512,3,32]{0,2,1:T(8,128)S(1)}, f32[512,3,32]{0,2,1:T(8,128)}, u32[]{:S(2)}) copy-start(f32[512,3,32]{0,2,1:T(8,128)} %copy-done.9) | copy-start | bytes 589828
  1158.2 43.5 %copy-start.4 = (f32[128,512]{1,0:T(8,128)S(1)}, f32[128,512]{1,0:T(8,128)}, u32[]{:S(2)}) copy-start(f32[128,512]{1,0:T(8,128)} %copy-done.2) | copy-start | bytes 786436
  1158.2 43.5 %copy-start.16 = (f32[128,512]{1,0:T(8,128)S(1)}, f32[128,512]{1,0:T(8,128)}, u32[]{:S(2)}) copy-start(f32[128,512]{1,0:T(8,128)} %copy-done.14) | copy-start | bytes 786436
  1158.2 65.3 %copy-start.6 = (f32[128,512]{1,0:T(8,128)S(1)}, f32[128,512]{1,0:T(8,128)}, u32[]{:S(2)}) copy-start(f32[128,512]{1,0:T(8,128)} %copy-done.5) | copy-start | bytes 786436
  1158.2 65.3 %copy-start.18 = (f32[128,512]{1,0:T(8,128)S(1)}, f32[128,512]{1,0:T(8,128)}, u32[]{:S(2)}) copy-start(f32[128,512]{1,0:T(8,128)} %copy-done.17) | copy-start | bytes 786436
  1179.9 43.6 %copy-start.30 = (f32[128,512]{1,0:T(8,128)S(1)}, f32[128,512]{1,0:T(8,128)}, u32[]{:S(2)}) copy-start(f32[128,512]{1,0:T(8,128)} %copy-done.28) | copy-start | bytes 786436
  1179.9 65.6 %copy-start.8 = (f32[128,512]{1,0:T(8,128)S(1)}, f32[128,512]{1,0:T(8,128)}, u32[]{:S(2)}) copy-start(f32[128,512]{1,0:T(8,128)} %copy-done.7) | copy-start | bytes 786436
  1179.9 65.6 %copy-start.20 = (f32[128,512]{1,0:T(8,128)S(1)}, f32[128,512]{1,0:T(8,128)}, u32[]{:S(2)}) copy-start(f32[128,512]{1,0:T(8,128)} %copy-done.19) | copy-start | bytes 786436
  1179.9 65.6 %copy-start.32 = (f32[128,512]{1,0:T(8,128)S(1)}, f32[128,512]{1,0:T(8,128)}, u32[]{:S(2)}) copy-start(f32[128,512]{1,0:T(8,128)} %copy-done.31) | copy-start | bytes 786436
  1202.9 42.6 %copy-start.38 = (f32[1,512,1,128]{3,1,2,0:T(8,128)S(1)}, f32[1,512,1,128]{3,1,2,0:T(8,128)}, u32[]{:S(2)}) copy-start(f32[1,512,1,128]{3,1,2,0:T(8,128)} %all-gather.6) | copy-start | bytes 786436
  1202.9 43.6 %copy-start.62 = (s32[32]{0:T(128)S(1)}, s32[32]{0:T(128)}, u32[]{:S(2)}) copy-start(s32[32]{0:T(128)} %iota_add_fusion) | copy-start | bytes 388
  1202.9 43.6 %copy-start.63 = (s32[128]{0:T(128)S(1)}, s32[128]{0:T(128)}, u32[]{:S(2)}) copy-start(s32[128]{0:T(128)} %iota_add_fusion.1) | copy-start | bytes 1540
  1223.5 25.1 %copy-start.60 = (f32[32,64]{1,0:T(8,128)S(1)}, f32[32,64]{1,0:T(8,128)}, u32[]{:S(2)}) copy-start(f32[32,64]{1,0:T(8,128)} %copy.156) | copy-start | bytes 24580
  1223.5 239.4 %copy-start.61 = (f32[64,64]{1,0:T(8,128)S(1)}, f32[64,64]{1,0:T(8,128)}, u32[]{:S(2)}) copy-start(f32[64,64]{1,0:T(8,128)} %param.38) | copy-start | bytes 49156
  1224.7 279.1 %copy-start.55 = (f32[1,1,1,32,4,1,128]{6,5,4,3,2,1,0:T(1,128)S(1)}, f32[1,1,1,32,4,1,128]{6,5,4,3,2,1,0:T(1,128)}, u32[]{:S(2)}) copy-start(f32[1,1,1,32,4,1,128]{6,5,4,3,2,1,0:T(1,128)} %stack.85) | copy-start | bytes 196612
  1224.7 280.1 %copy-start.54 = (f32[1,1,1,32,4,1,128]{6,5,4,3,2,1,0:T(1,128)S(1)}, f32[1,1,1,32,4,1,128]{6,5,4,3,2,1,0:T(1,128)}, u32[]{:S(2)}) copy-start(f32[1,1,1,32,4,1,128]{6,5,4,3,2,1,0:T(1,128)} %stack.90) | copy-start | bytes 196612
  1225.7 281.3 %copy-start.53 = (f32[1,4,1,32,4,1,128]{6,5,4,3,2,1,0:T(1,128)S(1)}, f32[1,4,1,32,4,1,128]{6,5,4,3,2,1,0:T(1,128)}, u32[]{:S(2)}) copy-start(f32[1,4,1,32,4,1,128]{6,5,4,3,2,1,0:T(1,128)} %param.36) | copy-start | bytes 786436
  1465.0 42.0 %collective-permute-start = (f32[128,512]{1,0:T(8,128)}, f32[128,512]{1,0:T(8,128)S(1)}, u32[]{:S(2)}, u32[]{:S(2)}) collective-permute-start(f32[128,512]{1,0:T(8,128)} %reduce-scatter.5.cloned.1.call-done), channel_id=1, source_target_pairs={{64,0},{128,64},{192,128},{65,1},{129,65},{193,129},{66,2},{130,66... | collective-permute-start | bytes 786440 | tf_op jit(solution)/shard_map/ppermute | solution.py:10
  (23 other events, 20.0 us)
Sparse Core Ops, SparseCore 0:
  10.4 41.4 all-gather.48
  54.2 25.1 all-gather.38
  227.6 45.5 all-gather.50
  298.9 24.9 all-gather.40
  481.4 36.8 all-gather.52
  520.6 39.4 all-gather.58
  561.9 37.2 all-gather.66
  601.6 25.1 all-gather.42
  628.6 39.4 all-gather.60
  669.8 37.2 all-gather.68
  785.3 27.0 all-gather.54
  814.1 38.8 all-gather.62
  854.8 37.1 all-gather.70
  893.7 25.1 all-gather.56
  920.7 39.2 all-gather.64
  961.6 37.5 all-gather.72
  1095.8 26.9 all-gather.46
  1124.5 27.0 all-gather.44
  1154.1 64.1 reduce-scatter.4
  1220.7 62.9 reduce-scatter.2
where the time goes:
time: 1530 us; the launch traced here: 1520 us
  other arithmetic  503 us (33%)
  blocking collectives  338 us (22%)
  waiting for transfers between devices  323 us (21%)
  local copies, waits for them, and re-layouts  159 us (10%)
  matrix products  126 us (8%)
  starting transfers between devices  40 us (3%)
  between operations  26.5 us (2%)
    another operation x59, other arithmetic, per_device(): factor = jnp.linalg.cholesky(diagonal_full)  329 us
    psum x1, blocking collectives, per_device(): arrow_total = lax.psum(arrow_local, ('tm', 'col'))  214 us
    another operation x9, other arithmetic, lower_inverse(): lax.linalg.triangular_solve(factor, identity, left_side=True, lower=True)  161 us
    all_gather x3, waiting for transfers between devices, per_device(): lax.all_gather(owned[:, 1:, None, :], 'row', axis=2, tiled=True)  77.4 us
    all_gather x4, waiting for transfers between devices, per_device(): lax.all_gather(gathered_day[:, 0:1, :], 'row', axis=1, tiled=True)  76.9 us
    dot_general x31, matrix products, product(): jnp.dot(left, right, precision=lax.Precision.HIGHEST, preferred_element_t...  73.6 us
    all_gather x4, blocking collectives, per_device(): lax.all_gather(arrow_part[current], 'col', axis=0, tiled=True)  66.3 us
    all_gather x3, blocking collectives, per_device(): lax.all_gather(matrix[current, :, current:, :], 'col', axis=0, tiled=True)  58.1 us
  transfers between devices with their start and end apart: 21, of which 15 were waited for; matrix products, arithmetic and copies ran while one was open for 31% of the time, Pallas kernels for 0%

commit v1 on v0

--- a/solution.py
+++ b/solution.py
@@ -126,7 +126,8 @@
     from_next = passed_along(left_term, "tm", -1)
     separator = separator_local - right_term - from_next
     arrow_local = product(arrow_solved.T, arrow_solved)
-    arrow_total = lax.psum(arrow_local, ("tm", "col"))
+    arrow_local = jnp.where(row_index == 0, arrow_local, 0.0)
+    arrow_total = lax.psum(arrow_local, ("tm", "row", "col"))
     arrowhead = arrow_block - arrow_total
     return (
         day_factor,

time: 1530 us -> 1360 us (0.89)
  blocking collectives: 338 us -> 199 us
  starting transfers between devices: 40 us -> 5.53 us
    psum x1, blocking collectives: 214 us -> 74.6 us  [per_device(): arrow_total = lax.psum(arrow_local, ('tm', 'row', 'col'))]
    ppermute x1, starting transfers between devices: 37.8 us -> 3.33 us  [passed_along(): lax.ppermute(value, axis, [(source, source + steps) for source in range(i...]
  transfers between devices with their start and end apart: 21 -> 21, of which waited for: 15 -> 15; matrix products, arithmetic and copies ran while one was open for 31% -> 35% of each run, Pallas kernels for 0% -> 0%
where the time goes in v1:
time: 1360 us; the launch traced here: 1340 us
  other arithmetic  503 us (37%)
  waiting for transfers between devices  325 us (24%)
  blocking collectives  199 us (15%)
  local copies, waits for them, and re-layouts  159 us (12%)
  matrix products  126 us (9%)
  between operations  26.5 us (2%)
    another operation x59, other arithmetic, per_device(): factor = jnp.linalg.cholesky(diagonal_full)  329 us
    another operation x9, other arithmetic, lower_inverse(): lax.linalg.triangular_solve(factor, identity, left_side=True, lower=True)  161 us
    all_gather x3, waiting for transfers between devices, per_device(): lax.all_gather(owned[:, 1:, None, :], 'row', axis=2, tiled=True)  77.4 us
    all_gather x4, waiting for transfers between devices, per_device(): lax.all_gather(gathered_day[:, 0:1, :], 'row', axis=1, tiled=True)  76.9 us
    psum x1, blocking collectives, per_device(): arrow_total = lax.psum(arrow_local, ('tm', 'row', 'col'))  74.6 us
    dot_general x31, matrix products, product(): jnp.dot(left, right, precision=lax.Precision.HIGHEST, preferred_element_t...  73.6 us
    all_gather x4, blocking collectives, per_device(): lax.all_gather(arrow_part[current], 'col', axis=0, tiled=True)  66.2 us
    all_gather x3, blocking collectives, per_device(): lax.all_gather(matrix[current, :, current:, :], 'col', axis=0, tiled=True)  58.1 us
  transfers between devices with their start and end apart: 21, of which 15 were waited for; matrix products, arithmetic and copies ran while one was open for 35% of the time, Pallas kernels for 0%

profile of v1, /device:TPU:8, one launch (start us, length us, event | category | flops | bytes accessed | tf_op | source)
XLA Modules:
  0.0 1344.5 jit_solution(15966232665213219999)
XLA Ops:
  8.8 43.1 %all-gather.49.cloned.1.call-done = f32[1,1,1,512,4,1,128]{6,4,5,2,1,0,3:T(4,128)} async-done(((f32[1,1,1,32,4,1,128]{6,4,5,2,1,0,3:T(4,128)}), f32[1,1,1,512,4,1,128]{6,4,5,2,1,0,3:T(4,128)}) %all-gather.49.cloned.1.call-update) | async-done | bytes 1048592 | tf_op jit(solution)/shard_map/all_gather | solution.py:60
  56.7 22.7 %all-gather.39.cloned.1.call-done = f32[512,4,128]{2,0,1:T(8,128)} async-done(((f32[512,1,128]{2,0,1:T(8,128)}), f32[512,4,128]{2,0,1:T(8,128)}) %all-gather.39.cloned.1.call-update) | async-done | bytes 1048592 | tf_op jit(solution)/shard_map/all_gather | solution.py:65
  82.6 11.7 cholesky.462
  94.3 9.8 custom-call.35
  106.8 11.7 cholesky.481
  118.5 10.2 custom-call.36
  130.3 11.7 cholesky.502
  142.7 9.8 custom-call.37
  154.0 11.9 cholesky.519
  169.9 8.0 while.20
  177.9 39.3 %custom-call.38 = f32[4,128,128]{1,2,0:T(8,128)S(1)} custom-call(f32[4,128,128]{2,1,0:T(8,128)S(1)} %get-tuple-element.178), custom_call_target="InvertDiagBlocksLowerTriangular" | custom-call | tf_op jit(solution)/shard_map/triangular_solve/custom-call.3 | solution.py:19
  229.1 44.2 %all-gather.51.cloned.1.call-done = f32[512,3,512]{2,0,1:T(8,128)} async-done(((f32[512,3,128]{2,0,1:T(8,128)}), f32[512,3,512]{2,0,1:T(8,128)}) %all-gather.51.cloned.1.call-update) | async-done | bytes 3145744 | tf_op jit(solution)/shard_map/all_gather | solution.py:74
  278.4 19.6 %all-gather.2 = f32[1,512,3,128]{3,1,2,0:T(8,128)S(1)} all-gather(f32[1,32,3,128]{3,1,2,0:T(8,128)S(1)} %slice.678), channel_id=4, replica_groups=mesh['tm'=4,'row'=4,'col'=16] {'col'}, dimensions={1}, use_global_device_ids=true | all-gather | bytes 835584 | tf_op jit(solution)/shard_map/all_gather | solution.py:60
  300.2 23.7 %all-gather.41.cloned.1.call-done = f32[512,4,128]{2,0,1:T(8,128)} async-done(((f32[512,1,128]{2,0,1:T(8,128)}), f32[512,4,128]{2,0,1:T(8,128)}) %all-gather.41.cloned.1.call-update) | async-done | bytes 1048592 | tf_op jit(solution)/shard_map/all_gather | solution.py:65
  329.1 11.7 cholesky.534
  341.5 9.8 custom-call.39
  354.0 11.7 cholesky.553
  366.4 10.2 custom-call.40
  378.2 11.7 cholesky.574
  390.6 9.8 custom-call.41
  401.8 11.9 cholesky.591
  418.2 11.6 while.21
  429.8 39.3 %custom-call.42 = f32[4,128,128]{1,2,0:T(8,128)S(1)} custom-call(f32[4,128,128]{2,1,0:T(8,128)S(1)} %get-tuple-element.179), custom_call_target="InvertDiagBlocksLowerTriangular" | custom-call | tf_op jit(solution)/shard_map/triangular_solve/custom-call.3 | solution.py:19
  486.5 31.8 %all-gather.53.cloned.1.call-done = f32[512,2,512]{2,0,1:T(8,128)} async-done(((f32[512,2,128]{2,0,1:T(8,128)}), f32[512,2,512]{2,0,1:T(8,128)}) %all-gather.53.cloned.1.call-update) | async-done | bytes 2097168 | tf_op jit(solution)/shard_map/all_gather | solution.py:74
  523.3 19.0 %all-gather.4 = f32[1,512,2,128]{3,1,2,0:T(8,128)S(1)} all-gather(f32[1,32,2,128]{3,1,2,0:T(8,128)S(1)} %slice.689), channel_id=6, replica_groups=mesh['tm'=4,'row'=4,'col'=16] {'col'}, dimensions={1}, use_global_device_ids=true | all-gather | bytes 557056 | tf_op jit(solution)/shard_map/all_gather | solution.py:60
  543.9 16.2 %all-gather.59.cloned.1.call-done = f32[1,1,1,512,4,1,128]{6,4,5,2,1,0,3:T(4,128)} async-done(((f32[1,1,1,32,4,1,128]{6,4,5,2,1,0,3:T(4,128)}), f32[1,1,1,512,4,1,128]{6,4,5,2,1,0,3:T(4,128)}) %all-gather.59.cloned.1.call-update) | async-done | bytes 1048592 | tf_op jit(solution)/shard_map/all_gather | solution.py:61
  560.1 4.0 fusion.20
  571.4 27.8 %all-gather.67.cloned.1.call-done = f32[1,1,1,512,4,1,128]{6,4,5,2,1,0,3:T(4,128)} async-done(((f32[1,1,1,32,4,1,128]{6,4,5,2,1,0,3:T(4,128)}), f32[1,1,1,512,4,1,128]{6,4,5,2,1,0,3:T(4,128)}) %all-gather.67.cloned.1.call-update) | async-done | bytes 1048592 | tf_op jit(solution)/shard_map/all_gather | solution.py:62
  610.7 16.1 %all-gather.43.cloned.1.call-done = f32[512,4,128]{2,0,1:T(8,128)} async-done(((f32[512,1,128]{2,0,1:T(8,128)}), f32[512,4,128]{2,0,1:T(8,128)}) %all-gather.43.cloned.1.call-update) | async-done | bytes 1048592 | tf_op jit(solution)/shard_map/all_gather | solution.py:65
  632.0 11.7 cholesky.606
  644.4 9.8 custom-call.43
  657.5 11.7 cholesky.625
  669.9 10.0 custom-call.44
  682.4 11.7 cholesky.646
  694.8 9.8 custom-call.45
  706.0 11.9 cholesky.663
  722.3 11.5 while.22
  733.8 39.3 %custom-call.46 = f32[4,128,128]{1,2,0:T(8,128)S(1)} custom-call(f32[4,128,128]{2,1,0:T(8,128)S(1)} %get-tuple-element.180), custom_call_target="InvertDiagBlocksLowerTriangular" | custom-call | tf_op jit(solution)/shard_map/triangular_solve/custom-call.3 | solution.py:19
  787.8 4.1 fusion.197
  801.1 4.0 fusion.196
  816.1 19.5 %all-gather.6 = f32[1,512,1,128]{3,1,2,0:T(8,128)} all-gather(f32[1,32,1,128]{3,1,2,0:T(8,128)S(1)} %fusion.16), channel_id=8, replica_groups=mesh['tm'=4,'row'=4,'col'=16] {'col'}, dimensions={1}, use_global_device_ids=true | all-gather | bytes 278528 | tf_op jit(solution)/shard_map/all_gather | solution.py:60
  835.7 17.2 %all-gather.63.cloned.1.call-done = f32[1,512,4,128]{3,1,2,0:T(8,128)} async-done(((f32[1,32,4,128]{3,1,2,0:T(8,128)}), f32[1,512,4,128]{3,1,2,0:T(8,128)}) %all-gather.63.cloned.1.call-update) | async-done | bytes 1048592 | tf_op jit(solution)/shard_map/all_gather | solution.py:61
  855.5 4.1 fusion.195
  868.1 24.0 %all-gather.71.cloned.1.call-done = f32[1,512,4,128]{3,1,2,0:T(8,128)} async-done(((f32[1,32,4,128]{3,1,2,0:T(8,128)}), f32[1,512,4,128]{3,1,2,0:T(8,128)}) %all-gather.71.cloned.1.call-update) | async-done | bytes 1048592 | tf_op jit(solution)/shard_map/all_gather | solution.py:62
  894.6 4.1 fusion.194
  904.5 14.4 %all-gather.57.cloned.1.call-done = f32[1,512,4,128]{3,1,0,2:T(8,128)} async-done(((f32[1,512,1,128]{3,1,0,2:T(8,128)}), f32[1,512,4,128]{3,1,0,2:T(8,128)}) %all-gather.57.cloned.1.call-update) | async-done | bytes 1048592 | tf_op jit(solution)/shard_map/all_gather | solution.py:65
  924.2 11.7 cholesky.678
  936.6 10.4 custom-call.47
  951.8 13.2 cholesky.697
  967.1 11.5 custom-call.48
  982.4 13.2 cholesky.718
  997.7 11.3 custom-call.49
  1011.9 13.6 %cholesky.735 = f32[128,128]{1,0:T(8,128)} custom-call(f32[128,128]{1,0:T(8,128)} %convolution_subtract_fusion.20), custom_call_target="Cholesky" | custom-call | tf_op jit(solution)/shard_map/jit(cholesky)/cholesky | solution.py:68
  1030.7 11.6 while.23
  1042.3 39.3 %custom-call.50 = f32[4,128,128]{1,2,0:T(8,128)S(1)} custom-call(f32[4,128,128]{2,1,0:T(8,128)S(1)} %get-tuple-element.181), custom_call_target="InvertDiagBlocksLowerTriangular" | custom-call | tf_op jit(solution)/shard_map/triangular_solve/custom-call.3 | solution.py:19
  1106.4 16.4 %all-gather.47.cloned.1.call-done = f32[128,4,4,128]{3,0,1,2:T(8,128)} async-done(((f32[128,4,1,128]{3,0,1,2:T(8,128)}), f32[128,4,4,128]{3,0,1,2:T(8,128)}) %all-gather.47.cloned.1.call-update) | async-done | bytes 1048592 | tf_op jit(solution)/shard_map/all_gather | solution.py:30
  1124.5 5.0 fusion.203
  1129.7 21.8 %all-gather.45.cloned.1.call-done = f32[128,4,4,128]{3,0,1,2:T(8,128)} async-done(((f32[128,4,1,128]{3,0,1,2:T(8,128)}), f32[128,4,4,128]{3,0,1,2:T(8,128)}) %all-gather.45.cloned.1.call-update) | async-done | bytes 1048592 | tf_op jit(solution)/shard_map/all_gather | solution.py:30
  1153.2 5.0 fusion.202
  1158.8 18.3 %all-gather.16 = f32[1,1,1,512,64]{4,3,2,1,0:T(8,128)S(1)} all-gather(f32[1,1,1,32,64]{4,3,2,1,0:T(8,128)S(1)} %slice-done.1), channel_id=18, replica_groups=mesh['tm'=4,'row'=4,'col'=16] {'col'}, dimensions={3}, use_global_device_ids=true | all-gather | bytes 139264 | tf_op jit(solution)/shard_map/all_gather | solution.py:63
  1186.0 15.8 %all-gather.17 = f32[1,512,64]{2,1,0:T(8,128)S(1)} all-gather(f32[1,32,64]{2,1,0:T(8,128)S(1)} %slice.716), channel_id=19, replica_groups=mesh['tm'=4,'row'=4,'col'=16] {'col'}, dimensions={1}, use_global_device_ids=true | all-gather | bytes 139264 | tf_op jit(solution)/shard_map/all_gather | solution.py:63
  1207.3 16.2 %all-gather.18 = f32[1,512,64]{2,1,0:T(8,128)S(1)} all-gather(f32[1,32,64]{2,1,0:T(8,128)S(1)} %slice.718), channel_id=20, replica_groups=mesh['tm'=4,'row'=4,'col'=16] {'col'}, dimensions={1}, use_global_device_ids=true | all-gather | bytes 139264 | tf_op jit(solution)/shard_map/all_gather | solution.py:63
  1229.5 15.9 %all-gather.19 = f32[1,512,64]{2,1,0:T(8,128)S(1)} all-gather(f32[1,32,64]{2,1,0:T(8,128)S(1)} %fusion.14), channel_id=21, replica_groups=mesh['tm'=4,'row'=4,'col'=16] {'col'}, dimensions={1}, use_global_device_ids=true | all-gather | bytes 139264 | tf_op jit(solution)/shard_map/all_gather | solution.py:63
  1248.8 74.6 %psum.7 = f32[64,64]{1,0:T(8,128)S(1)} all-reduce(f32[64,64]{1,0:T(8,128)S(1)} %fusion.12), channel_id=1, replica_groups=mesh['tm'=4,'row'=4,'col'=16] {'tm','row','col'}, use_global_device_ids=true, to_apply=%region_10.0 | all-reduce | flops 4096 | bytes 32768 | tf_op jit(solution)/shard_map/psum | solution.py:130
  (478 shorter events, 296.6 us)
Async XLA Ops:
  7.2 44.7 %all-gather.49.cloned.1.call-start = ((), (), s32[]{:S(2)}) async-start(), calls=%async_computation.9 | async-start | bytes 1114112 | tf_op jit(solution)/shard_map/all_gather | solution.py:60
  8.7 70.7 %all-gather.39.cloned.1.call-start = ((), (), s32[]{:S(2)}) async-start(), calls=%async_computation.2 | async-start | bytes 1310720 | tf_op jit(solution)/shard_map/all_gather | solution.py:65
  54.0 219.3 %all-gather.51.cloned.1.call-start = ((), (), s32[]{:S(2)}) async-start(), calls=%async_computation.10 | async-start | bytes 3932160 | tf_op jit(solution)/shard_map/all_gather | solution.py:74
  177.9 39.8 %copy-start.23 = (f32[512,512]{1,0:T(8,128)}, f32[512,512]{1,0:T(8,128)S(1)}, u32[]{:S(2)}) copy-start(f32[512,512]{1,0:T(8,128)S(1)} %get-tuple-element.505) | copy-start | bytes 3145732
  219.8 7.7 copy-start.59
  220.3 378.9 %copy-start = (f32[128,512]{1,0:T(8,128)}, f32[128,512]{1,0:T(8,128)S(1)}, u32[]{:S(2)}) copy-start(f32[128,512]{1,0:T(8,128)S(1)} %fusion.152) | copy-start | bytes 786436
  222.4 53.1 %copy-start.11 = (f32[128,512]{1,0:T(8,128)}, f32[128,512]{1,0:T(8,128)S(1)}, u32[]{:S(2)}) copy-start(f32[128,512]{1,0:T(8,128)S(1)} %fusion.151) | copy-start | bytes 786436
  227.5 96.4 %all-gather.41.cloned.1.call-start = ((), (), s32[]{:S(2)}) async-start(), calls=%async_computation.3 | async-start | bytes 1310720 | tf_op jit(solution)/shard_map/all_gather | solution.py:65
  276.9 327.9 %copy-start.9 = (f32[512,3,32]{0,2,1:T(8,128)}, f32[512,3,32]{0,2,1:T(8,128)S(1)}, u32[]{:S(2)}) copy-start(f32[512,3,32]{0,2,1:T(8,128)S(1)} %copy.124) | copy-start | bytes 589828
  298.7 219.6 %all-gather.53.cloned.1.call-start = ((), (), s32[]{:S(2)}) async-start(), calls=%async_computation.11 | async-start | bytes 2621440 | tf_op jit(solution)/shard_map/all_gather | solution.py:74
  469.1 3.4 copy-start.50
  472.9 47.4 %copy-start.2 = (f32[128,512]{1,0:T(8,128)}, f32[128,512]{1,0:T(8,128)S(1)}, u32[]{:S(2)}) copy-start(f32[128,512]{1,0:T(8,128)S(1)} %fusion.146) | copy-start | bytes 786436
  480.5 79.6 %copy-start.12 = (f32[128,512]{1,0:T(8,128)S(1)}, f32[128,512]{1,0:T(8,128)}, u32[]{:S(2)}) copy-start(f32[128,512]{1,0:T(8,128)} %copy-done.11) | copy-start | bytes 786436
  481.3 78.8 %all-gather.59.cloned.1.call-start = ((), (), s32[]{:S(2)}) async-start(), calls=%async_computation.14 | async-start | bytes 1114112 | tf_op jit(solution)/shard_map/all_gather | solution.py:61
  482.9 116.3 %all-gather.67.cloned.1.call-start = ((), (), s32[]{:S(2)}) async-start(), calls=%async_computation.18 | async-start | bytes 1114112 | tf_op jit(solution)/shard_map/all_gather | solution.py:62
  484.4 142.4 %all-gather.43.cloned.1.call-start = ((), (), s32[]{:S(2)}) async-start(), calls=%async_computation.4 | async-start | bytes 1310720 | tf_op jit(solution)/shard_map/all_gather | solution.py:65
  520.4 46.3 %slice-start = ((f32[1,4,1,32,4,1,128]{6,5,4,3,2,1,0:T(1,128)}), f32[1,3,1,32,4,1,128]{6,5,4,3,2,1,0:T(1,128)S(1)}, s32[]{:S(2)}) async-start(f32[1,4,1,32,4,1,128]{6,5,4,3,2,1,0:T(1,128)} %param.34), calls=%async_computation.22 | async-start | bytes 393216 | tf_op jit(solution)/shard_map/slice.420
  523.3 45.8 %copy-start.57 = (f32[2,32,2,128]{3,1,2,0:T(8,128)}, f32[2,32,2,128]{3,1,2,0:T(8,128)S(1)}, u32[]{:S(2)}) copy-start(f32[2,32,2,128]{3,1,2,0:T(8,128)S(1)} %fusion.9) | copy-start | bytes 196612
  543.8 241.4 %all-gather.61.cloned.1.call-start = ((), (), s32[]{:S(2)}) async-start(), calls=%async_computation.15 | async-start | bytes 1114112 | tf_op jit(solution)/shard_map/all_gather | solution.py:61
  569.1 34.2 %copy-start.39 = (f32[3,32,4,128]{3,1,2,0:T(8,128)}, f32[3,32,4,128]{3,1,2,0:T(8,128)S(1)}, u32[]{:S(2)}) copy-start(f32[3,32,4,128]{3,1,2,0:T(8,128)S(1)} %fusion) | copy-start | bytes 589828
  569.8 228.8 %all-gather.69.cloned.1.call-start = ((), (), s32[]{:S(2)}) async-start(), calls=%async_computation.19 | async-start | bytes 1114112 | tf_op jit(solution)/shard_map/all_gather | solution.py:62
  608.2 204.1 %all-gather.55.cloned.1.call-start = ((), (), s32[]{:S(2)}) async-start(), calls=%async_computation.12 | async-start | bytes 1310720 | tf_op jit(solution)/shard_map/all_gather | solution.py:74
  775.2 119.4 %copy-start.5 = (f32[128,512]{1,0:T(8,128)}, f32[128,512]{1,0:T(8,128)S(1)}, u32[]{:S(2)}) copy-start(f32[128,512]{1,0:T(8,128)S(1)} %fusion.142) | copy-start | bytes 786436
  775.2 12.6 copy-start.3
  775.2 12.6 copy-start.15
  777.9 116.7 %copy-start.17 = (f32[128,512]{1,0:T(8,128)}, f32[128,512]{1,0:T(8,128)S(1)}, u32[]{:S(2)}) copy-start(f32[128,512]{1,0:T(8,128)S(1)} %fusion.140) | copy-start | bytes 786436
  785.2 67.8 %all-gather.63.cloned.1.call-start = ((), (), s32[]{:S(2)}) async-start(), calls=%async_computation.16 | async-start | bytes 1114112 | tf_op jit(solution)/shard_map/all_gather | solution.py:61
  798.1 94.0 %all-gather.71.cloned.1.call-start = ((), (), s32[]{:S(2)}) async-start(), calls=%async_computation.20 | async-start | bytes 1114112 | tf_op jit(solution)/shard_map/all_gather | solution.py:62
  805.2 50.4 %copy-start.29 = (f32[128,512]{1,0:T(8,128)S(1)}, f32[128,512]{1,0:T(8,128)}, u32[]{:S(2)}) copy-start(f32[128,512]{1,0:T(8,128)} %copy-done.28) | copy-start | bytes 786436
  810.1 49.5 %copy-start.45 = (f32[2,32,4,128]{3,1,2,0:T(8,128)}, f32[2,32,4,128]{3,1,2,0:T(8,128)S(1)}, u32[]{:S(2)}) copy-start(f32[2,32,4,128]{3,1,2,0:T(8,128)S(1)} %fusion.3) | copy-start | bytes 393220
  810.8 108.1 %all-gather.57.cloned.1.call-start = ((), (), s32[]{:S(2)}) async-start(), calls=%async_computation.13 | async-start | bytes 1310720 | tf_op jit(solution)/shard_map/all_gather | solution.py:65
  814.9 47.2 %copy-start.47 = (f32[2,32,4,128]{3,1,2,0:T(8,128)S(1)}, f32[2,32,4,128]{3,1,2,0:T(8,128)}, u32[]{:S(2)}) copy-start(f32[2,32,4,128]{3,1,2,0:T(8,128)} %copy-done.46) | copy-start | bytes 393220
  835.7 253.7 %all-gather.65.cloned.1.call-start = ((), (), s32[]{:S(2)}) async-start(), calls=%async_computation.17 | async-start | bytes 1114112 | tf_op jit(solution)/shard_map/all_gather | solution.py:61
  865.1 235.0 %all-gather.73.cloned.1.call-start = ((), (), s32[]{:S(2)}) async-start(), calls=%async_computation.21 | async-start | bytes 1114112 | tf_op jit(solution)/shard_map/all_gather | solution.py:62
  904.3 218.5 %all-gather.47.cloned.1.call-start = ((), (), s32[]{:S(2)}) async-start(), calls=%async_computation.7 | async-start | bytes 1310720 | tf_op jit(solution)/shard_map/all_gather | solution.py:30
  1083.7 18.0 %copy-start.7 = (f32[128,512]{1,0:T(8,128)}, f32[128,512]{1,0:T(8,128)S(1)}, u32[]{:S(2)}) copy-start(f32[128,512]{1,0:T(8,128)S(1)} %fusion.136) | copy-start | bytes 786436
  1086.4 15.3 %copy-start.19 = (f32[128,512]{1,0:T(8,128)}, f32[128,512]{1,0:T(8,128)S(1)}, u32[]{:S(2)}) copy-start(f32[128,512]{1,0:T(8,128)S(1)} %fusion.134) | copy-start | bytes 786436
  1089.3 12.4 copy-start.31
  1094.8 5.3 copy-start.33
  1095.7 55.9 %all-gather.45.cloned.1.call-start = ((), (), s32[]{:S(2)}) async-start(), calls=%async_computation.5 | async-start | bytes 1310720 | tf_op jit(solution)/shard_map/all_gather | solution.py:30
  1104.6 19.9 %copy-start.34 = (f32[4,32,512]{2,1,0:T(8,128)S(1)}, f32[4,32,512]{2,1,0:T(8,128)}, u32[]{:S(2)}) copy-start(f32[4,32,512]{2,1,0:T(8,128)} %copy-done.33) | copy-start | bytes 786436
  1106.4 219.2 %reduce-scatter.5.cloned.1.call-start = ((), (), s32[]{:S(2)}) async-start(), calls=%async_computation.8 | async-start | bytes 4456448 | tf_op jit(solution)/shard_map/reduce_scatter | solution.py:34
  1129.5 202.3 %reduce-scatter.3.cloned.1.call-start = ((), (), s32[]{:S(2)}) async-start(), calls=%async_computation.6 | async-start | bytes 4456448 | tf_op jit(solution)/shard_map/reduce_scatter | solution.py:34
  1153.2 5.6 slice-start.1
  1153.2 25.0 %copy-start.1 = (f32[128,512]{1,0:T(8,128)S(1)}, f32[128,512]{1,0:T(8,128)}, u32[]{:S(2)}) copy-start(f32[128,512]{1,0:T(8,128)} %copy-done) | copy-start | bytes 786436
  1153.2 24.9 %copy-start.13 = (f32[128,512]{1,0:T(8,128)S(1)}, f32[128,512]{1,0:T(8,128)}, u32[]{:S(2)}) copy-start(f32[128,512]{1,0:T(8,128)} %copy-done.11) | copy-start | bytes 786436
  1158.2 25.9 %copy-start.10 = (f32[512,3,32]{0,2,1:T(8,128)S(1)}, f32[512,3,32]{0,2,1:T(8,128)}, u32[]{:S(2)}) copy-start(f32[512,3,32]{0,2,1:T(8,128)} %copy-done.9) | copy-start | bytes 589828
  1158.2 43.5 %copy-start.4 = (f32[128,512]{1,0:T(8,128)S(1)}, f32[128,512]{1,0:T(8,128)}, u32[]{:S(2)}) copy-start(f32[128,512]{1,0:T(8,128)} %copy-done.2) | copy-start | bytes 786436
  1158.2 43.5 %copy-start.16 = (f32[128,512]{1,0:T(8,128)S(1)}, f32[128,512]{1,0:T(8,128)}, u32[]{:S(2)}) copy-start(f32[128,512]{1,0:T(8,128)} %copy-done.14) | copy-start | bytes 786436
  1158.2 65.3 %copy-start.6 = (f32[128,512]{1,0:T(8,128)S(1)}, f32[128,512]{1,0:T(8,128)}, u32[]{:S(2)}) copy-start(f32[128,512]{1,0:T(8,128)} %copy-done.5) | copy-start | bytes 786436
  1158.2 65.3 %copy-start.18 = (f32[128,512]{1,0:T(8,128)S(1)}, f32[128,512]{1,0:T(8,128)}, u32[]{:S(2)}) copy-start(f32[128,512]{1,0:T(8,128)} %copy-done.17) | copy-start | bytes 786436
  1180.0 43.6 %copy-start.30 = (f32[128,512]{1,0:T(8,128)S(1)}, f32[128,512]{1,0:T(8,128)}, u32[]{:S(2)}) copy-start(f32[128,512]{1,0:T(8,128)} %copy-done.28) | copy-start | bytes 786436
  1180.0 65.4 %copy-start.8 = (f32[128,512]{1,0:T(8,128)S(1)}, f32[128,512]{1,0:T(8,128)}, u32[]{:S(2)}) copy-start(f32[128,512]{1,0:T(8,128)} %copy-done.7) | copy-start | bytes 786436
  1180.0 65.4 %copy-start.20 = (f32[128,512]{1,0:T(8,128)S(1)}, f32[128,512]{1,0:T(8,128)}, u32[]{:S(2)}) copy-start(f32[128,512]{1,0:T(8,128)} %copy-done.19) | copy-start | bytes 786436
  1180.0 65.4 %copy-start.32 = (f32[128,512]{1,0:T(8,128)S(1)}, f32[128,512]{1,0:T(8,128)}, u32[]{:S(2)}) copy-start(f32[128,512]{1,0:T(8,128)} %copy-done.31) | copy-start | bytes 786436
  1202.9 42.5 %copy-start.38 = (f32[1,512,1,128]{3,1,2,0:T(8,128)S(1)}, f32[1,512,1,128]{3,1,2,0:T(8,128)}, u32[]{:S(2)}) copy-start(f32[1,512,1,128]{3,1,2,0:T(8,128)} %all-gather.6) | copy-start | bytes 786436
  1202.9 43.5 %copy-start.62 = (s32[32]{0:T(128)S(1)}, s32[32]{0:T(128)}, u32[]{:S(2)}) copy-start(s32[32]{0:T(128)} %iota_add_fusion) | copy-start | bytes 388
  1202.9 43.5 %copy-start.63 = (s32[128]{0:T(128)S(1)}, s32[128]{0:T(128)}, u32[]{:S(2)}) copy-start(s32[128]{0:T(128)} %iota_add_fusion.1) | copy-start | bytes 1540
  1223.6 24.9 %copy-start.60 = (f32[32,64]{1,0:T(8,128)S(1)}, f32[32,64]{1,0:T(8,128)}, u32[]{:S(2)}) copy-start(f32[32,64]{1,0:T(8,128)} %copy.156) | copy-start | bytes 24580
  1223.6 99.8 %copy-start.61 = (f32[64,64]{1,0:T(8,128)S(1)}, f32[64,64]{1,0:T(8,128)}, u32[]{:S(2)}) copy-start(f32[64,64]{1,0:T(8,128)} %param.38) | copy-start | bytes 49156
  1224.7 105.1 %copy-start.55 = (f32[1,1,1,32,4,1,128]{6,5,4,3,2,1,0:T(1,128)S(1)}, f32[1,1,1,32,4,1,128]{6,5,4,3,2,1,0:T(1,128)}, u32[]{:S(2)}) copy-start(f32[1,1,1,32,4,1,128]{6,5,4,3,2,1,0:T(1,128)} %stack.85) | copy-start | bytes 196612
  1224.7 106.1 %copy-start.54 = (f32[1,1,1,32,4,1,128]{6,5,4,3,2,1,0:T(1,128)S(1)}, f32[1,1,1,32,4,1,128]{6,5,4,3,2,1,0:T(1,128)}, u32[]{:S(2)}) copy-start(f32[1,1,1,32,4,1,128]{6,5,4,3,2,1,0:T(1,128)} %stack.90) | copy-start | bytes 196612
  1225.8 109.9 %copy-start.53 = (f32[1,4,1,32,4,1,128]{6,5,4,3,2,1,0:T(1,128)S(1)}, f32[1,4,1,32,4,1,128]{6,5,4,3,2,1,0:T(1,128)}, u32[]{:S(2)}) copy-start(f32[1,4,1,32,4,1,128]{6,5,4,3,2,1,0:T(1,128)} %param.36) | copy-start | bytes 786436
  1325.5 10.1 collective-permute-start
  (23 other events, 20.0 us)
Sparse Core Ops, SparseCore 0:
  10.4 41.4 all-gather.48
  54.2 25.1 all-gather.38
  227.6 45.5 all-gather.50
  298.9 24.9 all-gather.40
  481.4 36.8 all-gather.52
  520.6 39.4 all-gather.58
  561.9 37.2 all-gather.66
  601.6 25.1 all-gather.42
  628.6 39.4 all-gather.60
  669.8 37.2 all-gather.68
  785.3 27.0 all-gather.54
  814.1 38.8 all-gather.62
  854.8 37.1 all-gather.70
  893.7 25.1 all-gather.56
  920.7 39.2 all-gather.64
  961.6 37.5 all-gather.72
  1095.8 26.9 all-gather.46
  1124.5 27.0 all-gather.44
  1154.1 64.2 reduce-scatter.4
  1220.7 63.1 reduce-scatter.2

commit v2 on v0

v2 whole, which is shorter than its diff:
```python
import jax
import jax.numpy as jnp
from jax import lax
from jax.sharding import PartitionSpec as P


def passed_along(value, axis, steps):
    count = lax.axis_size(axis)
    initial, last = (max(0, -steps), min(count, count - steps))
    return lax.ppermute(value, axis, [(source, source + steps) for source in range(initial, last)])


def product(left, right):
    return jnp.dot(left, right, precision=lax.Precision.HIGHEST, preferred_element_type=jnp.float32)


def lower_inverse(factor):
    identity = jnp.eye(factor.shape[0], dtype=jnp.float32)
    return lax.linalg.triangular_solve(factor, identity, left_side=True, lower=True)


def reorder_nodes(whole, panels, col_width):
    count = whole.shape[0]
    col_count = lax.axis_size("col")
    spread = whole.reshape(count, panels, col_count, col_width)
    return jnp.transpose(spread, (2, 1, 3, 0)).reshape(col_count * panels * col_width, count)


def separator_term(solved, panels, col_width, row_width):
    whole = lax.all_gather(
        solved.reshape(solved.shape[0], panels, 1, row_width), "row", axis=2, tiled=True
    )
    ordered = reorder_nodes(whole, panels, col_width)
    return lax.psum_scatter(product(ordered, solved), "col", scatter_dimension=0, tiled=True)


def product_tn(left, right):
    return lax.dot_general(
        left,
        right,
        (((0,), (0,)), ((), ())),
        precision=lax.Precision.HIGHEST,
        preferred_element_type=jnp.float32,
    )


def per_device(
    day_block, left_coupling, right_coupling, separator_block, arrow_coupling, arrow_block
):
    panels = day_block.shape[1]
    col_width = day_block.shape[3]
    row_width = day_block.shape[6]
    col_count = lax.axis_size("col")
    row_count = lax.axis_size("row")
    panel_size = col_width * col_count
    arrow_rows = arrow_block.shape[0]
    col_index = lax.axis_index("col")
    row_index = lax.axis_index("row")
    matrix = day_block.reshape(panels, col_width, panels, row_width)
    left_part = left_coupling.reshape(panels, col_width, panels * row_width)
    right_part = right_coupling.reshape(panels, col_width, panels * row_width)
    arrow_part = arrow_coupling.reshape(panels, col_width, arrow_rows)
    left_full = [lax.all_gather(left_part[k], "col", axis=0, tiled=True) for k in range(panels)]
    right_full = [lax.all_gather(right_part[k], "col", axis=0, tiled=True) for k in range(panels)]
    arrow_full = [lax.all_gather(arrow_part[k], "col", axis=0, tiled=True) for k in range(panels)]
    rows_at = col_index * col_width + lax.broadcasted_iota(jnp.int32, (col_width, row_width), 0)
    cols_at = row_index * row_width + lax.broadcasted_iota(jnp.int32, (col_width, row_width), 1)
    per_slice = row_width // col_width
    owner = col_index // per_slice
    offset = (col_index % per_slice) * col_width

    def own_columns(solved):
        spread = solved.reshape(panel_size, panels, row_width)
        picked = lax.dynamic_slice_in_dim(spread, offset, col_width, 2)
        picked = jnp.where(row_index == owner, picked, 0.0)
        return lax.psum(picked, "row").reshape(panel_size, panels * col_width)

    factor_blocks = []
    left_solved = []
    right_solved = []
    arrow_solved = []
    right_term = jnp.zeros((panels * col_width, panels * row_width), jnp.float32)
    left_term = jnp.zeros((panels * col_width, panels * row_width), jnp.float32)
    arrow_term = jnp.zeros((arrow_rows, arrow_rows), jnp.float32)
    for current in range(panels):
        remain = panels - current
        gathered_day = lax.all_gather(matrix[current, :, current:, :], "col", axis=0, tiled=True)
        diagonal_full = lax.all_gather(gathered_day[:, 0:1, :], "row", axis=1, tiled=True).reshape(
            panel_size, panel_size
        )
        factor = jnp.linalg.cholesky(diagonal_full)
        inverse = lower_inverse(factor)
        owned = product(inverse, gathered_day.reshape(panel_size, remain * row_width)).reshape(
            panel_size, remain, row_width
        )
        if remain > 1:
            later = lax.all_gather(owned[:, 1:, None, :], "row", axis=2, tiled=True).reshape(
                panel_size, (remain - 1) * panel_size
            )
        solved_left = product(inverse, left_full[current])
        solved_right = product(inverse, right_full[current])
        solved_arrow = product(inverse, arrow_full[current])
        left_solved.append(solved_left)
        right_solved.append(solved_right)
        arrow_solved.append(solved_arrow)
        right_term = right_term + product_tn(own_columns(solved_right), solved_right)
        left_term = left_term + product_tn(own_columns(solved_left), solved_left)
        arrow_term = arrow_term + product_tn(solved_arrow, solved_arrow)
        mine_rows = lax.dynamic_slice_in_dim(owned, col_index * col_width, col_width, 0)
        diagonal_part = jnp.where(cols_at >= rows_at, mine_rows[:, 0, :], 0.0)
        factor_blocks.append(
            jnp.concatenate(
                [
                    jnp.zeros((col_width, current, row_width), jnp.float32),
                    diagonal_part[:, None, :],
                    mine_rows[:, 1:, :],
                ],
                axis=1,
            )
        )
        if remain > 1:
            mine_later = lax.dynamic_slice_in_dim(
                later.reshape(panel_size, remain - 1, panel_size), col_index * col_width, col_width, 2
            )
            mine_later = mine_later.reshape(panel_size, (remain - 1) * col_width).T
            owned_later = owned[:, 1:, :].reshape(panel_size, (remain - 1) * row_width)
            matrix = matrix.at[current + 1 :, :, current + 1 :, :].add(
                -product(mine_later, owned_later).reshape(
                    remain - 1, col_width, remain - 1, row_width
                )
            )
            left_update = product_tn(later, solved_left)
            right_update = product_tn(later, solved_right)
            arrow_update = product_tn(later, solved_arrow)
            for step in range(remain - 1):
                rows = slice(step * panel_size, (step + 1) * panel_size)
                left_full[current + 1 + step] = left_full[current + 1 + step] - left_update[rows]
                right_full[current + 1 + step] = right_full[current + 1 + step] - right_update[rows]
                arrow_full[current + 1 + step] = arrow_full[current + 1 + step] - arrow_update[rows]
    day_factor = jnp.stack(factor_blocks).reshape(day_block.shape)

    def mine(parts, width):
        whole = jnp.stack(parts).reshape(panels, col_count, col_width, width)
        return lax.dynamic_index_in_dim(whole, col_index, 1, keepdims=False)

    left_out = mine(left_solved, panels * row_width)
    right_out = mine(right_solved, panels * row_width)
    arrow_out = mine(arrow_solved, arrow_rows)
    separator_local = separator_block.reshape(panels * col_width, panels * row_width)
    from_next = passed_along(left_term, "tm", -1)
    separator = separator_local - right_term - from_next
    arrow_total = jnp.sum(lax.all_gather(arrow_term, "tm", axis=0, tiled=False), axis=0)
    arrowhead = arrow_block - arrow_total
    return (
        day_factor,
        left_out.reshape(left_coupling.shape),
        right_out.reshape(right_coupling.shape),
        arrow_out.reshape(arrow_coupling.shape),
        separator.reshape(separator_block.shape),
        arrowhead,
    )


def solution(mesh):
    return jax.shard_map(
        per_device,
        mesh=mesh,
        in_specs=(
            P("tm", None, "col", None, None, "row", None),
            P("tm", None, "col", None, None, "row", None),
            P("tm", None, "col", None, None, "row", None),
            P("tm", None, "col", None, None, "row", None),
            P("tm", None, "col", None, None),
            P(),
        ),
        out_specs=(
            P("tm", None, "col", None, None, "row", None),
            P("tm", None, "col", None, None, "row", None),
            P("tm", None, "col", None, None, "row", None),
            P("tm", None, "col", None, None),
            P("tm", None, "col", None, None, "row", None),
            P(),
        ),
        check_vma=False,
    )
```

time: 1530 us -> 1210 us (0.79)
  blocking collectives: 338 us -> 134 us
  waiting for transfers between devices: 323 us -> 243 us
  starting transfers between devices: 40 us -> 3.59 us
  matrix products: 126 us -> 152 us
  local copies, waits for them, and re-layouts: 159 us -> 134 us
    psum x1 -> x0, blocking collectives: 214 us -> none  [per_device(): arrow_total = lax.psum(arrow_local, ('tm', 'col'))]
    all_gather x10 -> x8, waiting for transfers between devices: 124 us -> 0.74 us  [the longest x4 0.72 us: per_device(): lax.all_gather(left_part[k], 'col', axis=0, tiled=True)]
    dot_general x0 -> x21, matrix products: none -> 54.5 us  [product_tn(): lax.dot_general(left, right, (((0,), (0,)), ((), ())), precision=lax.Prec...]
    ppermute x1, starting transfers between devices: 37.8 us -> 2.45 us  [passed_along(): lax.ppermute(value, axis, [(source, source + steps) for source in range(i...]
    psum x0 -> x1, waiting for transfers between devices: none -> 28.7 us  [own_columns(): return lax.psum(picked, 'row').reshape(panel_size, panels * col_width)]
    dot_general x31 -> x19, matrix products: 73.6 us -> 47.8 us  [product(): jnp.dot(left, right, precision=lax.Precision.HIGHEST, preferred_element_t...]
    all_gather x4 -> x5, blocking collectives: 66.3 us -> 78.2 us  [the longest x4 65.9 us: per_device(): lax.all_gather(arrow_part[k], 'col', axis=0, tiled=True)]
  transfers between devices with their start and end apart: 21 -> 18, of which waited for: 15 -> 10; matrix products, arithmetic and copies ran while one was open for 31% -> 25% of each run, Pallas kernels for 0% -> 0%
where the time goes in v2:
time: 1210 us; the launch traced here: 1200 us
  other arithmetic  508 us (42%)
  waiting for transfers between devices  243 us (20%)
  matrix products  152 us (13%)
  local copies, waits for them, and re-layouts  134 us (11%)
  blocking collectives  134 us (11%)
  between operations  26.2 us (2%)
    another operation x59, other arithmetic, per_device(): factor = jnp.linalg.cholesky(diagonal_full)  320 us
    another operation x9, other arithmetic, lower_inverse(): lax.linalg.triangular_solve(factor, identity, left_side=True, lower=True)  162 us
    all_gather x4, waiting for transfers between devices, per_device(): lax.all_gather(gathered_day[:, 0:1, :], 'row', axis=1, tiled=True)  84.7 us
    all_gather x3, waiting for transfers between devices, per_device(): lax.all_gather(owned[:, 1:, None, :], 'row', axis=2, tiled=True)  79.9 us
    all_gather x4, blocking collectives, per_device(): lax.all_gather(arrow_part[k], 'col', axis=0, tiled=True)  65.9 us
    all_gather x3, blocking collectives, per_device(): lax.all_gather(matrix[current, :, current:, :], 'col', axis=0, tiled=True)  55.5 us
    dot_general x21, matrix products, product_tn(): lax.dot_general(left, right, (((0,), (0,)), ((), ())), precision=lax.Prec...  54.5 us
    another operation x53, local copies, waits for them, and re-layouts, lower_inverse(): lax.linalg.triangular_solve(factor, identity, left_side=True, lower=True)  53.4 us
  transfers between devices with their start and end apart: 18, of which 10 were waited for; matrix products, arithmetic and copies ran while one was open for 25% of the time, Pallas kernels for 0%

profile of v2, /device:TPU:8, one launch (start us, length us, event | category | flops | bytes accessed | tf_op | source)
XLA Modules:
  0.0 1201.3 jit_solution(16378004464532108727)
XLA Ops:
  8.8 43.1 %all-gather.52.cloned.1.call-done = f32[1,1,1,512,4,1,128]{6,4,5,2,1,0,3:T(4,128)} async-done(((f32[1,1,1,32,4,1,128]{6,4,5,2,1,0,3:T(4,128)}), f32[1,1,1,512,4,1,128]{6,4,5,2,1,0,3:T(4,128)}) %all-gather.52.cloned.1.call-update) | async-done | bytes 1048592 | tf_op jit(solution)/shard_map/all_gather | solution.py:87
  57.1 22.3 %all-gather.30.cloned.1.call-done = f32[512,4,128]{2,0,1:T(8,128)} async-done(((f32[512,1,128]{2,0,1:T(8,128)}), f32[512,4,128]{2,0,1:T(8,128)}) %all-gather.30.cloned.1.call-update) | async-done | bytes 1048592 | tf_op jit(solution)/shard_map/all_gather | solution.py:88
  82.5 11.7 cholesky.462
  94.3 9.8 custom-call.35
  106.7 11.7 cholesky.481
  118.5 10.3 custom-call.36
  130.3 11.7 cholesky.502
  142.1 9.8 custom-call.37
  153.3 11.9 cholesky.519
  170.4 10.5 while.11
  180.9 39.9 %custom-call.38 = f32[4,128,128]{1,2,0:T(8,128)} custom-call(f32[4,128,128]{2,1,0:T(8,128)S(1)} %get-tuple-element.70), custom_call_target="InvertDiagBlocksLowerTriangular" | custom-call | tf_op jit(solution)/shard_map/triangular_solve/custom-call.3 | solution.py:19
  233.1 44.2 %all-gather.54.cloned.1.call-done = f32[512,3,512]{2,0,1:T(8,128)} async-done(((f32[512,3,128]{2,0,1:T(8,128)}), f32[512,3,512]{2,0,1:T(8,128)}) %all-gather.54.cloned.1.call-update) | async-done | bytes 3145744 | tf_op jit(solution)/shard_map/all_gather | solution.py:97
  281.8 19.6 %all-gather.2 = f32[1,512,3,128]{3,1,2,0:T(8,128)S(1)} all-gather(f32[1,32,3,128]{3,1,2,0:T(8,128)S(1)} %slice.489), channel_id=4, replica_groups=mesh['tm'=4,'row'=4,'col'=16] {'col'}, dimensions={1}, use_global_device_ids=true | all-gather | bytes 835584 | tf_op jit(solution)/shard_map/all_gather | solution.py:87
  303.5 23.7 %all-gather.32.cloned.1.call-done = f32[512,4,128]{2,0,1:T(8,128)} async-done(((f32[512,1,128]{2,0,1:T(8,128)}), f32[512,4,128]{2,0,1:T(8,128)}) %all-gather.32.cloned.1.call-update) | async-done | bytes 1048592 | tf_op jit(solution)/shard_map/all_gather | solution.py:88
  332.4 11.7 cholesky.534
  344.8 9.8 custom-call.39
  357.2 11.7 cholesky.553
  370.8 10.2 custom-call.40
  382.6 11.7 cholesky.574
  395.0 9.8 custom-call.41
  406.3 11.9 cholesky.591
  422.5 14.0 %while.12 = (s32[]{:T(128)}, f32[512,512]{1,0:T(8,128)}, s32[4,2]{0,1:T(2,128)}, f32[4,128,128]{2,1,0:T(8,128)S(1)}, s32[]{:T(128)}) while((s32[]{:T(128)}, f32[512,512]{1,0:T(8,128)}, s32[4,2]{0,1:T(2,128)}, f32[4,128,128]{2,1,0:T(8,128)S(1)}, s32[]{:T(128)}) %tuple.131), condition=%wide.while_cond.3.clone, body=%wide.while_body.3.clone.sunk | while | flops 2 | bytes 131181 | solution.py:19
  436.5 39.3 %custom-call.42 = f32[4,128,128]{1,2,0:T(8,128)S(1)} custom-call(f32[4,128,128]{2,1,0:T(8,128)S(1)} %get-tuple-element.71), custom_call_target="InvertDiagBlocksLowerTriangular" | custom-call | tf_op jit(solution)/shard_map/triangular_solve/custom-call.3 | solution.py:19
  488.1 35.7 %all-gather.56.cloned.1.call-done = f32[512,2,512]{2,0,1:T(8,128)} async-done(((f32[512,2,128]{2,0,1:T(8,128)}), f32[512,2,512]{2,0,1:T(8,128)}) %all-gather.56.cloned.1.call-update) | async-done | bytes 2097168 | tf_op jit(solution)/shard_map/all_gather | solution.py:97
  527.8 18.9 %all-gather.4 = f32[1,512,2,128]{3,1,2,0:T(8,128)S(1)} all-gather(f32[1,32,2,128]{3,1,2,0:T(8,128)S(1)} %slice.500), channel_id=6, replica_groups=mesh['tm'=4,'row'=4,'col'=16] {'col'}, dimensions={1}, use_global_device_ids=true | all-gather | bytes 557056 | tf_op jit(solution)/shard_map/all_gather | solution.py:87
  555.6 17.0 %all-gather.34.cloned.1.call-done = f32[512,4,128]{2,0,1:T(8,128)} async-done(((f32[512,1,128]{2,0,1:T(8,128)}), f32[512,4,128]{2,0,1:T(8,128)}) %all-gather.34.cloned.1.call-update) | async-done | bytes 1048592 | tf_op jit(solution)/shard_map/all_gather | solution.py:88
  577.8 11.7 cholesky.606
  589.6 9.8 custom-call.43
  602.7 11.7 cholesky.625
  615.8 10.2 custom-call.44
  628.5 11.7 cholesky.646
  640.9 9.8 custom-call.45
  652.1 11.9 cholesky.663
  668.3 14.5 %while.13 = (s32[]{:T(128)}, f32[512,512]{1,0:T(8,128)}, s32[4,2]{0,1:T(2,128)}, f32[4,128,128]{2,1,0:T(8,128)S(1)}, s32[]{:T(128)}) while((s32[]{:T(128)}, f32[512,512]{1,0:T(8,128)}, s32[4,2]{0,1:T(2,128)}, f32[4,128,128]{2,1,0:T(8,128)S(1)}, s32[]{:T(128)}) %tuple.134), condition=%wide.while_cond.3.clone.1, body=%wide.while_body.3.clone.1.sunk | while | flops 2 | bytes 131181 | solution.py:19
  682.8 39.3 %custom-call.46 = f32[4,128,128]{1,2,0:T(8,128)S(1)} custom-call(f32[4,128,128]{2,1,0:T(8,128)S(1)} %get-tuple-element.72), custom_call_target="InvertDiagBlocksLowerTriangular" | custom-call | tf_op jit(solution)/shard_map/triangular_solve/custom-call.3 | solution.py:19
  735.0 18.1 %all-gather.8 = f32[1,1,1,512,64]{4,3,2,1,0:T(8,128)S(1)} all-gather(f32[1,1,1,32,64]{4,3,2,1,0:T(8,128)S(1)} %get-tuple-element.153), channel_id=10, replica_groups=mesh['tm'=4,'row'=4,'col'=16] {'col'}, dimensions={3}, use_global_device_ids=true | all-gather | bytes 139264 | tf_op jit(solution)/shard_map/all_gather | solution.py:65
  753.1 16.1 %all-gather.9 = f32[1,1,1,512,64]{4,2,1,0,3:T(1,128)S(1)} all-gather(f32[1,1,1,32,64]{4,2,1,0,3:T(1,128)S(1)} %bitcast.517), channel_id=11, replica_groups=mesh['tm'=4,'row'=4,'col'=16] {'col'}, dimensions={3}, use_global_device_ids=true | all-gather | bytes 139264 | tf_op jit(solution)/shard_map/all_gather | solution.py:65
  769.9 15.6 %all-gather.10 = f32[1,1,1,512,64]{4,2,1,0,3:T(1,128)S(1)} all-gather(f32[1,1,1,32,64]{4,2,1,0,3:T(1,128)S(1)} %bitcast.516), channel_id=12, replica_groups=mesh['tm'=4,'row'=4,'col'=16] {'col'}, dimensions={3}, use_global_device_ids=true | all-gather | bytes 139264 | tf_op jit(solution)/shard_map/all_gather | solution.py:65
  786.3 16.2 %all-gather.11 = f32[1,1,1,512,64]{4,2,1,0,3:T(1,128)S(1)} all-gather(f32[1,1,1,32,64]{4,2,1,0,3:T(1,128)S(1)} %bitcast.515), channel_id=13, replica_groups=mesh['tm'=4,'row'=4,'col'=16] {'col'}, dimensions={3}, use_global_device_ids=true | all-gather | bytes 139264 | tf_op jit(solution)/shard_map/all_gather | solution.py:65
  824.9 6.8 fusion.179
  831.8 6.8 fusion.177
  843.8 3.7 fusion.7
  848.6 3.4 fusion.9
  858.5 4.8 fusion.180
  863.4 4.8 fusion.178
  868.2 4.0 fusion.6
  872.3 4.3 fusion.8
  881.2 17.0 %all-gather.6 = f32[1,512,1,128]{3,1,2,0:T(8,128)} all-gather(f32[1,32,1,128]{3,1,2,0:T(8,128)S(1)} %fusion.5), channel_id=8, replica_groups=mesh['tm'=4,'row'=4,'col'=16] {'col'}, dimensions={1}, use_global_device_ids=true | all-gather | bytes 278528 | tf_op jit(solution)/shard_map/all_gather | solution.py:87
  910.4 5.1 convolution_subtract_fusion
  916.2 5.0 convolution_subtract_fusion.1
  921.2 21.8 %all-gather.60.cloned.1.call-done = f32[1,512,4,128]{3,1,0,2:T(8,128)} async-done(((f32[1,512,1,128]{3,1,0,2:T(8,128)}), f32[1,512,4,128]{3,1,0,2:T(8,128)}) %all-gather.60.cloned.1.call-update) | async-done | bytes 1048592 | tf_op jit(solution)/shard_map/all_gather | solution.py:88
  946.1 11.7 cholesky.678
  958.5 10.0 custom-call.47
  971.8 11.7 cholesky.697
  985.5 9.8 custom-call.48
  997.8 11.7 cholesky.718
  1010.2 10.0 custom-call.49
  1021.6 11.7 cholesky.735
  1037.7 14.0 %while.14 = (s32[]{:T(128)}, f32[512,512]{1,0:T(8,128)}, s32[4,2]{0,1:T(2,128)}, f32[4,128,128]{2,1,0:T(8,128)S(1)}, s32[]{:T(128)}) while((s32[]{:T(128)}, f32[512,512]{1,0:T(8,128)}, s32[4,2]{0,1:T(2,128)}, f32[4,128,128]{2,1,0:T(8,128)S(1)}, s32[]{:T(128)}) %tuple.137), condition=%wide.while_cond.3.clone.2, body=%wide.while_body.3.clone.2.sunk | while | flops 2 | bytes 131181 | solution.py:19
  1051.8 39.7 %custom-call.50 = f32[4,128,128]{1,2,0:T(8,128)S(1)} custom-call(f32[4,128,128]{2,1,0:T(8,128)S(1)} %get-tuple-element.73), custom_call_target="InvertDiagBlocksLowerTriangular" | custom-call | tf_op jit(solution)/shard_map/triangular_solve/custom-call.3 | solution.py:19
  1104.7 4.1 fusion.169
  1133.8 12.2 %all-gather.12 = f32[256,64]{1,0:T(8,128)S(1)} all-gather(f32[64,64]{1,0:T(8,128)S(1)} %convolution_add_fusion.6), channel_id=14, replica_groups=mesh['tm'=4,'row'=4,'col'=16] {'tm'}, dimensions={0}, use_global_device_ids=true | all-gather | bytes 81920 | tf_op jit(solution)/shard_map/all_gather | solution.py:152
  1148.9 28.7 %all-reduce.5.cloned.1.call-done = (f32[512,128]{0,1:T(8,128)}, f32[512,128]{0,1:T(8,128)}, f32[512,128]{0,1:T(8,128)}, f32[512,128]{0,1:T(8,128)}, f32[512,128]...) async-done(((f32[512,128]{0,1:T(8,128)}, f32[512,128]{0,1:T(8,128)}, f32[512,128]{0,1:T(8,128)}, f32[512,128]{0,1:T(8,128)}, ...) | async-done | bytes 2097168 | tf_op jit(solution)/shard_map/psum | solution.py:76
  1187.2 5.8 collective-permute-done
  (455 shorter events, 280.6 us)
Async XLA Ops:
  7.2 44.7 %all-gather.52.cloned.1.call-start = ((), (), s32[]{:S(2)}) async-start(), calls=%async_computation.11 | async-start | bytes 1114112 | tf_op jit(solution)/shard_map/all_gather | solution.py:87
  8.7 70.7 %all-gather.30.cloned.1.call-start = ((), (), s32[]{:S(2)}) async-start(), calls=%async_computation | async-start | bytes 1310720 | tf_op jit(solution)/shard_map/all_gather | solution.py:88
  54.0 223.3 %all-gather.54.cloned.1.call-start = ((), (), s32[]{:S(2)}) async-start(), calls=%async_computation.12 | async-start | bytes 3932160 | tf_op jit(solution)/shard_map/all_gather | solution.py:97
  54.2 672.0 %copy-start.6 = (f32[512,512]{1,0:T(8,128)}, f32[512,512]{1,0:T(8,128)S(1)}, u32[]{:S(2)}) copy-start(f32[512,512]{1,0:T(8,128)S(1)} %fusion.21) | copy-start | bytes 3145732
  180.9 41.3 %copy-start.39 = (f32[512,512]{1,0:T(8,128)}, f32[512,512]{1,0:T(8,128)S(1)}, u32[]{:S(2)}) copy-start(f32[512,512]{1,0:T(8,128)S(1)} %get-tuple-element.425) | copy-start | bytes 3145732
  180.9 46.7 %copy-start.35 = (f32[1,1,1,512,4,1,128]{3,6,4,5,2,1,0:T(8,128)S(1)}, f32[1,1,1,512,4,1,128]{3,6,4,5,2,1,0:T(8,128)}, u32[]{:S(2)}) copy-start(f32[1,1,1,512,4,1,128]{3,6,4,5,2,1,0:T(8,128)} %copy.110) | copy-start | bytes 3145732
  227.7 5.4 copy-start.29
  231.5 95.7 %all-gather.32.cloned.1.call-start = ((), (), s32[]{:S(2)}) async-start(), calls=%async_computation.1 | async-start | bytes 1310720 | tf_op jit(solution)/shard_map/all_gather | solution.py:88
  302.1 221.7 %all-gather.56.cloned.1.call-start = ((), (), s32[]{:S(2)}) async-start(), calls=%async_computation.13 | async-start | bytes 2621440 | tf_op jit(solution)/shard_map/all_gather | solution.py:97
  477.9 7.0 copy-start.19
  479.8 7.0 copy-start.24
  481.9 44.1 %copy-start.32 = (f32[128,512]{1,0:T(8,128)}, f32[128,512]{1,0:T(8,128)S(1)}, u32[]{:S(2)}) copy-start(f32[128,512]{1,0:T(8,128)S(1)} %fusion.130) | copy-start | bytes 786436
  486.8 85.7 %all-gather.34.cloned.1.call-start = ((), (), s32[]{:S(2)}) async-start(), calls=%async_computation.2 | async-start | bytes 1310720 | tf_op jit(solution)/shard_map/all_gather | solution.py:88
  527.8 19.6 %copy-start.61 = (f32[2,32,2,128]{3,1,2,0:T(8,128)}, f32[2,32,2,128]{3,1,2,0:T(8,128)S(1)}, u32[]{:S(2)}) copy-start(f32[2,32,2,128]{3,1,2,0:T(8,128)S(1)} %fusion.3) | copy-start | bytes 196612
  547.4 259.8 %all-gather.44.cloned.1.call-start = ((), (), s32[]{:S(2)}) async-start(), calls=%async_computation.7 | async-start | bytes 1114112 | tf_op jit(solution)/shard_map/all_gather | solution.py:64
  550.7 261.0 %all-gather.36.cloned.1.call-start = ((), (), s32[]{:S(2)}) async-start(), calls=%async_computation.3 | async-start | bytes 1114112 | tf_op jit(solution)/shard_map/all_gather | solution.py:63
  551.4 292.3 %all-gather.46.cloned.1.call-start = ((), (), s32[]{:S(2)}) async-start(), calls=%async_computation.8 | async-start | bytes 1114112 | tf_op jit(solution)/shard_map/all_gather | solution.py:64
  552.2 296.4 %all-gather.38.cloned.1.call-start = ((), (), s32[]{:S(2)}) async-start(), calls=%async_computation.4 | async-start | bytes 1114112 | tf_op jit(solution)/shard_map/all_gather | solution.py:63
  552.9 315.3 %all-gather.48.cloned.1.call-start = ((), (), s32[]{:S(2)}) async-start(), calls=%async_computation.9 | async-start | bytes 1114112 | tf_op jit(solution)/shard_map/all_gather | solution.py:64
  553.6 318.7 %all-gather.40.cloned.1.call-start = ((), (), s32[]{:S(2)}) async-start(), calls=%async_computation.5 | async-start | bytes 1114112 | tf_op jit(solution)/shard_map/all_gather | solution.py:63
  554.3 322.4 %all-gather.58.cloned.1.call-start = ((), (), s32[]{:S(2)}) async-start(), calls=%async_computation.14 | async-start | bytes 1310720 | tf_op jit(solution)/shard_map/all_gather | solution.py:97
  722.5 8.8 copy-start.22
  724.3 7.9 copy-start.27
  726.1 43.8 %copy-start.36 = (f32[128,512]{1,0:T(8,128)}, f32[128,512]{1,0:T(8,128)S(1)}, u32[]{:S(2)}) copy-start(f32[128,512]{1,0:T(8,128)S(1)} %fusion.125) | copy-start | bytes 786436
  727.8 76.6 %copy-start.30 = (f32[128,512]{1,0:T(8,128)S(1)}, f32[128,512]{1,0:T(8,128)}, u32[]{:S(2)}) copy-start(f32[128,512]{1,0:T(8,128)} %copy-done.29) | copy-start | bytes 786436
  729.1 76.4 %copy-start.44 = (f32[128,512]{1,0:T(8,128)}, f32[128,512]{1,0:T(8,128)S(1)}, u32[]{:S(2)}) copy-start(f32[128,512]{1,0:T(8,128)S(1)} %fusion.124) | copy-start | bytes 786436
  731.3 79.0 %copy-start.50 = (f32[512,2,128]{2,0,1:T(8,128)}, f32[512,2,128]{2,0,1:T(8,128)S(1)}, u32[]{:S(2)}) copy-start(f32[512,2,128]{2,0,1:T(8,128)S(1)} %fusion.16) | copy-start | bytes 1572868
  732.1 178.3 %all-gather.50.cloned.1.call-start = ((), (), s32[]{:S(2)}) async-start(), calls=%async_computation.10 | async-start | bytes 1114112 | tf_op jit(solution)/shard_map/all_gather | solution.py:64
  732.8 183.3 %all-gather.42.cloned.1.call-start = ((), (), s32[]{:S(2)}) async-start(), calls=%async_computation.6 | async-start | bytes 1114112 | tf_op jit(solution)/shard_map/all_gather | solution.py:63
  733.5 209.5 %all-gather.60.cloned.1.call-start = ((), (), s32[]{:S(2)}) async-start(), calls=%async_computation.15 | async-start | bytes 1310720 | tf_op jit(solution)/shard_map/all_gather | solution.py:88
  805.5 6.1 copy-start.31
  810.3 4.7 copy-start
  824.9 15.0 %copy-start.49 = (f32[1536,64]{0,1:T(8,128)}, f32[1536,64]{0,1:T(8,128)S(1)}, u32[]{:S(2)}) copy-start(f32[1536,64]{0,1:T(8,128)S(1)} %fusion.181) | copy-start | bytes 1179652
  824.9 6.8 copy-start.4
  831.7 8.2 copy-start.20
  831.7 8.2 copy-start.25
  831.7 8.2 copy-start.33
  831.7 8.2 copy-start.63
  843.7 4.8 copy-start.21
  843.7 4.8 copy-start.26
  843.7 4.8 copy-start.34
  858.5 4.8 copy-start.9
  863.4 4.8 copy-start.23
  872.2 38.2 %copy-start.11 = (f32[512,512]{1,0:T(8,128)}, f32[512,512]{1,0:T(8,128)S(1)}, u32[]{:S(2)}) copy-start(f32[512,512]{1,0:T(8,128)S(1)} %fusion.6) | copy-start | bytes 3145732
  876.6 39.5 %copy-start.13 = (f32[512,512]{1,0:T(8,128)}, f32[512,512]{1,0:T(8,128)S(1)}, u32[]{:S(2)}) copy-start(f32[512,512]{1,0:T(8,128)S(1)} %fusion.8) | copy-start | bytes 3145732
  898.2 279.3 %all-reduce.5.cloned.1.call-start = ((), (), s32[]{:S(2)}) async-start(), calls=%async_computation.16 | async-start | bytes 4194304 | tf_op jit(solution)/shard_map/psum | solution.py:76
  900.6 9.1 copy-start.66
  969.7 121.8 %copy-start.7 = (f32[512,512]{1,0:T(8,128)S(1)}, f32[512,512]{1,0:T(8,128)}, u32[]{:S(2)}) copy-start(f32[512,512]{1,0:T(8,128)} %copy-done.6) | copy-start | bytes 3145732
  1093.6 11.0 copy-start.28
  1095.5 9.2 copy-start.37
  1098.4 6.2 copy-start.45
  1101.6 9.8 copy-start.16
  1108.7 7.5 copy-start.15
  1113.1 8.4 copy-start.2
  1125.0 5.8 copy-start.64
  1125.0 5.8 copy-start.65
  1177.5 5.0 copy-start.18
  1177.5 5.0 copy-start.55
  1181.0 4.7 copy-start.54
  1181.8 4.7 copy-start.12
  1182.5 10.5 copy-start.17
  1182.5 10.5 copy-start.51
  1182.6 10.5 copy-start.52
  1183.3 9.8 collective-permute-start
  (21 other events, 54.7 us)
Sparse Core Ops, SparseCore 0:
  10.4 41.4 all-gather.51
  54.2 25.1 all-gather.29
  231.6 45.5 all-gather.53
  302.2 24.9 all-gather.31
  487.0 36.8 all-gather.55
  547.5 24.9 all-gather.33
  574.4 39.0 all-gather.43
  615.3 37.4 all-gather.35
  654.6 37.3 all-gather.45
  693.7 37.4 all-gather.37
  733.0 37.0 all-gather.47
  771.8 37.1 all-gather.39
  811.3 25.2 all-gather.57
  838.3 38.9 all-gather.49
  878.9 37.1 all-gather.41
  917.8 25.1 all-gather.59
  1113.2 64.2 all-reduce.4

commit v3 on v2

--- a/solution.py
+++ b/solution.py
@@ -60,9 +60,16 @@
     left_part = left_coupling.reshape(panels, col_width, panels * row_width)
     right_part = right_coupling.reshape(panels, col_width, panels * row_width)
     arrow_part = arrow_coupling.reshape(panels, col_width, arrow_rows)
+    block_rows = []
+    for k in range(panels):
+        remain = panels - k
+        by_col = lax.all_gather(matrix[k, :, k:, :], "col", axis=0, tiled=True)
+        whole = lax.all_gather(by_col[:, :, None, :], "row", axis=2, tiled=True)
+        block_rows.append(whole.reshape(panel_size, remain * panel_size))
     left_full = [lax.all_gather(left_part[k], "col", axis=0, tiled=True) for k in range(panels)]
     right_full = [lax.all_gather(right_part[k], "col", axis=0, tiled=True) for k in range(panels)]
-    arrow_full = [lax.all_gather(arrow_part[k], "col", axis=0, tiled=True) for k in range(panels)]
+    arrow_all = lax.all_gather(arrow_part, "col", axis=1, tiled=True)
+    arrow_full = [arrow_all[k] for k in range(panels)]
     rows_at = col_index * col_width + lax.broadcasted_iota(jnp.int32, (col_width, row_width), 0)
     cols_at = row_index * row_width + lax.broadcasted_iota(jnp.int32, (col_width, row_width), 1)
     per_slice = row_width // col_width
@@ -84,19 +91,14 @@
     arrow_term = jnp.zeros((arrow_rows, arrow_rows), jnp.float32)
     for current in range(panels):
         remain = panels - current
-        gathered_day = lax.all_gather(matrix[current, :, current:, :], "col", axis=0, tiled=True)
-        diagonal_full = lax.all_gather(gathered_day[:, 0:1, :], "row", axis=1, tiled=True).reshape(
-            panel_size, panel_size
-        )
+        block_row = block_rows[current]
+        diagonal_full = block_row[:, :panel_size]
         factor = jnp.linalg.cholesky(diagonal_full)
         inverse = lower_inverse(factor)
-        owned = product(inverse, gathered_day.reshape(panel_size, remain * row_width)).reshape(
-            panel_size, remain, row_width
-        )
-        if remain > 1:
-            later = lax.all_gather(owned[:, 1:, None, :], "row", axis=2, tiled=True).reshape(
-                panel_size, (remain - 1) * panel_size
-            )
+        owned_full = product(inverse, block_row)
+        owned = lax.dynamic_slice_in_dim(
+            owned_full.reshape(panel_size, remain, row_count, row_width), row_index, 1, 2
+        ).reshape(panel_size, remain, row_width)
         solved_left = product(inverse, left_full[current])
         solved_right = product(inverse, right_full[current])
         solved_arrow = product(inverse, arrow_full[current])
@@ -119,16 +121,13 @@
             )
         )
         if remain > 1:
-            mine_later = lax.dynamic_slice_in_dim(
-                later.reshape(panel_size, remain - 1, panel_size), col_index * col_width, col_width, 2
-            )
-            mine_later = mine_later.reshape(panel_size, (remain - 1) * col_width).T
-            owned_later = owned[:, 1:, :].reshape(panel_size, (remain - 1) * row_width)
-            matrix = matrix.at[current + 1 :, :, current + 1 :, :].add(
-                -product(mine_later, owned_later).reshape(
-                    remain - 1, col_width, remain - 1, row_width
+            later = owned_full[:, panel_size:]
+            for step in range(remain - 1):
+                target = current + 1 + step
+                rows = slice(step * panel_size, (step + 1) * panel_size)
+                block_rows[target] = block_rows[target] - product_tn(
+                    later[:, rows], later[:, step * panel_size :]
                 )
-            )
             left_update = product_tn(later, solved_left)
             right_update = product_tn(later, solved_right)
             arrow_update = product_tn(later, solved_arrow)

time: 1210 us -> 1180 us (0.975)
  waiting for transfers between devices: 243 us -> 160 us
  blocking collectives: 134 us -> 89.1 us
  matrix products: 152 us -> 189 us
  other arithmetic: 508 us -> 542 us
  local copies, waits for them, and re-layouts: 134 us -> 161 us
    all_gather x8 -> x5, waiting for transfers between devices: 208 us -> 127 us  [the longest x4 127 us: per_device(): whole = lax.all_gather(by_col[:, :, None, :], 'row', axis=2, tiled=True)]
    all_gather x7 -> x4, blocking collectives: 121 us -> 77.1 us  [the longest x3 59.6 us: per_device(): by_col = lax.all_gather(matrix[k, :, k:, :], 'col', axis=0, tiled=True)]
    another operation x59, other arithmetic: 320 us -> 349 us  [per_device(): factor = jnp.linalg.cholesky(diagonal_full)]
    dot_general x21 -> x27, matrix products: 54.5 us -> 78.8 us  [product_tn(): lax.dot_general(left, right, (((0,), (0,)), ((), ())), precision=lax.Prec...]
    dot_general x19 -> x16, matrix products: 47.8 us -> 58.4 us  [product(): jnp.dot(left, right, precision=lax.Precision.HIGHEST, preferred_element_t...]
  transfers between devices with their start and end apart: 18 -> 15, of which waited for: 10 -> 5; matrix products, arithmetic and copies ran while one was open for 25% -> 73% of each run, Pallas kernels for 0% -> 0%
where the time goes in v3:
time: 1180 us; the launch traced here: 1170 us
  other arithmetic  542 us (46%)
  matrix products  189 us (16%)
  local copies, waits for them, and re-layouts  161 us (14%)
  waiting for transfers between devices  160 us (14%)
  blocking collectives  89.1 us (8%)
  between operations  26.2 us (2%)
    another operation x59, other arithmetic, per_device(): factor = jnp.linalg.cholesky(diagonal_full)  349 us
    another operation x9, other arithmetic, lower_inverse(): lax.linalg.triangular_solve(factor, identity, left_side=True, lower=True)  166 us
    all_gather x4, waiting for transfers between devices, per_device(): whole = lax.all_gather(by_col[:, :, None, :], 'row', axis=2, tiled=True)  127 us
    dot_general x27, matrix products, product_tn(): lax.dot_general(left, right, (((0,), (0,)), ((), ())), precision=lax.Prec...  78.8 us
    all_gather x3, blocking collectives, per_device(): by_col = lax.all_gather(matrix[k, :, k:, :], 'col', axis=0, tiled=True)  59.6 us
    dot_general x16, matrix products, product(): jnp.dot(left, right, precision=lax.Precision.HIGHEST, preferred_element_t...  58.4 us
    another operation x53, local copies, waits for them, and re-layouts, lower_inverse(): lax.linalg.triangular_solve(factor, identity, left_side=True, lower=True)  45.3 us
    another operation x24, matrix products, per_device(): factor = jnp.linalg.cholesky(diagonal_full)  27.8 us
  transfers between devices with their start and end apart: 15, of which 5 were waited for; matrix products, arithmetic and copies ran while one was open for 73% of the time, Pallas kernels for 0%

profile of v3, /device:TPU:8, one launch (start us, length us, event | category | flops | bytes accessed | tf_op | source)
XLA Modules:
  0.0 1170.1 jit_solution(9855859366023069316)
XLA Ops:
  9.9 22.4 %all-gather.6 = f32[1,512,1,128]{3,2,0,1:T(1,128)} all-gather(f32[1,32,1,128]{3,2,0,1:T(1,128)S(1)} %slice_bitcast_fusion.32), channel_id=8, replica_groups=mesh['tm'=4,'row'=4,'col'=16] {'col'}, dimensions={1}, use_global_device_ids=true | all-gather | bytes 278528 | tf_op jit(solution)/shard_map/all_gather | solution.py:66
  32.4 18.0 %all-gather.4 = f32[1,512,2,128]{3,2,0,1:T(2,128)} all-gather(f32[1,32,2,128]{3,2,0,1:T(2,128)S(1)} %bitcast.423), channel_id=6, replica_groups=mesh['tm'=4,'row'=4,'col'=16] {'col'}, dimensions={1}, use_global_device_ids=true | all-gather | bytes 557056 | tf_op jit(solution)/shard_map/all_gather | solution.py:66
  50.5 19.2 %all-gather.2 = f32[1,512,3,128]{3,0,2,1:T(1,128)} all-gather(f32[1,32,3,128]{3,0,2,1:T(1,128)S(1)} %slice.416), channel_id=4, replica_groups=mesh['tm'=4,'row'=4,'col'=16] {'col'}, dimensions={1}, use_global_device_ids=true | all-gather | bytes 835584 | tf_op jit(solution)/shard_map/all_gather | solution.py:66
  80.3 17.5 %all-gather.8 = f32[1,4,1,512,64]{4,1,2,0,3:T(4,128)S(1)} all-gather(f32[1,4,1,32,64]{4,1,2,0,3:T(4,128)S(1)} %copy.87), channel_id=10, replica_groups=mesh['tm'=4,'row'=4,'col'=16] {'col'}, dimensions={3}, use_global_device_ids=true | all-gather | bytes 557056 | tf_op jit(solution)/shard_map/all_gather | solution.py:71
  105.1 12.6 %all-gather.46.cloned.1.call-done = f32[1,512,2,512]{3,2,0,1:T(2,128)} async-done(((f32[1,512,2,128]{3,2,0,1:T(2,128)}), f32[1,512,2,512]{3,2,0,1:T(2,128)}) %all-gather.46.cloned.1.call-update) | async-done | bytes 2097168 | tf_op jit(solution)/shard_map/all_gather | solution.py:67
  121.8 69.2 %all-gather.44.cloned.1.call-done = f32[1,512,3,512]{3,0,2,1:T(1,128)} async-done(((f32[1,512,3,128]{3,0,2,1:T(1,128)}), f32[1,512,3,512]{3,0,2,1:T(1,128)}) %all-gather.44.cloned.1.call-update) | async-done | bytes 3145744 | tf_op jit(solution)/shard_map/all_gather | solution.py:67
  191.1 8.5 copy.69
  199.6 44.9 %all-gather.42.cloned.1.call-done = f32[1,1,1,512,4,4,128]{6,3,4,2,1,0,5:T(8,128)} async-done(((f32[1,1,1,512,4,1,128]{6,3,4,2,1,0,5:T(8,128)}), f32[1,1,1,512,4,4,128]{6,3,4,2,1,0,5:T(8,128)}) %all-gather.42.cloned.1.call-update) | async-done | bytes 4194320 | tf_op jit(solution)/shard_map/all_gather | solution.py:67
  244.5 5.5 copy.65
  253.1 11.7 %cholesky.462 = f32[128,128]{1,0:T(8,128)S(1)} custom-call(f32[128,128]{1,0:T(8,128)S(1)} %cholesky.746), custom_call_target="Cholesky" | custom-call | tf_op jit(solution)/shard_map/jit(cholesky)/cholesky | solution.py:96
  264.9 9.8 custom-call.35
  275.5 11.7 %cholesky.481 = f32[128,128]{1,0:T(8,128)S(1)} custom-call(f32[128,128]{1,0:T(8,128)S(1)} %cholesky.750), custom_call_target="Cholesky" | custom-call | tf_op jit(solution)/shard_map/jit(cholesky)/cholesky | solution.py:96
  287.2 10.2 custom-call.36
  298.1 11.7 %cholesky.502 = f32[128,128]{1,0:T(8,128)S(1)} custom-call(f32[128,128]{1,0:T(8,128)S(1)} %cholesky.755), custom_call_target="Cholesky" | custom-call | tf_op jit(solution)/shard_map/jit(cholesky)/cholesky | solution.py:96
  309.9 9.8 custom-call.37
  320.3 11.7 %cholesky.519 = f32[128,128]{1,0:T(8,128)S(1)} custom-call(f32[128,128]{1,0:T(8,128)S(1)} %convolution_subtract_fusion.30), custom_call_target="Cholesky" | custom-call | tf_op jit(solution)/shard_map/jit(cholesky)/cholesky | solution.py:96
  336.9 8.0 while.8
  344.9 39.3 %custom-call.38 = f32[4,128,128]{1,2,0:T(8,128)S(1)} custom-call(f32[4,128,128]{2,1,0:T(8,128)S(1)} %get-tuple-element.34), custom_call_target="InvertDiagBlocksLowerTriangular" | custom-call | tf_op jit(solution)/shard_map/triangular_solve/custom-call.3 | solution.py:19
  387.4 7.1 fusion.179
  394.6 5.3 fusion.7
  399.9 5.5 convolution_subtract_fusion
  411.9 11.7 %cholesky.534 = f32[128,128]{1,0:T(8,128)S(1)} custom-call(f32[128,128]{1,0:T(8,128)S(1)} %cholesky.759), custom_call_target="Cholesky" | custom-call | tf_op jit(solution)/shard_map/jit(cholesky)/cholesky | solution.py:96
  423.7 10.0 custom-call.39
  436.3 11.7 %cholesky.553 = f32[128,128]{1,0:T(8,128)S(1)} custom-call(f32[128,128]{1,0:T(8,128)S(1)} %cholesky.763), custom_call_target="Cholesky" | custom-call | tf_op jit(solution)/shard_map/jit(cholesky)/cholesky | solution.py:96
  449.4 9.8 custom-call.40
  460.7 11.8 %cholesky.574 = f32[128,128]{1,0:T(8,128)S(1)} custom-call(f32[128,128]{1,0:T(8,128)S(1)} %cholesky.768), custom_call_target="Cholesky" | custom-call | tf_op jit(solution)/shard_map/jit(cholesky)/cholesky | solution.py:96
  473.2 9.8 custom-call.41
  484.5 11.7 %cholesky.591 = f32[128,128]{1,0:T(8,128)S(1)} custom-call(f32[128,128]{1,0:T(8,128)S(1)} %convolution_subtract_fusion.29), custom_call_target="Cholesky" | custom-call | tf_op jit(solution)/shard_map/jit(cholesky)/cholesky | solution.py:96
  499.4 7.9 while.9
  507.4 39.7 %custom-call.42 = f32[4,128,128]{1,2,0:T(8,128)S(1)} custom-call(f32[4,128,128]{2,1,0:T(8,128)S(1)} %get-tuple-element.35), custom_call_target="InvertDiagBlocksLowerTriangular" | custom-call | tf_op jit(solution)/shard_map/triangular_solve/custom-call.3 | solution.py:19
  551.0 7.1 fusion.175
  562.6 8.1 fusion.2
  570.7 4.6 fusion.23
  577.8 6.0 fusion.12
  588.2 8.1 fusion.4
  600.9 4.8 fusion.14
  618.0 5.9 fusion.9
  632.3 13.2 %cholesky.606 = f32[128,128]{1,0:T(8,128)} custom-call(f32[128,128]{1,0:T(8,128)} %cholesky.772), custom_call_target="Cholesky" | custom-call | tf_op jit(solution)/shard_map/jit(cholesky)/cholesky | solution.py:96
  648.9 11.3 custom-call.43
  664.8 13.2 %cholesky.625 = f32[128,128]{1,0:T(8,128)} custom-call(f32[128,128]{1,0:T(8,128)} %cholesky.776), custom_call_target="Cholesky" | custom-call | tf_op jit(solution)/shard_map/jit(cholesky)/cholesky | solution.py:96
  680.7 11.4 custom-call.44
  696.7 13.2 %cholesky.646 = f32[128,128]{1,0:T(8,128)} custom-call(f32[128,128]{1,0:T(8,128)} %cholesky.781), custom_call_target="Cholesky" | custom-call | tf_op jit(solution)/shard_map/jit(cholesky)/cholesky | solution.py:96
  712.0 11.3 custom-call.45
  727.0 13.6 %cholesky.663 = f32[128,128]{1,0:T(8,128)} custom-call(f32[128,128]{1,0:T(8,128)} %convolution_subtract_fusion.28), custom_call_target="Cholesky" | custom-call | tf_op jit(solution)/shard_map/jit(cholesky)/cholesky | solution.py:96
  748.4 14.0 %while.10 = (s32[]{:T(128)}, f32[512,512]{1,0:T(8,128)}, s32[4,2]{0,1:T(2,128)S(1)}, f32[4,128,128]{2,1,0:T(8,128)}, s32[]{:T(128)}) while((s32[]{:T(128)}, f32[512,512]{1,0:T(8,128)}, s32[4,2]{0,1:T(2,128)S(1)}, f32[4,128,128]{2,1,0:T(8,128)}, s32[]{:T(128)}) %tuple.160), condition=%wide.while_cond.clone.1, body=%wide.while_body.clone.1.sunk | while | flops 2 | bytes 132705 | solution.py:19
  762.4 40.8 %custom-call.46 = f32[4,128,128]{1,2,0:T(8,128)} custom-call(f32[4,128,128]{2,1,0:T(8,128)} %get-tuple-element.36), custom_call_target="InvertDiagBlocksLowerTriangular" | custom-call | tf_op jit(solution)/shard_map/triangular_solve/custom-call.3 | solution.py:19
  811.7 4.9 fusion.174
  826.5 4.8 convolution_subtract_fusion.3
  837.1 13.2 %cholesky.678 = f32[128,128]{1,0:T(8,128)} custom-call(f32[128,128]{1,0:T(8,128)} %cholesky.785), custom_call_target="Cholesky" | custom-call | tf_op jit(solution)/shard_map/jit(cholesky)/cholesky | solution.py:96
  853.7 11.3 custom-call.47
  869.5 13.6 %cholesky.697 = f32[128,128]{1,0:T(8,128)} custom-call(f32[128,128]{1,0:T(8,128)} %cholesky.789), custom_call_target="Cholesky" | custom-call | tf_op jit(solution)/shard_map/jit(cholesky)/cholesky | solution.py:96
  885.8 11.3 custom-call.48
  901.6 13.2 %cholesky.718 = f32[128,128]{1,0:T(8,128)} custom-call(f32[128,128]{1,0:T(8,128)} %cholesky.794), custom_call_target="Cholesky" | custom-call | tf_op jit(solution)/shard_map/jit(cholesky)/cholesky | solution.py:96
  917.0 11.3 custom-call.49
  932.0 13.3 %cholesky.735 = f32[128,128]{1,0:T(8,128)} custom-call(f32[128,128]{1,0:T(8,128)} %convolution_subtract_fusion.27), custom_call_target="Cholesky" | custom-call | tf_op jit(solution)/shard_map/jit(cholesky)/cholesky | solution.py:96
  953.1 14.0 %while.11 = (s32[]{:T(128)}, f32[512,512]{1,0:T(8,128)}, s32[4,2]{0,1:T(2,128)S(1)}, f32[4,128,128]{2,1,0:T(8,128)}, s32[]{:T(128)}) while((s32[]{:T(128)}, f32[512,512]{1,0:T(8,128)}, s32[4,2]{0,1:T(2,128)S(1)}, f32[4,128,128]{2,1,0:T(8,128)}, s32[]{:T(128)}) %tuple.161), condition=%wide.while_cond.clone.2, body=%wide.while_body.clone.2.sunk | while | flops 2 | bytes 132705 | solution.py:19
  967.1 40.8 %custom-call.50 = f32[4,128,128]{1,2,0:T(8,128)} custom-call(f32[4,128,128]{2,1,0:T(8,128)} %get-tuple-element.37), custom_call_target="InvertDiagBlocksLowerTriangular" | custom-call | tf_op jit(solution)/shard_map/triangular_solve/custom-call.3 | solution.py:19
  1017.0 5.0 fusion.22
  1024.6 4.5 convolution_subtract_fusion.1
  1037.8 5.0 fusion.24
  1085.9 6.3 reshape.296
  1105.0 12.1 %all-gather.9 = f32[256,64]{1,0:T(8,128)S(1)} all-gather(f32[64,64]{1,0:T(8,128)S(1)} %convolution_add_fusion.6), channel_id=11, replica_groups=mesh['tm'=4,'row'=4,'col'=16] {'tm'}, dimensions={0}, use_global_device_ids=true | all-gather | bytes 81920 | tf_op jit(solution)/shard_map/all_gather | solution.py:151
  1119.8 26.4 %all-reduce.5.cloned.1.call-done = (f32[512,128]{0,1:T(8,128)}, f32[512,128]{0,1:T(8,128)}, f32[512,128]{0,1:T(8,128)}, f32[512,128]{0,1:T(8,128)}, f32[512,128]...) async-done(((f32[512,128]{0,1:T(8,128)}, f32[512,128]{0,1:T(8,128)}, f32[512,128]{0,1:T(8,128)}, f32[512,128]{0,1:T(8,128)}, ...) | async-done | bytes 2097168 | tf_op jit(solution)/shard_map/psum | solution.py:83
  1156.0 5.9 collective-permute-done
  (488 shorter events, 300.5 us)
Async XLA Ops:
  7.2 62.7 %all-gather.40.cloned.1.call-start = ((), (), s32[]{:S(2)}) async-start(), calls=%async_computation.8 | async-start | bytes 1114112 | tf_op jit(solution)/shard_map/all_gather | solution.py:66
  8.7 93.9 %all-gather.48.cloned.1.call-start = ((), (), s32[]{:S(2)}) async-start(), calls=%async_computation.12 | async-start | bytes 1310720 | tf_op jit(solution)/shard_map/all_gather | solution.py:67
  32.3 39.9 %copy-start.84 = (f32[1,4,1,32,4,1,128]{6,5,4,3,2,1,0:T(1,128)S(1)}, f32[1,4,1,32,4,1,128]{6,5,4,3,2,1,0:T(1,128)}, u32[]{:S(2)}) copy-start(f32[1,4,1,32,4,1,128]{6,5,4,3,2,1,0:T(1,128)} %param.11) | copy-start | bytes 786436
  32.3 39.9 %copy-start.85 = (f32[1,4,1,32,4,1,128]{6,5,4,3,2,1,0:T(1,128)S(1)}, f32[1,4,1,32,4,1,128]{6,5,4,3,2,1,0:T(1,128)}, u32[]{:S(2)}) copy-start(f32[1,4,1,32,4,1,128]{6,5,4,3,2,1,0:T(1,128)} %param.10) | copy-start | bytes 786436
  32.3 85.4 %all-gather.46.cloned.1.call-start = ((), (), s32[]{:S(2)}) async-start(), calls=%async_computation.11 | async-start | bytes 2621440 | tf_op jit(solution)/shard_map/all_gather | solution.py:67
  50.4 140.7 %all-gather.44.cloned.1.call-start = ((), (), s32[]{:S(2)}) async-start(), calls=%async_computation.10 | async-start | bytes 3932160 | tf_op jit(solution)/shard_map/all_gather | solution.py:67
  69.8 10.5 copy-start.88
  69.8 174.7 %all-gather.42.cloned.1.call-start = ((), (), s32[]{:S(2)}) async-start(), calls=%async_computation.9 | async-start | bytes 5242880 | tf_op jit(solution)/shard_map/all_gather | solution.py:67
  72.1 486.0 %all-gather.32.cloned.1.call-start = ((), (), s32[]{:S(2)}) async-start(), calls=%async_computation.4 | async-start | bytes 1114112 | tf_op jit(solution)/shard_map/all_gather | solution.py:70
  74.3 496.3 %all-gather.34.cloned.1.call-start = ((), (), s32[]{:S(2)}) async-start(), calls=%async_computation.5 | async-start | bytes 1114112 | tf_op jit(solution)/shard_map/all_gather | solution.py:70
  75.1 508.7 %all-gather.24.cloned.1.call-start = ((), (), s32[]{:S(2)}) async-start(), calls=%async_computation | async-start | bytes 1114112 | tf_op jit(solution)/shard_map/all_gather | solution.py:69
  75.8 520.5 %all-gather.26.cloned.1.call-start = ((), (), s32[]{:S(2)}) async-start(), calls=%async_computation.1 | async-start | bytes 1114112 | tf_op jit(solution)/shard_map/all_gather | solution.py:69
  76.6 940.4 %all-gather.36.cloned.1.call-start = ((), (), s32[]{:S(2)}) async-start(), calls=%async_computation.6 | async-start | bytes 1114112 | tf_op jit(solution)/shard_map/all_gather | solution.py:70
  77.3 947.3 %all-gather.38.cloned.1.call-start = ((), (), s32[]{:S(2)}) async-start(), calls=%async_computation.7 | async-start | bytes 1114112 | tf_op jit(solution)/shard_map/all_gather | solution.py:70
  78.0 959.8 %all-gather.28.cloned.1.call-start = ((), (), s32[]{:S(2)}) async-start(), calls=%async_computation.2 | async-start | bytes 1114112 | tf_op jit(solution)/shard_map/all_gather | solution.py:69
  78.7 982.5 %all-gather.30.cloned.1.call-start = ((), (), s32[]{:S(2)}) async-start(), calls=%async_computation.3 | async-start | bytes 1114112 | tf_op jit(solution)/shard_map/all_gather | solution.py:69
  79.5 1066.8 %all-reduce.5.cloned.1.call-start = ((), (), s32[]{:S(2)}) async-start(), calls=%async_computation.13 | async-start | bytes 4194304 | tf_op jit(solution)/shard_map/psum | solution.py:83
  79.6 306.7 %copy-start.8 = (f32[512,512]{1,0:T(8,128)}, f32[512,512]{1,0:T(8,128)S(1)}, u32[]{:S(2)}) copy-start(f32[512,512]{1,0:T(8,128)S(1)} %fusion.35) | copy-start | bytes 3145732
  384.6 9.9 copy-start.31
  385.5 9.1 copy-start.39
  386.3 8.3 copy-start.48
  387.4 7.2 copy-start.57
  394.6 10.8 copy-start
  394.6 5.3 copy-start.20
  405.5 5.4 copy-start.3
  434.9 112.2 %copy-start.9 = (f32[512,512]{1,0:T(8,128)S(1)}, f32[512,512]{1,0:T(8,128)}, u32[]{:S(2)}) copy-start(f32[512,512]{1,0:T(8,128)} %copy-done.8) | copy-start | bytes 3145732
  618.0 429.2 %copy-start.65 = (f32[512,64]{0,1:T(8,128)}, f32[512,64]{0,1:T(8,128)S(1)}, u32[]{:S(2)}) copy-start(f32[512,64]{0,1:T(8,128)S(1)} %fusion.176) | copy-start | bytes 393220
  803.2 5.8 copy-start.83
  803.2 8.5 copy-start.22
  804.7 11.9 %copy-start.29 = (f32[128,512]{1,0:T(8,128)}, f32[128,512]{1,0:T(8,128)S(1)}, u32[]{:S(2)}) copy-start(f32[128,512]{1,0:T(8,128)S(1)} %fusion.84) | copy-start | bytes 786436
  807.5 9.1 copy-start.37
  809.5 7.2 copy-start.46
  811.2 5.4 copy-start.61
  811.7 8.6 copy-start.55
  1007.8 5.7 copy-start.82
  1009.3 4.7 copy-start.32
  1045.4 6.3 copy-start.36
  1045.4 6.3 copy-start.45
  1045.4 6.3 copy-start.54
  1045.4 6.3 copy-start.87
  1047.2 7.2 copy-start.30
  1047.2 7.2 copy-start.38
  1047.2 7.2 copy-start.47
  1047.2 7.2 copy-start.56
  1047.2 7.2 copy-start.86
  1055.7 5.6 copy-start.2
  1055.7 5.6 copy-start.16
  1067.0 13.3 %copy-start.5 = (f32[512,512]{1,0:T(8,128)S(1)}, f32[512,512]{1,0:T(8,128)}, u32[]{:S(2)}) copy-start(f32[512,512]{1,0:T(8,128)} %copy-done.4) | copy-start | bytes 3145732
  1067.0 13.3 %copy-start.10 = (f32[512,512]{1,0:T(8,128)S(1)}, f32[512,512]{1,0:T(8,128)}, u32[]{:S(2)}) copy-start(f32[512,512]{1,0:T(8,128)} %fusion.23) | copy-start | bytes 3145732
  1068.4 11.9 %copy-start.14 = (f32[512,512]{1,0:T(8,128)S(1)}, f32[512,512]{1,0:T(8,128)}, u32[]{:S(2)}) copy-start(f32[512,512]{1,0:T(8,128)} %fusion.22) | copy-start | bytes 3145732
  1068.4 11.9 %copy-start.24 = (f32[512,512]{1,0:T(8,128)S(1)}, f32[512,512]{1,0:T(8,128)}, u32[]{:S(2)}) copy-start(f32[512,512]{1,0:T(8,128)} %fusion.171) | copy-start | bytes 3145732
  1071.9 9.2 copy-start.7
  1071.9 9.2 copy-start.12
  1071.9 9.2 copy-start.17
  1071.9 9.2 copy-start.27
  1098.8 5.9 copy-start.69
  1146.3 5.0 copy-start.28
  1146.3 5.0 copy-start.79
  1149.8 4.7 copy-start.78
  1150.5 4.7 copy-start.15
  1151.3 10.6 copy-start.25
  1151.3 10.5 copy-start.75
  1151.3 10.5 copy-start.76
  1152.0 9.8 collective-permute-start
  (40 other events, 108.9 us)
Sparse Core Ops, SparseCore 0:
  10.4 41.4 all-gather.39
  53.6 25.3 all-gather.47
  80.8 36.8 all-gather.45
  119.4 71.6 all-gather.43
  192.7 51.7 all-gather.41
  246.2 39.0 all-gather.31
  287.1 37.5 all-gather.33
  326.5 37.3 all-gather.23
  366.3 37.5 all-gather.25
  405.5 37.2 all-gather.35
  444.7 37.6 all-gather.37
  484.0 37.2 all-gather.27
  523.1 37.2 all-gather.29
  1082.0 64.2 all-reduce.4

commit v4 on v3

--- a/solution.py
+++ b/solution.py
@@ -60,16 +60,29 @@
     left_part = left_coupling.reshape(panels, col_width, panels * row_width)
     right_part = right_coupling.reshape(panels, col_width, panels * row_width)
     arrow_part = arrow_coupling.reshape(panels, col_width, arrow_rows)
-    block_rows = []
-    for k in range(panels):
-        remain = panels - k
-        by_col = lax.all_gather(matrix[k, :, k:, :], "col", axis=0, tiled=True)
+    def gather_block_row(k, after):
+        piece = matrix[k, :, k:, :]
+        if after is not None:
+            piece, _ = lax.optimization_barrier((piece, after))
+        by_col = lax.all_gather(piece, "col", axis=0, tiled=True)
         whole = lax.all_gather(by_col[:, :, None, :], "row", axis=2, tiled=True)
-        block_rows.append(whole.reshape(panel_size, remain * panel_size))
-    left_full = [lax.all_gather(left_part[k], "col", axis=0, tiled=True) for k in range(panels)]
-    right_full = [lax.all_gather(right_part[k], "col", axis=0, tiled=True) for k in range(panels)]
+        return whole.reshape(panel_size, (panels - k) * panel_size)
+
+    def gather_coupling(k, after):
+        pieces = (left_part[k], right_part[k])
+        if after is not None:
+            pieces, _ = lax.optimization_barrier((pieces, after))
+        return tuple(lax.all_gather(piece, "col", axis=0, tiled=True) for piece in pieces)
+
+    block_rows = [gather_block_row(0, None)] + [None] * (panels - 1)
+    left_full = [None] * panels
+    right_full = [None] * panels
+    left_full[0], right_full[0] = gather_coupling(0, None)
     arrow_all = lax.all_gather(arrow_part, "col", axis=1, tiled=True)
     arrow_full = [arrow_all[k] for k in range(panels)]
+    pending = [[] for _ in range(panels)]
+    pending_left = [[] for _ in range(panels)]
+    pending_right = [[] for _ in range(panels)]
     rows_at = col_index * col_width + lax.broadcasted_iota(jnp.int32, (col_width, row_width), 0)
     cols_at = row_index * row_width + lax.broadcasted_iota(jnp.int32, (col_width, row_width), 1)
     per_slice = row_width // col_width
@@ -92,8 +105,18 @@
     for current in range(panels):
         remain = panels - current
         block_row = block_rows[current]
+        for update in pending[current]:
+            block_row = block_row - update
         diagonal_full = block_row[:, :panel_size]
         factor = jnp.linalg.cholesky(diagonal_full)
+        if remain > 1:
+            block_rows[current + 1] = gather_block_row(current + 1, factor)
+            fresh_left, fresh_right = gather_coupling(current + 1, factor)
+            for update in pending_left[current + 1]:
+                fresh_left = fresh_left - update
+            for update in pending_right[current + 1]:
+                fresh_right = fresh_right - update
+            left_full[current + 1], right_full[current + 1] = fresh_left, fresh_right
         inverse = lower_inverse(factor)
         owned_full = product(inverse, block_row)
         owned = lax.dynamic_slice_in_dim(
@@ -125,17 +148,20 @@
             for step in range(remain - 1):
                 target = current + 1 + step
                 rows = slice(step * panel_size, (step + 1) * panel_size)
-                block_rows[target] = block_rows[target] - product_tn(
-                    later[:, rows], later[:, step * panel_size :]
-                )
+                pending[target].append(product_tn(later[:, rows], later[:, step * panel_size :]))
             left_update = product_tn(later, solved_left)
             right_update = product_tn(later, solved_right)
             arrow_update = product_tn(later, solved_arrow)
             for step in range(remain - 1):
                 rows = slice(step * panel_size, (step + 1) * panel_size)
-                left_full[current + 1 + step] = left_full[current + 1 + step] - left_update[rows]
-                right_full[current + 1 + step] = right_full[current + 1 + step] - right_update[rows]
-                arrow_full[current + 1 + step] = arrow_full[current + 1 + step] - arrow_update[rows]
+                target = current + 1 + step
+                if step == 0:
+                    left_full[target] = left_full[target] - left_update[rows]
+                    right_full[target] = right_full[target] - right_update[rows]
+                else:
+                    pending_left[target].append(left_update[rows])
+                    pending_right[target].append(right_update[rows])
+                arrow_full[target] = arrow_full[target] - arrow_update[rows]
     day_factor = jnp.stack(factor_blocks).reshape(day_block.shape)
 
     def mine(parts, width):

time: 1180 us -> 1060 us (0.90)
  waiting for transfers between devices: 160 us -> 109 us
  local copies, waits for them, and re-layouts: 161 us -> 126 us
  other arithmetic: 542 us -> 509 us
    all_gather x13, waiting for transfers between devices: 127 us -> 70 us  [the longest x1 43 us: gather_block_row(): by_col = lax.all_gather(piece, 'col', axis=0, tiled=True)]
    another operation x59, other arithmetic: 349 us -> 321 us  [per_device(): factor = jnp.linalg.cholesky(diagonal_full)]
  transfers between devices with their start and end apart: 15 -> 15, of which waited for: 5 -> 4; matrix products, arithmetic and copies ran while one was open for 73% -> 76% of each run, Pallas kernels for 0% -> 0%
where the time goes in v4:
time: 1060 us; the launch traced here: 1050 us
  other arithmetic  509 us (48%)
  matrix products  188 us (18%)
  local copies, waits for them, and re-layouts  126 us (12%)
  waiting for transfers between devices  109 us (10%)
  blocking collectives  87 us (8%)
  between operations  26.4 us (2%)
    another operation x59, other arithmetic, per_device(): factor = jnp.linalg.cholesky(diagonal_full)  321 us
    another operation x9, other arithmetic, lower_inverse(): lax.linalg.triangular_solve(factor, identity, left_side=True, lower=True)  163 us
    dot_general x27, matrix products, product_tn(): lax.dot_general(left, right, (((0,), (0,)), ((), ())), precision=lax.Prec...  79.9 us
    dot_general x16, matrix products, product(): jnp.dot(left, right, precision=lax.Precision.HIGHEST, preferred_element_t...  60.9 us
    all_gather x3, blocking collectives, gather_block_row(): by_col = lax.all_gather(piece, 'col', axis=0, tiled=True)  56.5 us
    all_gather x1, waiting for transfers between devices, gather_block_row(): by_col = lax.all_gather(piece, 'col', axis=0, tiled=True)  43 us
    another operation x53, local copies, waits for them, and re-layouts, lower_inverse(): lax.linalg.triangular_solve(factor, identity, left_side=True, lower=True)  38.9 us
    psum x1, waiting for transfers between devices, own_columns(): return lax.psum(picked, 'row').reshape(panel_size, panels * col_width)  32.9 us
  transfers between devices with their start and end apart: 15, of which 4 were waited for; matrix products, arithmetic and copies ran while one was open for 76% of the time, Pallas kernels for 0%

profile of v4, /device:TPU:8, one launch (start us, length us, event | category | flops | bytes accessed | tf_op | source)
XLA Modules:
  0.0 1049.3 jit_solution(13707844531146109400)
XLA Ops:
  8.9 43.0 %all-gather.37.cloned.1.call-done = f32[1,1,1,512,4,1,128]{6,4,5,2,1,0,3:T(4,128)} async-done(((f32[1,1,1,32,4,1,128]{6,4,5,2,1,0,3:T(4,128)}), f32[1,1,1,512,4,1,128]{6,4,5,2,1,0,3:T(4,128)}) %all-gather.37.cloned.1.call-update) | async-done | bytes 1048592 | tf_op jit(solution)/shard_map/all_gather | solution.py:67
  57.8 18.4 %all-gather.5 = f32[1,4,1,512,64]{4,1,2,0,3:T(4,128)S(1)} all-gather(f32[1,4,1,32,64]{4,1,2,0,3:T(4,128)S(1)} %copy.85), channel_id=7, replica_groups=mesh['tm'=4,'row'=4,'col'=16] {'col'}, dimensions={3}, use_global_device_ids=true | all-gather | bytes 557056 | tf_op jit(solution)/shard_map/all_gather | solution.py:81
  76.9 26.8 %all-gather.39.cloned.1.call-done = f32[1,1,1,512,4,4,128]{6,3,4,2,1,0,5:T(8,128)} async-done(((f32[1,1,1,512,4,1,128]{6,3,4,2,1,0,5:T(8,128)}), f32[1,1,1,512,4,4,128]{6,3,4,2,1,0,5:T(8,128)}) %all-gather.39.cloned.1.call-update) | async-done | bytes 4194320 | tf_op jit(solution)/shard_map/all_gather | solution.py:68
  103.6 5.5 copy.65
  112.2 11.7 %cholesky.462 = f32[128,128]{1,0:T(8,128)S(1)} custom-call(f32[128,128]{1,0:T(8,128)S(1)} %cholesky.746), custom_call_target="Cholesky" | custom-call | tf_op jit(solution)/shard_map/jit(cholesky)/cholesky | solution.py:111
  124.0 9.8 custom-call.35
  135.2 12.5 %cholesky.481 = f32[128,128]{1,0:T(8,128)S(1)} custom-call(f32[128,128]{1,0:T(8,128)} %cholesky.750), custom_call_target="Cholesky" | custom-call | tf_op jit(solution)/shard_map/jit(cholesky)/cholesky | solution.py:111
  148.4 11.1 %custom-call.36 = f32[1,128,128]{1,2,0:T(8,128)S(1)} custom-call(f32[1,128,128]{2,1,0:T(8,128)} %get-tuple-element.176), custom_call_target="InvertDiagBlocksLowerTriangular" | custom-call | tf_op jit(solution)/shard_map/jit(cholesky)/cholesky | solution.py:111
  160.3 11.7 %cholesky.502 = f32[128,128]{1,0:T(8,128)S(1)} custom-call(f32[128,128]{1,0:T(8,128)S(1)} %cholesky.755), custom_call_target="Cholesky" | custom-call | tf_op jit(solution)/shard_map/jit(cholesky)/cholesky | solution.py:111
  172.0 9.8 custom-call.37
  182.4 11.7 %cholesky.519 = f32[128,128]{1,0:T(8,128)S(1)} custom-call(f32[128,128]{1,0:T(8,128)S(1)} %convolution_subtract_fusion.30), custom_call_target="Cholesky" | custom-call | tf_op jit(solution)/shard_map/jit(cholesky)/cholesky | solution.py:111
  199.0 21.4 %all_gather.59 = f32[512,3,128]{2,0,1:T(8,128)} all-gather(f32[32,3,128]{2,0,1:T(8,128)} %slice_bitcast_fusion.32), channel_id=1, replica_groups=mesh['tm'=4,'row'=4,'col'=16] {'col'}, dimensions={0}, use_global_device_ids=true | all-gather | bytes 835584 | tf_op jit(solution)/shard_map/all_gather | solution.py:67
  230.8 8.0 while.8
  238.9 39.3 %custom-call.38 = f32[4,128,128]{1,2,0:T(8,128)S(1)} custom-call(f32[4,128,128]{2,1,0:T(8,128)S(1)} %get-tuple-element.52), custom_call_target="InvertDiagBlocksLowerTriangular" | custom-call | tf_op jit(solution)/shard_map/triangular_solve/custom-call.3 | solution.py:19
  283.3 8.6 fusion.183
  291.9 6.2 reshape.296
  314.0 4.8 fusion
  318.8 4.9 fusion.7
  323.7 7.6 fusion.2
  331.2 7.1 fusion.4
  341.9 7.8 convolution_subtract_fusion
  356.2 11.7 %cholesky.534 = f32[128,128]{1,0:T(8,128)S(1)} custom-call(f32[128,128]{1,0:T(8,128)S(1)} %cholesky.759), custom_call_target="Cholesky" | custom-call | tf_op jit(solution)/shard_map/jit(cholesky)/cholesky | solution.py:111
  368.1 9.8 custom-call.39
  380.4 11.7 %cholesky.553 = f32[128,128]{1,0:T(8,128)S(1)} custom-call(f32[128,128]{1,0:T(8,128)S(1)} %cholesky.763), custom_call_target="Cholesky" | custom-call | tf_op jit(solution)/shard_map/jit(cholesky)/cholesky | solution.py:111
  392.1 10.2 custom-call.40
  403.9 11.7 %cholesky.574 = f32[128,128]{1,0:T(8,128)S(1)} custom-call(f32[128,128]{1,0:T(8,128)S(1)} %cholesky.768), custom_call_target="Cholesky" | custom-call | tf_op jit(solution)/shard_map/jit(cholesky)/cholesky | solution.py:111
  415.7 9.8 custom-call.41
  427.0 11.7 %cholesky.591 = f32[128,128]{1,0:T(8,128)S(1)} custom-call(f32[128,128]{1,0:T(8,128)S(1)} %convolution_subtract_fusion.29), custom_call_target="Cholesky" | custom-call | tf_op jit(solution)/shard_map/jit(cholesky)/cholesky | solution.py:111
  444.2 17.9 %all_gather.61 = f32[512,2,128]{2,1,0:T(2,128)} all-gather(f32[32,2,128]{2,1,0:T(2,128)S(1)} %copy.73), channel_id=1, replica_groups=mesh['tm'=4,'row'=4,'col'=16] {'col'}, dimensions={0}, use_global_device_ids=true | all-gather | bytes 557056 | tf_op jit(solution)/shard_map/all_gather | solution.py:67
  462.1 8.0 while.9
  470.2 39.3 %custom-call.42 = f32[4,128,128]{1,2,0:T(8,128)S(1)} custom-call(f32[4,128,128]{2,1,0:T(8,128)S(1)} %get-tuple-element.53), custom_call_target="InvertDiagBlocksLowerTriangular" | custom-call | tf_op jit(solution)/shard_map/triangular_solve/custom-call.3 | solution.py:19
  527.5 7.4 fusion.179
  545.7 4.8 fusion.12
  550.5 4.8 fusion.14
  555.4 4.1 copy.74
  559.5 5.5 fusion.9
  572.8 11.7 %cholesky.606 = f32[128,128]{1,0:T(8,128)S(1)} custom-call(f32[128,128]{1,0:T(8,128)S(1)} %cholesky.772), custom_call_target="Cholesky" | custom-call | tf_op jit(solution)/shard_map/jit(cholesky)/cholesky | solution.py:111
  585.7 9.8 custom-call.43
  598.7 11.7 %cholesky.625 = f32[128,128]{1,0:T(8,128)S(1)} custom-call(f32[128,128]{1,0:T(8,128)S(1)} %cholesky.776), custom_call_target="Cholesky" | custom-call | tf_op jit(solution)/shard_map/jit(cholesky)/cholesky | solution.py:111
  612.3 10.2 custom-call.44
  624.9 11.7 %cholesky.646 = f32[128,128]{1,0:T(8,128)S(1)} custom-call(f32[128,128]{1,0:T(8,128)S(1)} %cholesky.781), custom_call_target="Cholesky" | custom-call | tf_op jit(solution)/shard_map/jit(cholesky)/cholesky | solution.py:111
  637.2 9.8 custom-call.45
  649.3 11.7 %cholesky.663 = f32[128,128]{1,0:T(8,128)S(1)} custom-call(f32[128,128]{1,0:T(8,128)S(1)} %convolution_subtract_fusion.28), custom_call_target="Cholesky" | custom-call | tf_op jit(solution)/shard_map/jit(cholesky)/cholesky | solution.py:111
  668.1 11.6 %while.10 = (s32[]{:T(128)}, f32[512,512]{1,0:T(8,128)}, s32[4,2]{0,1:T(2,128)S(1)}, f32[4,128,128]{2,1,0:T(8,128)S(1)}, s32[]{:T(128)}) while((s32[]{:T(128)}, f32[512,512]{1,0:T(8,128)}, s32[4,2]{0,1:T(2,128)S(1)}, f32[4,128,128]{2,1,0:T(8,128)S(1)}, s32[]{:T(128)}) %tuple.178), condition=%wide.while_cond.clone.1, body=%wide.while_body.clone.1.sunk | while | flops 2 | bytes 131181 | solution.py:19
  679.7 39.9 %custom-call.46 = f32[4,128,128]{1,2,0:T(8,128)} custom-call(f32[4,128,128]{2,1,0:T(8,128)S(1)} %get-tuple-element.54), custom_call_target="InvertDiagBlocksLowerTriangular" | custom-call | tf_op jit(solution)/shard_map/triangular_solve/custom-call.3 | solution.py:19
  719.6 17.3 %all_gather.63 = f32[512,1,128]{2,0,1:T(8,128)} all-gather(f32[32,1,128]{2,0,1:T(8,128)S(1)} %copy-done.73), channel_id=1, replica_groups=mesh['tm'=4,'row'=4,'col'=16] {'col'}, dimensions={0}, use_global_device_ids=true | all-gather | bytes 278528 | tf_op jit(solution)/shard_map/all_gather | solution.py:67
  746.1 5.1 fusion.22
  753.8 5.0 fusion.24
  764.6 6.7 fusion.178
  786.8 3.9 convolution_subtract_fusion.5
  795.1 11.7 %cholesky.678 = f32[128,128]{1,0:T(8,128)S(1)} custom-call(f32[128,128]{1,0:T(8,128)S(1)} %cholesky.785), custom_call_target="Cholesky" | custom-call | tf_op jit(solution)/shard_map/jit(cholesky)/cholesky | solution.py:111
  807.0 10.0 custom-call.47
  818.7 11.7 %cholesky.697 = f32[128,128]{1,0:T(8,128)S(1)} custom-call(f32[128,128]{1,0:T(8,128)S(1)} %cholesky.789), custom_call_target="Cholesky" | custom-call | tf_op jit(solution)/shard_map/jit(cholesky)/cholesky | solution.py:111
  831.7 9.8 custom-call.48
  843.1 11.7 %cholesky.718 = f32[128,128]{1,0:T(8,128)S(1)} custom-call(f32[128,128]{1,0:T(8,128)S(1)} %cholesky.794), custom_call_target="Cholesky" | custom-call | tf_op jit(solution)/shard_map/jit(cholesky)/cholesky | solution.py:111
  855.5 10.0 custom-call.49
  866.9 11.7 %cholesky.735 = f32[128,128]{1,0:T(8,128)S(1)} custom-call(f32[128,128]{1,0:T(8,128)S(1)} %convolution_subtract_fusion.27), custom_call_target="Cholesky" | custom-call | tf_op jit(solution)/shard_map/jit(cholesky)/cholesky | solution.py:111
  883.0 11.6 %while.11 = (s32[]{:T(128)}, f32[512,512]{1,0:T(8,128)}, s32[4,2]{0,1:T(2,128)S(1)}, f32[4,128,128]{2,1,0:T(8,128)S(1)}, s32[]{:T(128)}) while((s32[]{:T(128)}, f32[512,512]{1,0:T(8,128)}, s32[4,2]{0,1:T(2,128)S(1)}, f32[4,128,128]{2,1,0:T(8,128)S(1)}, s32[]{:T(128)}) %tuple.179), condition=%wide.while_cond.clone.2, body=%wide.while_body.clone.2.sunk | while | flops 2 | bytes 131181 | solution.py:19
  894.6 40.3 %custom-call.50 = f32[4,128,128]{1,2,0:T(8,128)} custom-call(f32[4,128,128]{2,1,0:T(8,128)S(1)} %get-tuple-element.55), custom_call_target="InvertDiagBlocksLowerTriangular" | custom-call | tf_op jit(solution)/shard_map/triangular_solve/custom-call.3 | solution.py:19
  943.5 4.2 convolution_subtract_fusion.1
  954.9 3.9 convolution_subtract_fusion.2
  973.7 12.0 %all-gather.6 = f32[256,64]{1,0:T(8,128)S(1)} all-gather(f32[64,64]{1,0:T(8,128)S(1)} %convolution_add_fusion.6), channel_id=8, replica_groups=mesh['tm'=4,'row'=4,'col'=16] {'tm'}, dimensions={0}, use_global_device_ids=true | all-gather | bytes 81920 | tf_op jit(solution)/shard_map/all_gather | solution.py:177
  992.5 32.9 %all-reduce.5.cloned.1.call-done = (f32[512,128]{0,1:T(8,128)}, f32[512,128]{0,1:T(8,128)}, f32[512,128]{0,1:T(8,128)}, f32[512,128]{0,1:T(8,128)}, f32[512,128]...) async-done(((f32[512,128]{0,1:T(8,128)}, f32[512,128]{0,1:T(8,128)}, f32[512,128]{0,1:T(8,128)}, f32[512,128]{0,1:T(8,128)}, ...) | async-done | bytes 2097168 | tf_op jit(solution)/shard_map/psum | solution.py:96
  1035.2 5.8 collective-permute-done
  (461 shorter events, 252.1 us)
Async XLA Ops:
  7.2 50.6 %copy-start.50 = (f32[1,4,1,32,4,1,128]{6,5,4,3,2,1,0:T(1,128)S(1)}, f32[1,4,1,32,4,1,128]{6,5,4,3,2,1,0:T(1,128)}, u32[]{:S(2)}) copy-start(f32[1,4,1,32,4,1,128]{6,5,4,3,2,1,0:T(1,128)} %param.9) | copy-start | bytes 786436
  7.2 47.1 %copy-start.66 = (f32[1,4,1,32,4,1,128]{6,5,4,3,2,1,0:T(1,128)S(1)}, f32[1,4,1,32,4,1,128]{6,5,4,3,2,1,0:T(1,128)}, u32[]{:S(2)}) copy-start(f32[1,4,1,32,4,1,128]{6,5,4,3,2,1,0:T(1,128)} %param.10) | copy-start | bytes 786436
  7.2 47.1 %copy-start.65 = (f32[1,4,1,32,4,1,128]{6,5,4,3,2,1,0:T(1,128)S(1)}, f32[1,4,1,32,4,1,128]{6,5,4,3,2,1,0:T(1,128)}, u32[]{:S(2)}) copy-start(f32[1,4,1,32,4,1,128]{6,5,4,3,2,1,0:T(1,128)} %param.11) | copy-start | bytes 786436
  7.2 50.6 %copy-start.74 = (f32[1,4,1,32,64]{4,3,2,1,0:T(8,128)S(1)}, f32[1,4,1,32,64]{4,3,2,1,0:T(8,128)}, u32[]{:S(2)}) copy-start(f32[1,4,1,32,64]{4,3,2,1,0:T(8,128)} %param.13) | copy-start | bytes 98308
  7.2 44.7 %all-gather.37.cloned.1.call-start = ((), (), s32[]{:S(2)}) async-start(), calls=%async_computation.8 | async-start | bytes 1114112 | tf_op jit(solution)/shard_map/all_gather | solution.py:67
  8.8 94.8 %all-gather.39.cloned.1.call-start = ((), (), s32[]{:S(2)}) async-start(), calls=%async_computation.9 | async-start | bytes 5242880 | tf_op jit(solution)/shard_map/all_gather | solution.py:68
  54.2 245.2 %all-gather.29.cloned.1.call-start = ((), (), s32[]{:S(2)}) async-start(), calls=%async_computation.4 | async-start | bytes 1114112 | tf_op jit(solution)/shard_map/all_gather | solution.py:75
  57.0 245.6 %all-gather.21.cloned.1.call-start = ((), (), s32[]{:S(2)}) async-start(), calls=%async_computation | async-start | bytes 1114112 | tf_op jit(solution)/shard_map/all_gather | solution.py:75
  57.7 280.7 %all-gather.41.cloned.1.call-start = ((), (), s32[]{:S(2)}) async-start(), calls=%async_computation.10 | async-start | bytes 3932160 | tf_op jit(solution)/shard_map/all_gather | solution.py:68
  57.8 18.4 %copy-start.49 = (f32[1,4,1,32,4,1,128]{6,3,4,1,5,2,0:T(8,128)}, f32[1,4,1,32,4,1,128]{6,3,4,1,5,2,0:T(8,128)S(1)}, u32[]{:S(2)}) copy-start(f32[1,4,1,32,4,1,128]{6,3,4,1,5,2,0:T(8,128)S(1)} %copy.144) | copy-start | bytes 786436
  199.0 25.2 %copy-start.63 = (f32[32,4,128]{2,1,0:T(4,128)S(1)}, f32[32,4,128]{2,1,0:T(4,128)}, u32[]{:S(2)}) copy-start(f32[32,4,128]{2,1,0:T(4,128)} %get-tuple-element.76) | copy-start | bytes 196612
  199.0 25.8 %copy-start.62 = (f32[32,4,128]{2,1,0:T(4,128)S(1)}, f32[32,4,128]{2,1,0:T(4,128)}, u32[]{:S(2)}) copy-start(f32[32,4,128]{2,1,0:T(4,128)} %get-tuple-element.199) | copy-start | bytes 196612
  199.0 26.4 %copy-start.61 = (f32[32,4,128]{2,1,0:T(4,128)S(1)}, f32[32,4,128]{2,1,0:T(4,128)}, u32[]{:S(2)}) copy-start(f32[32,4,128]{2,1,0:T(4,128)} %get-tuple-element.75) | copy-start | bytes 196612
  199.0 27.0 %copy-start.60 = (f32[32,4,128]{2,1,0:T(4,128)S(1)}, f32[32,4,128]{2,1,0:T(4,128)}, u32[]{:S(2)}) copy-start(f32[32,4,128]{2,1,0:T(4,128)} %get-tuple-element.197) | copy-start | bytes 196612
  220.4 294.3 %all-gather.31.cloned.1.call-start = ((), (), s32[]{:S(2)}) async-start(), calls=%async_computation.5 | async-start | bytes 1114112 | tf_op jit(solution)/shard_map/all_gather | solution.py:75
  228.1 54.7 %copy-start.8 = (f32[512,512]{1,0:T(8,128)}, f32[512,512]{1,0:T(8,128)S(1)}, u32[]{:S(2)}) copy-start(f32[512,512]{1,0:T(8,128)S(1)} %fusion.39) | copy-start | bytes 3145732
  238.9 39.8 %copy-start.43 = (f32[512,512]{1,0:T(8,128)}, f32[512,512]{1,0:T(8,128)S(1)}, u32[]{:S(2)}) copy-start(f32[512,512]{1,0:T(8,128)S(1)} %get-tuple-element.418) | copy-start | bytes 3145732
  278.2 5.1 copy-start.20
  291.9 6.2 copy-start.67
  299.2 220.4 %all-gather.23.cloned.1.call-start = ((), (), s32[]{:S(2)}) async-start(), calls=%async_computation.1 | async-start | bytes 1114112 | tf_op jit(solution)/shard_map/all_gather | solution.py:75
  302.5 21.1 %copy-start.4 = (f32[512,512]{1,0:T(8,128)}, f32[512,512]{1,0:T(8,128)S(1)}, u32[]{:S(2)}) copy-start(f32[512,512]{1,0:T(8,128)S(1)} %fusion.181) | copy-start | bytes 3145732
  306.0 25.2 %copy-start.6 = (f32[512,512]{1,0:T(8,128)}, f32[512,512]{1,0:T(8,128)S(1)}, u32[]{:S(2)}) copy-start(f32[512,512]{1,0:T(8,128)S(1)} %fusion.182) | copy-start | bytes 3145732
  309.7 9.1 copy-start
  309.7 13.9 %copy-start.64 = (f32[32,4,1,128]{3,0,1,2:T(8,128)}, f32[32,4,1,128]{3,0,1,2:T(8,128)S(1)}, u32[]{:S(2)}) copy-start(f32[32,4,1,128]{3,0,1,2:T(8,128)S(1)} %copy.153) | copy-start | bytes 196612
  338.3 217.1 %all-gather.43.cloned.1.call-start = ((), (), s32[]{:S(2)}) async-start(), calls=%async_computation.11 | async-start | bytes 2621440 | tf_op jit(solution)/shard_map/all_gather | solution.py:68
  349.7 5.5 copy-start.3
  368.1 76.1 %copy-start.71 = (f32[32,2,128]{2,0,1:T(8,128)S(1)}, f32[32,2,128]{2,0,1:T(8,128)}, u32[]{:S(2)}) copy-start(f32[32,2,128]{2,0,1:T(8,128)} %slice_bitcast_fusion.33) | copy-start | bytes 98308
  402.3 107.2 %copy-start.9 = (f32[512,512]{1,0:T(8,128)S(1)}, f32[512,512]{1,0:T(8,128)}, u32[]{:S(2)}) copy-start(f32[512,512]{1,0:T(8,128)} %copy-done.8) | copy-start | bytes 3145732
  462.1 284.1 %all-gather.33.cloned.1.call-start = ((), (), s32[]{:S(2)}) async-start(), calls=%async_computation.6 | async-start | bytes 1114112 | tf_op jit(solution)/shard_map/all_gather | solution.py:75
  470.2 39.8 %copy-start.44 = (f32[512,512]{1,0:T(8,128)}, f32[512,512]{1,0:T(8,128)S(1)}, u32[]{:S(2)}) copy-start(f32[512,512]{1,0:T(8,128)S(1)} %get-tuple-element.419) | copy-start | bytes 3145732
  510.7 13.8 %copy-start.31 = (f32[128,512]{1,0:T(8,128)}, f32[128,512]{1,0:T(8,128)S(1)}, u32[]{:S(2)}) copy-start(f32[128,512]{1,0:T(8,128)S(1)} %fusion.144) | copy-start | bytes 786436
  512.6 11.9 %copy-start.37 = (f32[128,512]{1,0:T(8,128)}, f32[128,512]{1,0:T(8,128)S(1)}, u32[]{:S(2)}) copy-start(f32[128,512]{1,0:T(8,128)S(1)} %fusion.142) | copy-start | bytes 786436
  514.7 9.8 copy-start.42
  518.2 4.8 copy-start.11
  519.6 4.9 copy-start.69
  527.5 226.3 %all-gather.25.cloned.1.call-start = ((), (), s32[]{:S(2)}) async-start(), calls=%async_computation.2 | async-start | bytes 1114112 | tf_op jit(solution)/shard_map/all_gather | solution.py:75
  534.9 7.8 copy-start.70
  537.6 8.1 copy-start.12
  538.7 11.8 %copy-start.68 = (f32[32,3,1,128]{3,0,2,1:T(8,128)}, f32[32,3,1,128]{3,0,2,1:T(8,128)S(1)}, u32[]{:S(2)}) copy-start(f32[32,3,1,128]{3,0,2,1:T(8,128)S(1)} %copy.154) | copy-start | bytes 147460
  545.7 4.8 copy-start.15
  555.3 228.9 %all-gather.45.cloned.1.call-start = ((), (), s32[]{:S(2)}) async-start(), calls=%async_computation.12 | async-start | bytes 1310720 | tf_op jit(solution)/shard_map/all_gather | solution.py:68
  597.4 122.2 %copy-start.73 = (f32[32,1,128]{2,0,1:T(8,128)S(1)}, f32[32,1,128]{2,0,1:T(8,128)}, u32[]{:S(2)}) copy-start(f32[32,1,128]{2,0,1:T(8,128)} %slice_bitcast_fusion.34) | copy-start | bytes 49156
  737.0 206.5 %all-gather.35.cloned.1.call-start = ((), (), s32[]{:S(2)}) async-start(), calls=%async_computation.7 | async-start | bytes 1114112 | tf_op jit(solution)/shard_map/all_gather | solution.py:75
  737.0 5.6 copy-start.58
  746.1 208.8 %all-gather.27.cloned.1.call-start = ((), (), s32[]{:S(2)}) async-start(), calls=%async_computation.3 | async-start | bytes 1114112 | tf_op jit(solution)/shard_map/all_gather | solution.py:75
  771.3 9.7 copy-start.48
  783.8 241.7 %all-reduce.5.cloned.1.call-start = ((), (), s32[]{:S(2)}) async-start(), calls=%async_computation.13 | async-start | bytes 4194304 | tf_op jit(solution)/shard_map/psum | solution.py:96
  786.8 5.8 copy-start.1
  794.5 12.5 %copy-start.22 = (f32[512,512]{0,1:T(8,128)}, f32[512,512]{0,1:T(8,128)S(1)}, u32[]{:S(2)}) copy-start(f32[512,512]{0,1:T(8,128)S(1)} %convolution_subtract_fusion.3) | copy-start | bytes 3145732
  795.1 21.9 %copy-start.45 = (f32[512,512]{1,0:T(8,128)}, f32[512,512]{1,0:T(8,128)S(1)}, u32[]{:S(2)}) copy-start(f32[512,512]{1,0:T(8,128)S(1)} %fusion.31) | copy-start | bytes 3145732
  817.3 117.7 %copy-start.10 = (f32[512,512]{1,0:T(8,128)S(1)}, f32[512,512]{1,0:T(8,128)}, u32[]{:S(2)}) copy-start(f32[512,512]{1,0:T(8,128)} %copy-done.8) | copy-start | bytes 3145732
  894.6 48.9 %copy-start.2 = (f32[512,1024]{1,0:T(8,128)S(1)}, f32[512,1024]{1,0:T(8,128)}, u32[]{:S(2)}) copy-start(f32[512,1024]{1,0:T(8,128)} %fusion.178) | copy-start | bytes 6291460
  935.0 5.3 copy-start.59
  947.7 7.1 copy-start.18
  960.7 5.1 copy-start.23
  965.7 23.0 %copy-start.5 = (f32[512,512]{1,0:T(8,128)S(1)}, f32[512,512]{1,0:T(8,128)}, u32[]{:S(2)}) copy-start(f32[512,512]{1,0:T(8,128)} %copy-done.4) | copy-start | bytes 3145732
  965.7 23.0 %copy-start.13 = (f32[512,512]{1,0:T(8,128)S(1)}, f32[512,512]{1,0:T(8,128)}, u32[]{:S(2)}) copy-start(f32[512,512]{1,0:T(8,128)} %copy-done.11) | copy-start | bytes 3145732
  985.8 4.8 copy-start.7
  1025.5 5.0 copy-start.26
  1025.5 5.1 copy-start.55
  1030.5 10.5 %copy-start.24 = (f32[512,512]{1,0:T(8,128)S(1)}, f32[512,512]{1,0:T(8,128)}, u32[]{:S(2)}) copy-start(f32[512,512]{1,0:T(8,128)} %fusion.175) | copy-start | bytes 3145732
  1030.5 10.5 %copy-start.51 = (f32[1,4,1,32,4,1,128]{6,5,4,3,2,1,0:T(1,128)S(1)}, f32[1,4,1,32,4,1,128]{6,5,4,3,2,1,0:T(1,128)}, u32[]{:S(2)}) copy-start(f32[1,4,1,32,4,1,128]{6,5,4,3,2,1,0:T(1,128)} %param.12) | copy-start | bytes 786436
  1030.5 10.5 %copy-start.52 = (f32[512,128]{0,1:T(8,128)S(1)}, f32[512,128]{0,1:T(8,128)}, u32[]{:S(2)}) copy-start(f32[512,128]{0,1:T(8,128)} %get-tuple-element.121) | copy-start | bytes 786436
  1031.3 9.8 collective-permute-start
  (26 other events, 87.3 us)
Sparse Core Ops, SparseCore 0:
  10.4 41.4 all-gather.36
  54.3 49.2 all-gather.38
  105.5 38.9 all-gather.28
  146.2 37.4 all-gather.20
  220.5 42.9 all-gather.40
  299.3 36.2 all-gather.30
  338.4 36.4 all-gather.22
  462.2 35.6 all-gather.42
  527.6 36.7 all-gather.32
  566.1 37.2 all-gather.24
  737.1 24.4 all-gather.44
  763.3 38.9 all-gather.34
  804.1 37.3 all-gather.26
  963.8 61.6 all-reduce.4

commit v5 on v4

--- a/solution.py
+++ b/solution.py
@@ -60,40 +60,55 @@
     left_part = left_coupling.reshape(panels, col_width, panels * row_width)
     right_part = right_coupling.reshape(panels, col_width, panels * row_width)
     arrow_part = arrow_coupling.reshape(panels, col_width, arrow_rows)
-    def gather_block_row(k, after):
-        piece = matrix[k, :, k:, :]
-        if after is not None:
-            piece, _ = lax.optimization_barrier((piece, after))
-        by_col = lax.all_gather(piece, "col", axis=0, tiled=True)
-        whole = lax.all_gather(by_col[:, :, None, :], "row", axis=2, tiled=True)
-        return whole.reshape(panel_size, (panels - k) * panel_size)
-
-    def gather_coupling(k, after):
-        pieces = (left_part[k], right_part[k])
+    day_width = lambda k: (panels - k) * row_width
+    wide = panels * row_width
+
+    def gather_panel(k, after):
+        pieces = [left_part[k], right_part[k], arrow_part[k]]
+        if k > 0:
+            pieces = [matrix[k, :, k:, :].reshape(col_width, day_width(k))] + pieces
         if after is not None:
             pieces, _ = lax.optimization_barrier((pieces, after))
-        return tuple(lax.all_gather(piece, "col", axis=0, tiled=True) for piece in pieces)
-
-    block_rows = [gather_block_row(0, None)] + [None] * (panels - 1)
+        joined = lax.all_gather(jnp.concatenate(pieces, axis=1), "col", axis=0, tiled=True)
+        start = day_width(k) if k > 0 else 0
+        left_new = joined[:, start : start + wide]
+        right_new = joined[:, start + wide : start + 2 * wide]
+        arrow_new = joined[:, start + 2 * wide :]
+        if k == 0:
+            return None, left_new, right_new, arrow_new
+        by_col = joined[:, :start].reshape(panel_size, panels - k, row_width)
+        whole = lax.all_gather(by_col[:, :, None, :], "row", axis=2, tiled=True)
+        return whole.reshape(panel_size, (panels - k) * panel_size), left_new, right_new, arrow_new
+
+    first_col = lax.all_gather(matrix[0], "col", axis=0, tiled=True)
+    first_row = lax.all_gather(first_col[:, :, None, :], "row", axis=2, tiled=True)
+    block_rows = [first_row.reshape(panel_size, panels * panel_size)] + [None] * (panels - 1)
     left_full = [None] * panels
     right_full = [None] * panels
-    left_full[0], right_full[0] = gather_coupling(0, None)
-    arrow_all = lax.all_gather(arrow_part, "col", axis=1, tiled=True)
-    arrow_full = [arrow_all[k] for k in range(panels)]
+    arrow_full = [None] * panels
+    _, left_full[0], right_full[0], arrow_full[0] = gather_panel(0, None)
     pending = [[] for _ in range(panels)]
     pending_left = [[] for _ in range(panels)]
     pending_right = [[] for _ in range(panels)]
+    pending_arrow = [[] for _ in range(panels)]
     rows_at = col_index * col_width + lax.broadcasted_iota(jnp.int32, (col_width, row_width), 0)
     cols_at = row_index * row_width + lax.broadcasted_iota(jnp.int32, (col_width, row_width), 1)
     per_slice = row_width // col_width
     owner = col_index // per_slice
     offset = (col_index % per_slice) * col_width
 
-    def own_columns(solved):
-        spread = solved.reshape(panel_size, panels, row_width)
-        picked = lax.dynamic_slice_in_dim(spread, offset, col_width, 2)
-        picked = jnp.where(row_index == owner, picked, 0.0)
-        return lax.psum(picked, "row").reshape(panel_size, panels * col_width)
+    def own_columns(solved_pair, after):
+        picked = []
+        for solved in solved_pair:
+            spread = solved.reshape(panel_size, panels, row_width)
+            part = lax.dynamic_slice_in_dim(spread, offset, col_width, 2)
+            picked.append(jnp.where(row_index == owner, part, 0.0))
+        if after is not None:
+            picked, _ = lax.optimization_barrier((picked, after))
+        summed = lax.psum(picked, "row")
+        return [part.reshape(panel_size, panels * col_width) for part in summed]
+
+    previous_sum = None
 
     factor_blocks = []
     left_solved = []
@@ -110,13 +125,18 @@
         diagonal_full = block_row[:, :panel_size]
         factor = jnp.linalg.cholesky(diagonal_full)
         if remain > 1:
-            block_rows[current + 1] = gather_block_row(current + 1, factor)
-            fresh_left, fresh_right = gather_coupling(current + 1, factor)
+            block_rows[current + 1], fresh_left, fresh_right, fresh_arrow = gather_panel(
+                current + 1, factor
+            )
             for update in pending_left[current + 1]:
                 fresh_left = fresh_left - update
             for update in pending_right[current + 1]:
                 fresh_right = fresh_right - update
-            left_full[current + 1], right_full[current + 1] = fresh_left, fresh_right
+            for update in pending_arrow[current + 1]:
+                fresh_arrow = fresh_arrow - update
+            left_full[current + 1] = fresh_left
+            right_full[current + 1] = fresh_right
+            arrow_full[current + 1] = fresh_arrow
         inverse = lower_inverse(factor)
         owned_full = product(inverse, block_row)
         owned = lax.dynamic_slice_in_dim(
@@ -128,8 +148,10 @@
         left_solved.append(solved_left)
         right_solved.append(solved_right)
         arrow_solved.append(solved_arrow)
-        right_term = right_term + product_tn(own_columns(solved_right), solved_right)
-        left_term = left_term + product_tn(own_columns(solved_left), solved_left)
+        own_right, own_left = own_columns((solved_right, solved_left), previous_sum)
+        previous_sum = own_left
+        right_term = right_term + product_tn(own_right, solved_right)
+        left_term = left_term + product_tn(own_left, solved_left)
         arrow_term = arrow_term + product_tn(solved_arrow, solved_arrow)
         mine_rows = lax.dynamic_slice_in_dim(owned, col_index * col_width, col_width, 0)
         diagonal_part = jnp.where(cols_at >= rows_at, mine_rows[:, 0, :], 0.0)
@@ -158,10 +180,11 @@
                 if step == 0:
                     left_full[target] = left_full[target] - left_update[rows]
                     right_full[target] = right_full[target] - right_update[rows]
+                    arrow_full[target] = arrow_full[target] - arrow_update[rows]
                 else:
                     pending_left[target].append(left_update[rows])
                     pending_right[target].append(right_update[rows])
-                arrow_full[target] = arrow_full[target] - arrow_update[rows]
+                    pending_arrow[target].append(arrow_update[rows])
     day_factor = jnp.stack(factor_blocks).reshape(day_block.shape)
 
     def mine(parts, width):

time: 1060 us -> 1110 us (1.047)
  waiting for transfers between devices: 109 us -> 218 us
  blocking collectives: 87 us -> 12.2 us
    all_gather x13 -> x9, waiting for transfers between devices: 70 us -> 156 us  [the longest x1 47.1 us: per_device(): lax.all_gather(first_col[:, :, None, :], 'row', axis=2, tiled=True)]
    all_gather x4 -> x0, blocking collectives: 74.9 us -> none  [the longest x3 56.5 us: gather_block_row(): by_col = lax.all_gather(piece, 'col', axis=0, tiled=True)]
    psum x1 -> x4, waiting for transfers between devices: 32.9 us -> 56.1 us  [own_columns(): summed = lax.psum(picked, 'row')]
  transfers between devices with their start and end apart: 15 -> 14, of which waited for: 4 -> 8; matrix products, arithmetic and copies ran while one was open for 76% -> 51% of each run, Pallas kernels for 0% -> 0%
where the time goes in v5:
time: 1110 us; the launch traced here: 1100 us
  other arithmetic  511 us (46%)
  waiting for transfers between devices  218 us (20%)
  matrix products  199 us (18%)
  local copies, waits for them, and re-layouts  135 us (12%)
  between operations  26.3 us (2%)
  blocking collectives  12.2 us (1%)
    another operation x59, other arithmetic, per_device(): factor = jnp.linalg.cholesky(diagonal_full)  321 us
    another operation x9, other arithmetic, lower_inverse(): lax.linalg.triangular_solve(factor, identity, left_side=True, lower=True)  162 us
    dot_general x27, matrix products, product_tn(): lax.dot_general(left, right, (((0,), (0,)), ((), ())), precision=lax.Prec...  90 us
    dot_general x16, matrix products, product(): jnp.dot(left, right, precision=lax.Precision.HIGHEST, preferred_element_t...  66 us
    psum x4, waiting for transfers between devices, own_columns(): summed = lax.psum(picked, 'row')  56.1 us
    all_gather x1, waiting for transfers between devices, per_device(): lax.all_gather(first_col[:, :, None, :], 'row', axis=2, tiled=True)  47.1 us
    all_gather x1, waiting for transfers between devices, per_device(): first_col = lax.all_gather(matrix[0], 'col', axis=0, tiled=True)  43 us
    all_gather x4, waiting for transfers between devices, gather_panel(): lax.all_gather(jnp.concatenate(pieces, axis=1), 'col', axis=0, tiled=True)  40.3 us
  transfers between devices with their start and end apart: 14, of which 8 were waited for; matrix products, arithmetic and copies ran while one was open for 51% of the time, Pallas kernels for 0%

profile of v5, /device:TPU:8, one launch (start us, length us, event | category | flops | bytes accessed | tf_op | source)
XLA Modules:
  0.0 1104.8 jit_solution(951911790519709675)
XLA Ops:
  8.9 43.0 %all-gather.26.cloned.1.call-done = f32[1,1,1,512,4,1,128]{6,4,5,2,1,0,3:T(4,128)} async-done(((f32[1,1,1,32,4,1,128]{6,4,5,2,1,0,3:T(4,128)}), f32[1,1,1,512,4,1,128]{6,4,5,2,1,0,3:T(4,128)}) %all-gather.26.cloned.1.call-update) | async-done | bytes 1048592 | tf_op jit(solution)/shard_map/all_gather | solution.py:83
  56.5 47.1 %all-gather.28.cloned.1.call-done = f32[1,1,1,512,4,4,128]{6,3,4,2,1,0,5:T(8,128)} async-done(((f32[1,1,1,512,4,1,128]{6,3,4,2,1,0,5:T(8,128)}), f32[1,1,1,512,4,4,128]{6,3,4,2,1,0,5:T(8,128)}) %all-gather.28.cloned.1.call-update) | async-done | bytes 4194320 | tf_op jit(solution)/shard_map/all_gather | solution.py:84
  103.6 5.8 copy.131
  112.5 11.7 %cholesky.462 = f32[128,128]{1,0:T(8,128)S(1)} custom-call(f32[128,128]{1,0:T(8,128)S(1)} %cholesky.746), custom_call_target="Cholesky" | custom-call | tf_op jit(solution)/shard_map/jit(cholesky)/cholesky | solution.py:126
  124.3 9.8 custom-call.35
  134.9 11.7 %cholesky.481 = f32[128,128]{1,0:T(8,128)S(1)} custom-call(f32[128,128]{1,0:T(8,128)S(1)} %cholesky.750), custom_call_target="Cholesky" | custom-call | tf_op jit(solution)/shard_map/jit(cholesky)/cholesky | solution.py:126
  146.6 10.0 custom-call.36
  157.3 11.7 %cholesky.502 = f32[128,128]{1,0:T(8,128)S(1)} custom-call(f32[128,128]{1,0:T(8,128)S(1)} %cholesky.755), custom_call_target="Cholesky" | custom-call | tf_op jit(solution)/shard_map/jit(cholesky)/cholesky | solution.py:126
  169.7 9.8 custom-call.37
  180.1 11.7 %cholesky.519 = f32[128,128]{1,0:T(8,128)S(1)} custom-call(f32[128,128]{1,0:T(8,128)S(1)} %convolution_subtract_fusion.30), custom_call_target="Cholesky" | custom-call | tf_op jit(solution)/shard_map/jit(cholesky)/cholesky | solution.py:126
  197.8 40.3 %all-gather.14.cloned.1.call-done = f32[512,1472]{1,0:T(8,128)} async-done(((f32[32,1472]{1,0:T(8,128)}), f32[512,1472]{1,0:T(8,128)}) %all-gather.14.cloned.1.call-update) | async-done | bytes 3014672 | tf_op jit(solution)/shard_map/all_gather | solution.py:72
  243.6 8.0 while.8
  251.6 39.3 %custom-call.38 = f32[4,128,128]{1,2,0:T(8,128)S(1)} custom-call(f32[4,128,128]{2,1,0:T(8,128)S(1)} %get-tuple-element.70), custom_call_target="InvertDiagBlocksLowerTriangular" | custom-call | tf_op jit(solution)/shard_map/triangular_solve/custom-call.3 | solution.py:19
  298.4 10.2 fusion.190
  308.7 12.7 %all-gather.16.cloned.1.call-done = f32[512,3,4,128]{3,0,1,2:T(8,128)} async-done(((f32[512,3,1,128]{3,0,1,2:T(8,128)}), f32[512,3,4,128]{3,0,1,2:T(8,128)}) %all-gather.16.cloned.1.call-update) | async-done | bytes 3145744 | tf_op jit(solution)/shard_map/all_gather | solution.py:80
  324.9 7.8 convolution_subtract_fusion
  339.7 12.5 %cholesky.534 = f32[128,128]{1,0:T(8,128)S(1)} custom-call(f32[128,128]{1,0:T(8,128)} %cholesky.759), custom_call_target="Cholesky" | custom-call | tf_op jit(solution)/shard_map/jit(cholesky)/cholesky | solution.py:126
  353.0 9.8 custom-call.39
  365.5 11.7 %cholesky.553 = f32[128,128]{1,0:T(8,128)S(1)} custom-call(f32[128,128]{1,0:T(8,128)S(1)} %cholesky.763), custom_call_target="Cholesky" | custom-call | tf_op jit(solution)/shard_map/jit(cholesky)/cholesky | solution.py:126
  377.9 10.2 custom-call.40
  389.7 11.7 %cholesky.574 = f32[128,128]{1,0:T(8,128)S(1)} custom-call(f32[128,128]{1,0:T(8,128)S(1)} %cholesky.768), custom_call_target="Cholesky" | custom-call | tf_op jit(solution)/shard_map/jit(cholesky)/cholesky | solution.py:126
  402.1 9.8 custom-call.41
  413.3 11.7 %cholesky.591 = f32[128,128]{1,0:T(8,128)S(1)} custom-call(f32[128,128]{1,0:T(8,128)S(1)} %convolution_subtract_fusion.29), custom_call_target="Cholesky" | custom-call | tf_op jit(solution)/shard_map/jit(cholesky)/cholesky | solution.py:126
  430.6 6.2 reshape.302
  439.6 4.1 fusion
  455.3 6.8 fusion.7
  462.1 7.3 fusion.2
  469.5 7.1 fusion.4
  478.9 8.0 while.9
  487.0 39.3 %custom-call.42 = f32[4,128,128]{1,2,0:T(8,128)S(1)} custom-call(f32[4,128,128]{2,1,0:T(8,128)S(1)} %get-tuple-element.71), custom_call_target="InvertDiagBlocksLowerTriangular" | custom-call | tf_op jit(solution)/shard_map/triangular_solve/custom-call.3 | solution.py:19
  536.1 7.4 fusion.189
  550.5 4.6 fusion.24
  557.7 4.7 fusion.30
  569.2 6.1 fusion.12
  575.3 5.6 fusion.9
  588.7 11.7 %cholesky.606 = f32[128,128]{1,0:T(8,128)S(1)} custom-call(f32[128,128]{1,0:T(8,128)S(1)} %cholesky.772), custom_call_target="Cholesky" | custom-call | tf_op jit(solution)/shard_map/jit(cholesky)/cholesky | solution.py:126
  601.1 9.8 custom-call.43
  616.0 12.5 %cholesky.625 = f32[128,128]{1,0:T(8,128)S(1)} custom-call(f32[128,128]{1,0:T(8,128)} %cholesky.776), custom_call_target="Cholesky" | custom-call | tf_op jit(solution)/shard_map/jit(cholesky)/cholesky | solution.py:126
  629.8 11.1 %custom-call.44 = f32[1,128,128]{1,2,0:T(8,128)S(1)} custom-call(f32[1,128,128]{2,1,0:T(8,128)} %get-tuple-element.179), custom_call_target="InvertDiagBlocksLowerTriangular" | custom-call | tf_op jit(solution)/shard_map/jit(cholesky)/cholesky | solution.py:126
  643.4 11.7 %cholesky.646 = f32[128,128]{1,0:T(8,128)S(1)} custom-call(f32[128,128]{1,0:T(8,128)S(1)} %cholesky.781), custom_call_target="Cholesky" | custom-call | tf_op jit(solution)/shard_map/jit(cholesky)/cholesky | solution.py:126
  656.4 9.8 custom-call.45
  668.5 11.7 %cholesky.663 = f32[128,128]{1,0:T(8,128)S(1)} custom-call(f32[128,128]{1,0:T(8,128)S(1)} %convolution_subtract_fusion.28), custom_call_target="Cholesky" | custom-call | tf_op jit(solution)/shard_map/jit(cholesky)/cholesky | solution.py:126
  689.9 6.0 fusion.14
  698.7 11.6 %while.10 = (s32[]{:T(128)}, f32[512,512]{1,0:T(8,128)}, s32[4,2]{0,1:T(2,128)S(1)}, f32[4,128,128]{2,1,0:T(8,128)S(1)}, s32[]{:T(128)}) while((s32[]{:T(128)}, f32[512,512]{1,0:T(8,128)}, s32[4,2]{0,1:T(2,128)S(1)}, f32[4,128,128]{2,1,0:T(8,128)S(1)}, s32[]{:T(128)}) %tuple.178), condition=%wide.while_cond.clone.1, body=%wide.while_body.clone.1.sunk | while | flops 2 | bytes 131189 | solution.py:19
  710.2 39.9 %custom-call.46 = f32[4,128,128]{1,2,0:T(8,128)} custom-call(f32[4,128,128]{2,1,0:T(8,128)S(1)} %get-tuple-element.72), custom_call_target="InvertDiagBlocksLowerTriangular" | custom-call | tf_op jit(solution)/shard_map/triangular_solve/custom-call.3 | solution.py:19
  759.3 4.5 fusion.22
  766.4 5.0 fusion.28
  777.8 6.8 fusion.188
  799.3 25.3 %all-reduce.12.cloned.1.call-done = f32[512,128]{0,1:T(8,128)} async-done(((f32[512,128]{0,1:T(8,128)}), f32[512,128]{0,1:T(8,128)}) %all-reduce.12.cloned.1.call-update) | async-done | bytes 262160 | tf_op jit(solution)/shard_map/psum | solution.py:108
  831.0 5.5 convolution_subtract_fusion.1
  836.5 4.2 convolution_subtract_fusion.2
  840.8 13.2 %all-gather.30.cloned.1.call-done = f32[512,512]{0,1:T(8,128)} async-done(((f32[512,128]{0,1:T(8,128)}), f32[512,512]{0,1:T(8,128)}) %all-gather.30.cloned.1.call-update) | async-done | bytes 1048592 | tf_op jit(solution)/shard_map/all_gather | solution.py:80
  863.4 11.7 %cholesky.678 = f32[128,128]{1,0:T(8,128)S(1)} custom-call(f32[128,128]{1,0:T(8,128)S(1)} %cholesky.785), custom_call_target="Cholesky" | custom-call | tf_op jit(solution)/shard_map/jit(cholesky)/cholesky | solution.py:126
  875.8 9.8 custom-call.47
  888.3 11.7 %cholesky.697 = f32[128,128]{1,0:T(8,128)S(1)} custom-call(f32[128,128]{1,0:T(8,128)S(1)} %cholesky.789), custom_call_target="Cholesky" | custom-call | tf_op jit(solution)/shard_map/jit(cholesky)/cholesky | solution.py:126
  900.7 10.2 custom-call.48
  912.5 11.7 %cholesky.718 = f32[128,128]{1,0:T(8,128)S(1)} custom-call(f32[128,128]{1,0:T(8,128)S(1)} %cholesky.794), custom_call_target="Cholesky" | custom-call | tf_op jit(solution)/shard_map/jit(cholesky)/cholesky | solution.py:126
  924.9 9.8 custom-call.49
  936.1 11.7 %cholesky.735 = f32[128,128]{1,0:T(8,128)S(1)} custom-call(f32[128,128]{1,0:T(8,128)S(1)} %convolution_subtract_fusion.27), custom_call_target="Cholesky" | custom-call | tf_op jit(solution)/shard_map/jit(cholesky)/cholesky | solution.py:126
  952.4 11.7 %while.11 = (s32[]{:T(128)}, f32[512,512]{1,0:T(8,128)}, s32[4,2]{0,1:T(2,128)S(1)}, f32[4,128,128]{2,1,0:T(8,128)S(1)}, s32[]{:T(128)}) while((s32[]{:T(128)}, f32[512,512]{1,0:T(8,128)}, s32[4,2]{0,1:T(2,128)S(1)}, f32[4,128,128]{2,1,0:T(8,128)S(1)}, s32[]{:T(128)}) %tuple.179), condition=%wide.while_cond.clone.2, body=%wide.while_body.clone.2.sunk | while | flops 2 | bytes 131189 | solution.py:19
  964.1 39.3 %custom-call.50 = f32[4,128,128]{1,2,0:T(8,128)S(1)} custom-call(f32[4,128,128]{2,1,0:T(8,128)S(1)} %get-tuple-element.73), custom_call_target="InvertDiagBlocksLowerTriangular" | custom-call | tf_op jit(solution)/shard_map/triangular_solve/custom-call.3 | solution.py:19
  1038.5 12.2 %all-gather.3 = f32[256,64]{1,0:T(8,128)S(1)} all-gather(f32[64,64]{1,0:T(8,128)S(1)} %convolution_add_fusion.6), channel_id=5, replica_groups=mesh['tm'=4,'row'=4,'col'=16] {'tm'}, dimensions={0}, use_global_device_ids=true | all-gather | bytes 81920 | tf_op jit(solution)/shard_map/all_gather | solution.py:200
  1052.9 30.8 %all-reduce.14.cloned.1.call-done = (f32[512,128]{0,1:T(8,128)}, f32[512,128]{0,1:T(8,128)}, f32[512,128]{0,1:T(8,128)}, f32[512,128]{0,1:T(8,128)}, f32[512,128]{0,1:T(8,128)}) async-done(((f32[512,128]{0,1:T(8,128)}, f32[512,128]{0,1:T(8,128)}, f32[512,128]{0,1:T(8,128)}, f32[512,128]{0,1:T(8,128)}, f32[512,128]{0,1:T(8,128)}), (f32[512,128]{0,1:T(8,128)}, f32[512,128]{0,1:T(8,128)}, ...) | async-done | bytes 1310736 | tf_op jit(solution)/shard_map/psum | solution.py:108
  1091.5 5.0 collective-permute-done
  (468 shorter events, 266.1 us)
Async XLA Ops:
  7.2 47.1 %copy-start.48 = (f32[1,4,1,32,4,1,128]{6,5,4,3,2,1,0:T(1,128)S(1)}, f32[1,4,1,32,4,1,128]{6,5,4,3,2,1,0:T(1,128)}, u32[]{:S(2)}) copy-start(f32[1,4,1,32,4,1,128]{6,5,4,3,2,1,0:T(1,128)} %param.9) | copy-start | bytes 786436
  7.2 47.2 %copy-start.62 = (f32[1,4,1,32,4,1,128]{6,5,4,3,2,1,0:T(1,128)S(1)}, f32[1,4,1,32,4,1,128]{6,5,4,3,2,1,0:T(1,128)}, u32[]{:S(2)}) copy-start(f32[1,4,1,32,4,1,128]{6,5,4,3,2,1,0:T(1,128)} %param.11) | copy-start | bytes 786436
  7.2 47.2 %copy-start.63 = (f32[1,4,1,32,4,1,128]{6,5,4,3,2,1,0:T(1,128)S(1)}, f32[1,4,1,32,4,1,128]{6,5,4,3,2,1,0:T(1,128)}, u32[]{:S(2)}) copy-start(f32[1,4,1,32,4,1,128]{6,5,4,3,2,1,0:T(1,128)} %param.10) | copy-start | bytes 786436
  7.2 48.6 %copy-start.71 = (f32[1,4,1,32,64]{4,3,2,1,0:T(8,128)S(1)}, f32[1,4,1,32,64]{4,3,2,1,0:T(8,128)}, u32[]{:S(2)}) copy-start(f32[1,4,1,32,64]{4,3,2,1,0:T(8,128)} %param.13) | copy-start | bytes 98308
  7.2 44.7 %all-gather.26.cloned.1.call-start = ((), (), s32[]{:S(2)}) async-start(), calls=%async_computation.9 | async-start | bytes 1114112 | tf_op jit(solution)/shard_map/all_gather | solution.py:83
  8.8 94.8 %all-gather.28.cloned.1.call-start = ((), (), s32[]{:S(2)}) async-start(), calls=%async_computation.10 | async-start | bytes 5242880 | tf_op jit(solution)/shard_map/all_gather | solution.py:84
  54.2 183.8 %all-gather.14.cloned.1.call-start = ((), (), s32[]{:S(2)}) async-start(), calls=%async_computation | async-start | bytes 3342336 | tf_op jit(solution)/shard_map/all_gather | solution.py:72
  196.9 97.2 %all-gather.24.cloned.1.call-start = ((), (), s32[]{:S(2)}) async-start(), calls=%async_computation.5 | async-start | bytes 2506752 | tf_op jit(solution)/shard_map/all_gather | solution.py:72
  197.7 123.6 %all-gather.16.cloned.1.call-start = ((), (), s32[]{:S(2)}) async-start(), calls=%async_computation.1 | async-start | bytes 3932160 | tf_op jit(solution)/shard_map/all_gather | solution.py:80
  240.8 235.8 %all-reduce.8.cloned.1.call-start = ((), (), s32[]{:S(2)}) async-start(), calls=%async_computation.6 | async-start | bytes 524288 | tf_op jit(solution)/shard_map/psum | solution.py:108
  242.9 50.8 %copy-start.9 = (f32[512,512]{1,0:T(8,128)}, f32[512,512]{1,0:T(8,128)S(1)}, u32[]{:S(2)}) copy-start(f32[512,512]{1,0:T(8,128)S(1)} %fusion.47) | copy-start | bytes 3145732
  292.1 6.2 copy-start.21
  294.1 14.5 %copy-start.33 = (f32[128,512]{1,0:T(8,128)}, f32[128,512]{1,0:T(8,128)S(1)}, u32[]{:S(2)}) copy-start(f32[128,512]{1,0:T(8,128)S(1)} %fusion.157) | copy-start | bytes 786436
  297.3 11.3 %copy-start.4 = (f32[512,512]{1,0:T(8,128)}, f32[512,512]{1,0:T(8,128)S(1)}, u32[]{:S(2)}) copy-start(f32[512,512]{1,0:T(8,128)S(1)} %fusion.32) | copy-start | bytes 3145732
  308.6 218.9 %all-gather.18.cloned.1.call-start = ((), (), s32[]{:S(2)}) async-start(), calls=%async_computation.2 | async-start | bytes 3063808 | tf_op jit(solution)/shard_map/all_gather | solution.py:72
  362.9 65.5 %copy-start.60 = (f32[4,8,4,128]{3,1,2,0:T(8,128)S(1)}, f32[4,8,4,128]{3,1,2,0:T(8,128)}, u32[]{:S(2)}) copy-start(f32[4,8,4,128]{3,1,2,0:T(8,128)} %copy.225) | copy-start | bytes 196612
  362.9 65.5 %copy-start.61 = (f32[4,8,4,128]{3,1,2,0:T(8,128)S(1)}, f32[4,8,4,128]{3,1,2,0:T(8,128)}, u32[]{:S(2)}) copy-start(f32[4,8,4,128]{3,1,2,0:T(8,128)} %copy.226) | copy-start | bytes 196612
  362.9 65.5 %copy-start.69 = (f32[4,8,2,128]{3,1,2,0:T(8,128)S(1)}, f32[4,8,2,128]{3,1,2,0:T(8,128)}, u32[]{:S(2)}) copy-start(f32[4,8,2,128]{3,1,2,0:T(8,128)} %copy.232) | copy-start | bytes 98308
  362.9 65.5 %copy-start.72 = (f32[32,64]{1,0:T(8,128)S(1)}, f32[32,64]{1,0:T(8,128)}, u32[]{:S(2)}) copy-start(f32[32,64]{1,0:T(8,128)} %get-tuple-element.33) | copy-start | bytes 24580
  429.2 146.1 %all-gather.20.cloned.1.call-start = ((), (), s32[]{:S(2)}) async-start(), calls=%async_computation.3 | async-start | bytes 2621440 | tf_op jit(solution)/shard_map/all_gather | solution.py:80
  430.5 6.2 copy-start.22
  430.5 6.2 copy-start.29
  430.5 6.2 copy-start.34
  449.3 12.8 %copy-start.7 = (f32[512,512]{1,0:T(8,128)}, f32[512,512]{1,0:T(8,128)S(1)}, u32[]{:S(2)}) copy-start(f32[512,512]{1,0:T(8,128)S(1)} %fusion.26) | copy-start | bytes 3145732
  451.7 10.4 copy-start
  462.1 7.3 copy-start.5
  469.5 56.8 %copy-start.10 = (f32[512,512]{1,0:T(8,128)S(1)}, f32[512,512]{1,0:T(8,128)}, u32[]{:S(2)}) copy-start(f32[512,512]{1,0:T(8,128)} %copy-done.9) | copy-start | bytes 3145732
  529.8 166.1 %all-reduce.10.cloned.1.call-start = ((), (), s32[]{:S(2)}) async-start(), calls=%async_computation.7 | async-start | bytes 524288 | tf_op jit(solution)/shard_map/psum | solution.py:108
  562.4 5.9 copy-start.67
  575.2 215.1 %all-gather.22.cloned.1.call-start = ((), (), s32[]{:S(2)}) async-start(), calls=%async_computation.4 | async-start | bytes 2785280 | tf_op jit(solution)/shard_map/all_gather | solution.py:72
  612.1 74.6 %copy-start.56 = (f32[4,8,4,128]{3,1,2,0:T(8,128)S(1)}, f32[4,8,4,128]{3,1,2,0:T(8,128)}, u32[]{:S(2)}) copy-start(f32[4,8,4,128]{3,1,2,0:T(8,128)} %copy.223) | copy-start | bytes 196612
  612.1 74.6 %copy-start.57 = (f32[4,8,4,128]{3,1,2,0:T(8,128)S(1)}, f32[4,8,4,128]{3,1,2,0:T(8,128)}, u32[]{:S(2)}) copy-start(f32[4,8,4,128]{3,1,2,0:T(8,128)} %copy.224) | copy-start | bytes 196612
  686.7 9.2 copy-start.46
  688.2 136.3 %all-reduce.12.cloned.1.call-start = ((), (), s32[]{:S(2)}) async-start(), calls=%async_computation.8 | async-start | bytes 524288 | tf_op jit(solution)/shard_map/psum | solution.py:108
  689.3 9.4 copy-start.64
  750.2 5.7 copy-start.55
  750.2 9.1 copy-start.26
  777.3 76.6 %all-gather.30.cloned.1.call-start = ((), (), s32[]{:S(2)}) async-start(), calls=%async_computation.11 | async-start | bytes 1310720 | tf_op jit(solution)/shard_map/all_gather | solution.py:80
  790.3 37.0 %slice-start = ((f32[512,1216]{1,0:T(8,128)}), f32[512,64]{1,0:T(8,128)S(1)}, s32[]{:S(2)}) async-start(f32[512,1216]{1,0:T(8,128)} %all-gather.22.cloned.1.call-done), calls=%async_computation.13 | async-start | bytes 524288 | tf_op jit(solution)/shard_map/slice | solution.py:76
  793.8 289.8 %all-reduce.14.cloned.1.call-start = ((), (), s32[]{:S(2)}) async-start(), calls=%async_computation.12 | async-start | bytes 2621440 | tf_op jit(solution)/shard_map/psum | solution.py:108
  828.1 8.5 copy-start.43
  831.0 5.5 copy-start.15
  831.0 5.5 copy-start.27
  853.9 5.8 copy-start.2
  887.0 116.5 %copy-start.11 = (f32[512,512]{1,0:T(8,128)S(1)}, f32[512,512]{1,0:T(8,128)}, u32[]{:S(2)}) copy-start(f32[512,512]{1,0:T(8,128)} %copy-done.9) | copy-start | bytes 3145732
  1005.5 8.9 copy-start.25
  1007.0 6.4 copy-start.70
  1007.4 7.1 copy-start.32
  1010.4 5.9 copy-start.37
  1017.7 10.2 copy-start.8
  1017.7 10.2 copy-start.12
  1023.5 6.1 copy-start.6
  1030.3 6.8 copy-start.65
  1030.3 6.8 copy-start.68
  1030.3 7.9 copy-start.66
  1030.3 20.5 %copy-start.73 = (f32[64,64]{1,0:T(8,128)S(1)}, f32[64,64]{1,0:T(8,128)}, u32[]{:S(2)}) copy-start(f32[64,64]{1,0:T(8,128)} %param.14) | copy-start | bytes 49156
  1032.3 53.2 %copy-start.45 = (f32[128,512]{1,0:T(8,128)S(1)}, f32[128,512]{1,0:T(8,128)}, u32[]{:S(2)}) copy-start(f32[128,512]{1,0:T(8,128)} %convolution_add_fusion.1) | copy-start | bytes 786436
  1051.4 39.4 %copy-start.14 = (f32[512,512]{1,0:T(8,128)S(1)}, f32[512,512]{1,0:T(8,128)}, u32[]{:S(2)}) copy-start(f32[512,512]{1,0:T(8,128)} %fusion.22) | copy-start | bytes 3145732
  1083.7 6.4 copy-start.52
  1083.7 7.1 copy-start.51
  1085.4 11.1 %copy-start.19 = (f32[512,512]{1,0:T(8,128)S(1)}, f32[512,512]{1,0:T(8,128)}, u32[]{:S(2)}) copy-start(f32[512,512]{1,0:T(8,128)} %copy-done.18) | copy-start | bytes 3145732
  1085.4 11.1 %copy-start.49 = (f32[1,4,1,32,4,1,128]{6,5,4,3,2,1,0:T(1,128)S(1)}, f32[1,4,1,32,4,1,128]{6,5,4,3,2,1,0:T(1,128)}, u32[]{:S(2)}) copy-start(f32[1,4,1,32,4,1,128]{6,5,4,3,2,1,0:T(1,128)} %param.12) | copy-start | bytes 786436
  1085.4 11.1 %copy-start.50 = (f32[512,128]{0,1:T(8,128)S(1)}, f32[512,128]{0,1:T(8,128)}, u32[]{:S(2)}) copy-start(f32[512,128]{0,1:T(8,128)} %get-tuple-element.142) | copy-start | bytes 786436
  1087.6 9.0 collective-permute-start
  (25 other events, 77.6 us)
Sparse Core Ops, SparseCore 0:
  10.4 41.4 all-gather.25
  54.3 49.2 all-gather.27
  197.1 40.9 all-gather.13
  240.3 38.6 all-gather.23
  280.6 40.6 all-gather.15
  323.5 47.5 all-reduce.7
  429.3 40.5 all-gather.17
  529.9 33.3 all-gather.19
  575.4 47.1 all-reduce.9
  688.3 40.5 all-gather.21
  777.5 47.0 all-reduce.11
  826.8 27.1 all-gather.29
  1030.5 53.1 all-reduce.13
